TPU v7x, 128 devices: a whole 4x4x4 slice. The times are simulated.
128 devices in a mesh: blk: 8 (over y_lo, x), dom: 16 (over y_hi, z, core).
Axes of the slice: x: 4, y: 4 (y_hi: 2, y_lo: 2; y = y_hi * 2 + y_lo), z: 4, core: 2. Of those that a mesh axis runs over, the one named last changes fastest.
Arguments:
- source_emb: bfloat16 [16384, 64], P(('blk', 'dom')), may hold values from -6 to 6
- target_emb: bfloat16 [98304, 64], P(('blk', 'dom')), may hold values from -6 to 6
- source_counts: int32 [16384, 128], P(('blk', 'dom')), may hold values from 1 to 4
- target_counts: int32 [98304, 128], P(('blk', 'dom')), may hold values from 1 to 4
- warm_start: float32 [98304, 128], P(('blk', 'dom')), may hold values from -8 to 263
Outputs:
- source_log_scaling: float32 [16384, 128], P(('blk', 'dom'))
- target_log_scaling: float32 [98304, 128], P(('blk', 'dom'))
All inputs are finite; a program needn't handle non-finite values.
Results may differ from a plain program's by a relative error of at most 0.0022.
Values may be sent and summed in bfloat16 or wider, within the bound.
No kernel may reach another device: no remote copies, remote signals or barrier semaphores. Data moves between devices by JAX's collectives and lax.ppermute only.
A program may use at most 64 MiB of HBM per device.

v0:
```python
import math

import jax
import jax.numpy as jnp
from jax import lax
from jax.sharding import PartitionSpec as P

ITERS = 2


entropic = 0.05


def normalized(values):
    widened = values.astype(jnp.float32)
    squared = jnp.sum(widened * widened, axis=1, keepdims=True) + 1e-06
    return (widened * lax.rsqrt(squared)).astype(jnp.bfloat16)


def block_rows(count, largest):
    if count <= largest:
        return count
    return math.gcd(count, largest)


def kernel_sums(row_emb, col_emb, col_weights):
    row_count = row_emb.shape[0]
    col_count = col_emb.shape[0]
    row_block = block_rows(row_count, 1024)
    col_block = block_rows(col_count, 2048)
    row_parts = row_emb.reshape(row_count // row_block, row_block, row_emb.shape[1])
    col_parts = col_emb.reshape(col_count // col_block, col_block, col_emb.shape[1])
    weight_parts = col_weights.reshape(col_count // col_block, col_block, col_weights.shape[1])

    def one_block(row_piece):

        def add_block(running, paired):
            col_piece, weight_piece = paired
            products = jnp.dot(row_piece, col_piece.T, preferred_element_type=jnp.float32)
            kernel = jnp.exp((products - 1.0) / entropic).astype(jnp.bfloat16)
            return (
                running + jnp.dot(kernel, weight_piece, preferred_element_type=jnp.float32),
                None,
            )

        initial = jnp.zeros((row_piece.shape[0], col_weights.shape[1]), jnp.float32)
        result, unused = lax.scan(add_block, initial, (col_parts, weight_parts))
        return result

    return lax.map(one_block, row_parts).reshape(row_count, col_weights.shape[1])


def column_peak(values):
    return lax.pmax(jnp.max(values, axis=0), ("blk", "dom"))


def body(source_emb, target_emb, source_counts, target_counts, warm_start):
    blk_count = lax.axis_size("blk")
    dom_count = lax.axis_size("dom")
    src_rows = source_emb.shape[0]
    tgt_rows = target_emb.shape[0]
    columns = warm_start.shape[1]
    all_sources = src_rows * blk_count * dom_count
    all_targets = tgt_rows * blk_count * dom_count
    source_block = lax.all_gather(normalized(source_emb), "dom", axis=0, tiled=True)
    own_targets = normalized(target_emb)
    target_group = lax.all_gather(own_targets, "blk", axis=0, tiled=True)
    log_target = jnp.log(target_counts.astype(jnp.float32)) - math.log(all_targets)
    log_source = jnp.log(source_counts.astype(jnp.float32)) - math.log(all_sources)
    target_logs = warm_start
    source_logs = jnp.zeros((src_rows, columns), jnp.float32)
    for iteration in range(ITERS):
        target_peak = column_peak(target_logs)
        scaled = jnp.exp(target_logs - target_peak).astype(jnp.bfloat16)
        partial_value = kernel_sums(
            source_block, target_group, lax.all_gather(scaled, "blk", axis=0, tiled=True)
        )
        shares = lax.psum_scatter(partial_value, "dom", scatter_dimension=0, tiled=True)
        source_logs = log_source - target_peak - jnp.log(shares)
        source_peak = column_peak(source_logs)
        block_logs = lax.all_gather(source_logs, "dom", axis=0, tiled=True)
        weights = jnp.exp(block_logs - source_peak).astype(jnp.bfloat16)
        target_sums = kernel_sums(
            own_targets,
            lax.all_gather(source_block, "blk", axis=0, tiled=True),
            lax.all_gather(weights, "blk", axis=0, tiled=True),
        )
        target_logs = log_target - source_peak - jnp.log(target_sums)
    return (source_logs, target_logs)


def solution(mesh):
    in_specs = (
        P(("blk", "dom"), None),
        P(("blk", "dom"), None),
        P(("blk", "dom"), None),
        P(("blk", "dom"), None),
        P(("blk", "dom"), None),
    )
    out_specs = (P(("blk", "dom"), None), P(("blk", "dom"), None))
    return jax.shard_map(body, mesh=mesh, in_specs=in_specs, out_specs=out_specs, check_vma=False)
```

profile of v0, /device:TPU:1, one launch (start us, length us, event | category | flops | bytes accessed | tf_op | source)
XLA Modules:
  0.0 745.7 jit_solution(10132864980534756513)
XLA Ops:
  8.3 68.7 %pmax.28 = f32[128]{0:T(128)S(1)} all-reduce(f32[128]{0:T(128)S(1)} %reduce_max.36), channel_id=1, replica_groups=mesh['blk'=8,'dom'=16] {'blk','dom'}, use_global_device_ids=true, to_apply=%region_1.0 | all-reduce | flops 128 | bytes 1024 | tf_op jit(solution)/shard_map/pmax | solution.py:54
  80.3 26.6 %all_gather.28 = bf16[2048,64]{0,1:T(8,128)(2,1)S(1)} all-gather(bf16[128,64]{0,1:T(8,128)(2,1)S(1)} %fusion.52), channel_id=1, replica_groups=mesh['blk'=8,'dom'=16] {'dom'}, dimensions={0}, use_global_device_ids=true | all-gather | bytes 278528 | tf_op jit(solution)/shard_map/all_gather | solution.py:65
  108.7 28.0 %all_gather.29 = bf16[6144,64]{1,0:T(8,128)(2,1)} all-gather(bf16[768,64]{1,0:T(8,128)(2,1)S(1)} %fusion.49), channel_id=1, replica_groups=mesh['blk'=8,'dom'=16] {'blk'}, dimensions={0}, use_global_device_ids=true | all-gather | bytes 884736 | tf_op jit(solution)/shard_map/all_gather | solution.py:67
  136.7 24.0 %while.105 = (s32[]{:T(128)}, f32[2,1024,128]{2,1,0:T(8,128)S(1)}, bf16[2,1024,64]{2,1,0:T(8,128)(2,1)S(1)}, bf16[3,2048,64]{2,1,0:T(8,128)(2,1)}, bf16[3,2048,1...) while((s32[]{:T(128)}, f32[2,1024,128]{2,1,0:T(8,128)S(1)}, ...), condition=%wide.region_7.8_spmd, body=%wide.region_4.7_spmd.sunk | while | flops 811859968 | bytes 3540747 | solution.py:50
  136.8 11.9 %while.110 = (s32[]{:T(128)}, f32[1024,128]{1,0:T(8,128)S(1)}, bf16[3,2048,64]{2,1,0:T(8,128)(2,1)}, bf16[1024,64]{1,0:T(8,128)(2,1)S(1)}, bf16[3,2048,128]{2,1,0:T(8,128)(2,1)}, /*index=5*/s32[]{:T(128)}, s32[]{:T(128)}) while((s32[]{:T(128)}, f32[1024,128]{1,0:T(8,128)S(1)}, bf16[3,2048,64]{2,1,0:T(8,128)(2,1)}, ...), condition=%wide.region_6.6_spmd.clone, body=%wide.region_5.5_spmd.clone.sunk | while | flops 811859968 | bytes 2229854 | solution.py:47
  136.8 3.9 fusion.90
  140.8 3.9 fusion.90
  144.7 3.9 fusion.90
  148.8 11.9 %while.110 = (s32[]{:T(128)}, f32[1024,128]{1,0:T(8,128)S(1)}, bf16[3,2048,64]{2,1,0:T(8,128)(2,1)}, bf16[1024,64]{1,0:T(8,128)(2,1)S(1)}, bf16[3,2048,128]{2,1,0:T(8,128)(2,1)}, /*index=5*/s32[]{:T(128)}, s32[]{:T(128)}) while((s32[]{:T(128)}, f32[1024,128]{1,0:T(8,128)S(1)}, bf16[3,2048,64]{2,1,0:T(8,128)(2,1)}, ...), condition=%wide.region_6.6_spmd.clone, body=%wide.region_5.5_spmd.clone.sunk | while | flops 811859968 | bytes 2229854 | solution.py:47
  148.8 3.9 fusion.90
  152.8 3.9 fusion.90
  156.8 4.0 fusion.90
  161.8 65.9 %reduce-scatter.3.cloned.1.call-done = f32[128,128]{1,0:T(8,128)} async-done(((f32[2048,128]{1,0:T(8,128)}), f32[128,128]{1,0:T(8,128)}) %reduce-scatter.3.cloned.1.call-update) | async-done | bytes 65552 | tf_op jit(solution)/shard_map/reduce_scatter | solution.py:78
  229.8 67.1 %pmax.29 = f32[128]{0:T(128)S(1)} all-reduce(f32[128]{0:T(128)S(1)} %get-tuple-element.580), channel_id=1, replica_groups=mesh['blk'=8,'dom'=16] {'blk','dom'}, use_global_device_ids=true, to_apply=%region_10.11 | all-reduce | flops 128 | bytes 1024 | tf_op jit(solution)/shard_map/pmax | solution.py:54
  299.2 14.0 %all-gather.10.cloned.1.call-done = bf16[16384,64]{0,1:T(8,128)(2,1)} async-done(((bf16[2048,64]{0,1:T(8,128)(2,1)}), bf16[16384,64]{0,1:T(8,128)(2,1)}) %all-gather.10.cloned.1.call-update) | async-done | bytes 2097168 | tf_op jit(solution)/shard_map/all_gather | solution.py:85
  313.2 4.8 copy.9
  318.0 54.0 %all-gather.14.cloned.1.call-done = bf16[16384,128]{1,0:T(8,128)(2,1)} async-done(((bf16[2048,128]{1,0:T(8,128)(2,1)}), bf16[16384,128]{1,0:T(8,128)(2,1)}) %all-gather.14.cloned.1.call-update) | async-done | bytes 4194320 | tf_op jit(solution)/shard_map/all_gather | solution.py:86
  372.0 26.9 %while.108 = (s32[]{:T(128)}, f32[768,128]{1,0:T(8,128)S(1)}, bf16[8,2048,64]{2,1,0:T(8,128)(2,1)}, bf16[768,64]{1,0:T(8,128)(2,1)S(1)}, bf16[8,2048,128]{2,1,0:T(8,128)(2,1)}, /*index=5*/s32[]{:T(128)}, s32[]{:T(128)}) while((s32[]{:T(128)}, f32[768,128]{1,0:T(8,128)S(1)}, bf16[8,2048,64]{2,1,0:T(8,128)(2,1)}, ...), condition=%wide.region_12.13_spmd.clone, body=%wide.region_11.12_spmd.clone.sunk | while | flops 608894976 | bytes 1934942 | solution.py:47
  372.0 3.4 fusion.78
  375.4 3.3 fusion.78
  378.8 3.3 fusion.78
  385.5 3.3 fusion.78
  388.9 3.3 fusion.78
  392.3 3.3 fusion.78
  395.6 3.3 fusion.78
  399.2 64.7 %pmax.30 = f32[128]{0:T(128)S(1)} all-reduce(f32[128]{0:T(128)S(1)} %fusion.50), channel_id=1, replica_groups=mesh['blk'=8,'dom'=16] {'blk','dom'}, use_global_device_ids=true, to_apply=%region_14.15 | all-reduce | flops 128 | bytes 1024 | tf_op jit(solution)/shard_map/pmax | solution.py:54
  464.9 31.1 %all-gather.16.cloned.1.call-done = bf16[6144,128]{1,0:T(8,128)(2,1)} async-done(((bf16[768,128]{1,0:T(8,128)(2,1)}), bf16[6144,128]{1,0:T(8,128)(2,1)}) %all-gather.16.cloned.1.call-update) | async-done | bytes 1572880 | tf_op jit(solution)/shard_map/all_gather | solution.py:76
  496.1 24.0 %while.107 = (s32[]{:T(128)}, f32[2,1024,128]{2,1,0:T(8,128)S(1)}, bf16[2,1024,64]{2,1,0:T(8,128)(2,1)S(1)}, bf16[3,2048,64]{2,1,0:T(8,128)(2,1)}, bf16[3,2048,1...) while((s32[]{:T(128)}, f32[2,1024,128]{2,1,0:T(8,128)S(1)}, ...), condition=%wide.region_18.19_spmd, body=%wide.region_15.18_spmd.sunk | while | flops 811859968 | bytes 3540747 | solution.py:50
  496.2 11.9 %while.111 = (s32[]{:T(128)}, f32[1024,128]{1,0:T(8,128)S(1)}, bf16[3,2048,64]{2,1,0:T(8,128)(2,1)}, bf16[1024,64]{1,0:T(8,128)(2,1)S(1)}, bf16[3,2048,128]{2,1,0:T(8,128)(2,1)}, /*index=5*/s32[]{:T(128)}, s32[]{:T(128)}) while((s32[]{:T(128)}, f32[1024,128]{1,0:T(8,128)S(1)}, bf16[3,2048,64]{2,1,0:T(8,128)(2,1)}, ...), condition=%wide.region_17.17_spmd.clone, body=%wide.region_16.16_spmd.clone.sunk | while | flops 811859968 | bytes 2229854 | solution.py:47
  496.2 3.9 fusion.86
  500.2 3.9 fusion.86
  504.1 3.9 fusion.86
  508.2 11.9 %while.111 = (s32[]{:T(128)}, f32[1024,128]{1,0:T(8,128)S(1)}, bf16[3,2048,64]{2,1,0:T(8,128)(2,1)}, bf16[1024,64]{1,0:T(8,128)(2,1)S(1)}, bf16[3,2048,128]{2,1,0:T(8,128)(2,1)}, /*index=5*/s32[]{:T(128)}, s32[]{:T(128)}) while((s32[]{:T(128)}, f32[1024,128]{1,0:T(8,128)S(1)}, bf16[3,2048,64]{2,1,0:T(8,128)(2,1)}, ...), condition=%wide.region_17.17_spmd.clone, body=%wide.region_16.16_spmd.clone.sunk | while | flops 811859968 | bytes 2229854 | solution.py:47
  508.2 3.9 fusion.86
  512.2 3.9 fusion.86
  516.2 3.9 fusion.86
  521.2 70.8 %reduce-scatter.5.cloned.1.call-done = f32[128,128]{1,0:T(8,128)} async-done(((f32[2048,128]{1,0:T(8,128)}), f32[128,128]{1,0:T(8,128)}) %reduce-scatter.5.cloned.1.call-update) | async-done | bytes 65552 | tf_op jit(solution)/shard_map/reduce_scatter | solution.py:78
  593.6 66.7 %pmax.31 = f32[128]{0:T(128)S(1)} all-reduce(f32[128]{0:T(128)S(1)} %get-tuple-element.578), channel_id=1, replica_groups=mesh['blk'=8,'dom'=16] {'blk','dom'}, use_global_device_ids=true, to_apply=%region_21.22 | all-reduce | flops 128 | bytes 1024 | tf_op jit(solution)/shard_map/pmax | solution.py:54
  662.5 48.9 %all-gather.20.cloned.1.call-done = bf16[16384,128]{1,0:T(8,128)(2,1)} async-done(((bf16[2048,128]{1,0:T(8,128)(2,1)}), bf16[16384,128]{1,0:T(8,128)(2,1)}) %all-gather.20.cloned.1.call-update) | async-done | bytes 4194320 | tf_op jit(solution)/shard_map/all_gather | solution.py:86
  711.4 26.9 %while.109 = (s32[]{:T(128)}, f32[768,128]{1,0:T(8,128)S(1)}, bf16[8,2048,64]{2,1,0:T(8,128)(2,1)}, bf16[768,64]{1,0:T(8,128)(2,1)S(1)}, bf16[8,2048,128]{2,1,0:T(8,128)(2,1)}, /*index=5*/s32[]{:T(128)}, s32[]{:T(128)}) while((s32[]{:T(128)}, f32[768,128]{1,0:T(8,128)S(1)}, bf16[8,2048,64]{2,1,0:T(8,128)(2,1)}, ...), condition=%wide.region_23.24_spmd.clone, body=%wide.region_22.23_spmd.clone.sunk | while | flops 608894976 | bytes 1934942 | solution.py:47
  711.4 3.3 fusion.82
  714.7 3.3 fusion.82
  718.1 3.3 fusion.82
  721.4 3.3 fusion.82
  724.8 3.3 fusion.82
  728.2 3.3 fusion.82
  731.5 3.3 fusion.82
  734.9 3.3 fusion.82
  (65 shorter events, 22.2 us)
Async XLA Ops:
  7.2 129.5 %all-gather.8.cloned.1.call-start = ((), (), s32[]{:S(2)}) async-start(), calls=%async_computation.2 | async-start | bytes 1769472 | tf_op jit(solution)/shard_map/all_gather | solution.py:76
  78.8 148.9 %reduce-scatter.3.cloned.1.call-start = ((), (), s32[]{:S(2)}) async-start(), calls=%async_computation.3 | async-start | bytes 1114112 | tf_op jit(solution)/shard_map/reduce_scatter | solution.py:78
  106.9 29.8 %copy-start.3 = (bf16[2048,64]{0,1:T(8,128)(2,1)}, bf16[2048,64]{0,1:T(8,128)(2,1)S(1)}, u32[]{:S(2)}) copy-start(bf16[2048,64]{0,1:T(8,128)(2,1)S(1)} %all_gather.28) | copy-start | bytes 786436
  136.7 91.0 %copy-start.4 = (s32[128,128]{1,0:T(8,128)S(1)}, s32[128,128]{1,0:T(8,128)}, u32[]{:S(2)}) copy-start(s32[128,128]{1,0:T(8,128)} %param.19) | copy-start | bytes 196612
  160.8 1.0 copy-start.1
  161.8 135.2 %all-gather.12.cloned.1.call-start = ((), (), s32[]{:S(2)}) async-start(), calls=%async_computation.5 | async-start | bytes 1114112 | tf_op jit(solution)/shard_map/all_gather | solution.py:81
  229.2 84.0 %all-gather.10.cloned.1.call-start = ((), (), s32[]{:S(2)}) async-start(), calls=%async_computation.4 | async-start | bytes 2359296 | tf_op jit(solution)/shard_map/all_gather | solution.py:85
  229.8 142.2 %all-gather.14.cloned.1.call-start = ((), (), s32[]{:S(2)}) async-start(), calls=%async_computation.6 | async-start | bytes 4718592 | tf_op jit(solution)/shard_map/all_gather | solution.py:86
  299.2 196.9 %all-gather.16.cloned.1.call-start = ((), (), s32[]{:S(2)}) async-start(), calls=%async_computation.7 | async-start | bytes 1769472 | tf_op jit(solution)/shard_map/all_gather | solution.py:76
  372.0 27.0 %copy-start.2 = (s32[768,128]{1,0:T(8,128)S(1)}, s32[768,128]{1,0:T(8,128)}, u32[]{:S(2)}) copy-start(s32[768,128]{1,0:T(8,128)} %param.20) | copy-start | bytes 1179652
  464.7 127.3 %reduce-scatter.5.cloned.1.call-start = ((), (), s32[]{:S(2)}) async-start(), calls=%async_computation.8 | async-start | bytes 1114112 | tf_op jit(solution)/shard_map/reduce_scatter | solution.py:78
  520.2 1.0 copy-start
  521.2 139.1 %all-gather.18.cloned.1.call-start = ((), (), s32[]{:S(2)}) async-start(), calls=%async_computation.9 | async-start | bytes 1114112 | tf_op jit(solution)/shard_map/all_gather | solution.py:81
  593.5 117.8 %all-gather.20.cloned.1.call-start = ((), (), s32[]{:S(2)}) async-start(), calls=%async_computation.10 | async-start | bytes 4718592 | tf_op jit(solution)/shard_map/all_gather | solution.py:86
Sparse Core Ops, SparseCore 0:
  78.9 31.5 all-gather.7
  161.9 65.7 reduce-scatter.2
  230.7 46.2 all-gather.11
  279.1 34.1 all-gather.9
  314.7 57.2 all-gather.13
  464.8 31.1 all-gather.15
  521.3 70.6 reduce-scatter.4
  595.0 46.1 all-gather.17
  662.6 48.6 all-gather.19
where the time goes:
time: 747 us; the launch traced here: 746 us
  blocking collectives  322 us (43%)
  waiting for transfers between devices  285 us (38%)
  matrix products  101 us (14%)
  other arithmetic  14 us (2%)
  between operations  14 us (2%)
  local copies, waits for them, and re-layouts  8.45 us (1%)
    pmax x4, blocking collectives, column_peak(): return lax.pmax(jnp.max(values, axis=0), ('blk', 'dom'))  267 us
    reduce_scatter x2, waiting for transfers between devices, body(): lax.psum_scatter(partial_value, 'dom', scatter_dimension=0, tiled=True)  137 us
    all_gather x2, waiting for transfers between devices, body(): lax.all_gather(weights, 'blk', axis=0, tiled=True)  103 us
    dot_general x28, matrix products, add_block(): jnp.dot(kernel, weight_piece, preferred_element_type=jnp.float32)  101 us
    all_gather x2, waiting for transfers between devices, body(): lax.all_gather(scaled, 'blk', axis=0, tiled=True)  31.1 us
    all_gather x1, blocking collectives, body(): target_group = lax.all_gather(own_targets, 'blk', axis=0, tiled=True)  28 us
    all_gather x1, blocking collectives, body(): lax.all_gather(normalized(source_emb), 'dom', axis=0, tiled=True)  26.6 us
  transfers between devices with their start and end apart: 9, of which 6 were waited for; matrix products, arithmetic and copies ran while one was open for 1% of the time, Pallas kernels for 0%

commit v1 on v0

v1 whole, which is shorter than its diff:
```python
import math

import jax
import jax.numpy as jnp
from jax import lax
from jax.sharding import PartitionSpec as P

ITERS = 2


entropic = 0.05


def normalized(values):
    widened = values.astype(jnp.float32)
    squared = jnp.sum(widened * widened, axis=1, keepdims=True) + 1e-06
    return (widened * lax.rsqrt(squared)).astype(jnp.bfloat16)


def kernel_block(row_piece, col_piece):
    products = jnp.dot(row_piece, col_piece.T, preferred_element_type=jnp.float32)
    return jnp.exp((products - 1.0) / entropic).astype(jnp.bfloat16)


def segment_sums(row_emb, col_segments, weight_segments, factors, row_block):
    row_count = row_emb.shape[0]
    row_parts = row_emb.reshape(row_count // row_block, row_block, row_emb.shape[1])

    def one_block(row_piece):

        def add_segment(running, paired):
            col_piece, weight_piece, factor = paired
            kernel = kernel_block(row_piece, col_piece)
            part = jnp.dot(kernel, weight_piece, preferred_element_type=jnp.float32)
            return (running + factor[None, :] * part, None)

        initial = jnp.zeros((row_piece.shape[0], weight_segments.shape[-1]), jnp.float32)
        result, unused = lax.scan(add_segment, initial, (col_segments, weight_segments, factors))
        return result

    return lax.map(one_block, row_parts).reshape(row_count, weight_segments.shape[-1])


def plain_sums(row_emb, col_emb, col_weights, row_block, col_block):
    col_count = col_emb.shape[0]
    segments = col_count // col_block
    return segment_sums(
        row_emb,
        col_emb.reshape(segments, col_block, col_emb.shape[1]),
        col_weights.reshape(segments, col_block, col_weights.shape[1]),
        jnp.ones((segments, col_weights.shape[1]), jnp.float32),
        row_block,
    )


def permute_gather(value, axis, count):
    me = lax.axis_index(axis)
    received = [value]
    for shift in range(1, count):
        received.append(lax.ppermute(value, axis, [(i, (i + shift) % count) for i in range(count)]))
    stacked = jnp.stack(received[::-1], 0)
    return jnp.roll(stacked, me + 1, axis=0)


def shift_of(values):
    return jnp.max(values, axis=0).astype(jnp.bfloat16).astype(jnp.float32)


def padded_rows(rows, multiple):
    return -(-rows // multiple) * multiple


def body(source_emb, target_emb, source_counts, target_counts, warm_start):
    blk_count = lax.axis_size("blk")
    dom_count = lax.axis_size("dom")
    src_rows = source_emb.shape[0]
    tgt_rows = target_emb.shape[0]
    columns = warm_start.shape[1]
    width = source_emb.shape[1]
    all_sources = src_rows * blk_count * dom_count
    all_targets = tgt_rows * blk_count * dom_count
    block_rows = src_rows * dom_count
    group_rows = tgt_rows * blk_count

    source_block = lax.all_gather(normalized(source_emb), "dom", axis=0, tiled=True)
    own_targets = normalized(target_emb)
    log_target = jnp.log(target_counts.astype(jnp.float32)) - math.log(all_targets)
    log_source = jnp.log(source_counts.astype(jnp.float32)) - math.log(all_sources)

    tgt_payload_rows = padded_rows(tgt_rows + 1, 16)
    src_piece_rows = padded_rows(src_rows + 1, 8)
    tgt_piece_rows = padded_rows(tgt_rows + 1, 8)

    target_logs = warm_start
    target_group = None
    source_logs = None
    for iteration in range(ITERS):
        shift = shift_of(target_logs)
        weights = jnp.exp(target_logs - shift).astype(jnp.bfloat16)
        payload = jnp.concatenate(
            [weights, shift.astype(jnp.bfloat16)[None, :],
             jnp.zeros((tgt_payload_rows - tgt_rows - 1, columns), jnp.bfloat16)], axis=0)
        if target_group is None:
            emb_rows = jnp.concatenate(
                [own_targets, jnp.zeros((tgt_payload_rows - tgt_rows, width), jnp.bfloat16)], axis=0)
            payload = jnp.concatenate([emb_rows, payload], axis=1)
            gathered = permute_gather(payload, "blk", blk_count)
            target_group = gathered[:, :tgt_rows, :width].reshape(group_rows, width)
            gathered = gathered[:, :, width:]
        else:
            gathered = permute_gather(payload, "blk", blk_count)
        weight_segments = gathered[:, :tgt_rows, :]
        segment_shift = gathered[:, tgt_rows, :].astype(jnp.float32)
        group_shift = jnp.max(segment_shift, axis=0)
        factors = jnp.exp(segment_shift - group_shift[None, :])
        partial_value = segment_sums(
            source_block,
            target_group.reshape(blk_count, tgt_rows, width),
            weight_segments,
            factors,
            min(block_rows, 1024),
        )
        pieces = jnp.concatenate(
            [partial_value.reshape(dom_count, src_rows, columns),
             jnp.broadcast_to(group_shift[None, None, :], (dom_count, 1, columns)),
             jnp.zeros((dom_count, src_piece_rows - src_rows - 1, columns), jnp.float32)], axis=1)
        received = lax.all_to_all(pieces, "dom", 0, 0, tiled=False)
        group_shifts = received[:, src_rows, :]
        target_peak = jnp.max(group_shifts, axis=0)
        scale = jnp.exp(group_shifts - target_peak[None, :])
        shares = jnp.sum(received[:, :src_rows, :] * scale[:, None, :], axis=0)
        source_logs = log_source - target_peak - jnp.log(shares)

        block_logs = lax.all_gather(source_logs, "dom", axis=0, tiled=True)
        block_peak = jnp.max(block_logs, axis=0)
        source_weights = jnp.exp(block_logs - block_peak).astype(jnp.bfloat16)
        target_partial = plain_sums(target_group, source_block, source_weights, 1024, block_rows)
        pieces = jnp.concatenate(
            [target_partial.reshape(blk_count, tgt_rows, columns),
             jnp.broadcast_to(block_peak[None, None, :], (blk_count, 1, columns)),
             jnp.zeros((blk_count, tgt_piece_rows - tgt_rows - 1, columns), jnp.float32)], axis=1)
        received = lax.all_to_all(pieces, "blk", 0, 0, tiled=False)
        block_peaks = received[:, tgt_rows, :]
        source_peak = jnp.max(block_peaks, axis=0)
        scale = jnp.exp(block_peaks - source_peak[None, :])
        target_sums = jnp.sum(received[:, :tgt_rows, :] * scale[:, None, :], axis=0)
        target_logs = log_target - source_peak - jnp.log(target_sums)
    return (source_logs, target_logs)


def solution(mesh):
    in_specs = (
        P(("blk", "dom"), None),
        P(("blk", "dom"), None),
        P(("blk", "dom"), None),
        P(("blk", "dom"), None),
        P(("blk", "dom"), None),
    )
    out_specs = (P(("blk", "dom"), None), P(("blk", "dom"), None))
    return jax.shard_map(body, mesh=mesh, in_specs=in_specs, out_specs=out_specs, check_vma=False)
```

time: 747 us -> 485 us (0.65)
  waiting for transfers between devices: 285 us -> 111 us
  blocking collectives: 322 us -> 164 us
  starting transfers between devices: 0.55 us -> 39.2 us
  matrix products: 101 us -> 123 us
    pmax x4 -> x0, blocking collectives: 267 us -> none  [column_peak(): return lax.pmax(jnp.max(values, axis=0), ('blk', 'dom'))]
    all_gather x5 -> x0, waiting for transfers between devices: 148 us -> none  [the longest x2 103 us: body(): lax.all_gather(weights, 'blk', axis=0, tiled=True)]
    reduce_scatter x2 -> x0, waiting for transfers between devices: 137 us -> none  [body(): lax.psum_scatter(partial_value, 'dom', scatter_dimension=0, tiled=True)]
    all_to_all x0 -> x4, blocking collectives: none -> 134 us  [the longest x2 84.8 us: body(): received = lax.all_to_all(pieces, 'blk', 0, 0, tiled=False)]
    all_gather x2, waiting for transfers between devices: 0.02 us -> 81 us  [body(): block_logs = lax.all_gather(source_logs, 'dom', axis=0, tiled=True)]
    ppermute x0 -> x14, starting transfers between devices: none -> 39.2 us  [permute_gather(): lax.ppermute(value, axis, [(i, (i + shift) % count) for i in range(count)])]
    ppermute x0 -> x14, waiting for transfers between devices: none -> 30.1 us  [permute_gather(): lax.ppermute(value, axis, [(i, (i + shift) % count) for i in range(count)])]
    all_gather x1 -> x0, blocking collectives: 28 us -> none  [body(): target_group = lax.all_gather(own_targets, 'blk', axis=0, tiled=True)]
  transfers between devices with their start and end apart: 9 -> 16, of which waited for: 6 -> 9; matrix products, arithmetic and copies ran while one was open for 1% -> 1% of each run, Pallas kernels for 0% -> 0%
where the time goes in v1:
time: 485 us; the launch traced here: 483 us
  blocking collectives  164 us (34%)
  matrix products  123 us (25%)
  waiting for transfers between devices  111 us (23%)
  starting transfers between devices  39.2 us (8%)
  other arithmetic  19.9 us (4%)
  between operations  14.5 us (3%)
  local copies, waits for them, and re-layouts  9.53 us (2%)
    dot_general x44, matrix products, add_segment(): part = jnp.dot(kernel, weight_piece, preferred_element_type=jnp.float32)  123 us
    all_to_all x2, blocking collectives, body(): received = lax.all_to_all(pieces, 'blk', 0, 0, tiled=False)  84.8 us
    all_gather x2, waiting for transfers between devices, body(): block_logs = lax.all_gather(source_logs, 'dom', axis=0, tiled=True)  81 us
    all_to_all x2, blocking collectives, body(): received = lax.all_to_all(pieces, 'dom', 0, 0, tiled=False)  48.8 us
    ppermute x14, starting transfers between devices, permute_gather(): lax.ppermute(value, axis, [(i, (i + shift) % count) for i in range(count)])  39.2 us
    all_gather x1, blocking collectives, body(): lax.all_gather(normalized(source_emb), 'dom', axis=0, tiled=True)  30.5 us
    ppermute x14, waiting for transfers between devices, permute_gather(): lax.ppermute(value, axis, [(i, (i + shift) % count) for i in range(count)])  30.1 us
  transfers between devices with their start and end apart: 16, of which 9 were waited for; matrix products, arithmetic and copies ran while one was open for 1% of the time, Pallas kernels for 0%

profile of v1, /device:TPU:1, one launch (start us, length us, event | category | flops | bytes accessed | tf_op | source)
XLA Modules:
  0.0 483.0 jit_solution(5146353734694326220)
XLA Ops:
  12.3 4.3 collective-permute-start
  21.5 30.5 %all_gather.9 = bf16[2048,64]{0,1:T(8,128)(2,1)S(1)} all-gather(bf16[128,64]{0,1:T(8,128)(2,1)S(1)} %fusion.68), channel_id=1, replica_groups=mesh['blk'=8,'dom'=16] {'dom'}, dimensions={0}, use_global_device_ids=true | all-gather | bytes 278528 | tf_op jit(solution)/shard_map/all_gather | solution.py:85
  52.4 21.2 %collective-permute-start.5 = (bf16[784,192]{1,0:T(8,128)(2,1)}, bf16[784,192]{1,0:T(8,128)(2,1)S(1)}, u32[]{:S(2)}, u32[]{:S(2)}) collective-permute-start(bf16[784,192]{1,0:T(8,128)(2,1)} %fusion.63), channel_id=1, source_target_pairs={{0,32},{16,48},{32,64},{48,80},{64,96},{80,112},{96,0},{112,16},{1... | collective-permute-start | bytes 903176 | tf_op jit(solution)/shard_map/ppermute | solution.py:60
  73.9 9.4 %collective-permute-done.5 = bf16[784,192]{1,0:T(8,128)(2,1)S(1)} collective-permute-done((bf16[784,192]{1,0:T(8,128)(2,1)}, bf16[784,192]{1,0:T(8,128)(2,1)S(1)}, u32[]{:S(2)}, u32[]{:S(2)}) %collective-permute-start.5) | collective-permute-done | bytes 301088 | tf_op jit(solution)/shard_map/ppermute | solution.py:60
  83.4 8.8 %collective-permute-done.6 = bf16[784,192]{1,0:T(8,128)(2,1)S(1)} collective-permute-done((bf16[784,192]{1,0:T(8,128)(2,1)}, bf16[784,192]{1,0:T(8,128)(2,1)S(1)}, u32[]{:S(2)}, u32[]{:S(2)}) %collective-permute-start.6) | collective-permute-done | bytes 301088 | tf_op jit(solution)/shard_map/ppermute | solution.py:60
  96.2 38.7 %while.97 = (s32[]{:T(128)}, f32[2,1024,128]{2,1,0:T(8,128)S(1)}, bf16[2,1024,64]{2,1,0:T(8,128)(2,1)S(1)}, f32[8,128]{1,0:T(8,128)S(1)}, bf16[8,768,64]{2,1,0:T...) while((s32[]{:T(128)}, f32[2,1024,128]{2,1,0:T(8,128)S(1)}, ...), condition=%wide.region_7.8_spmd, body=%wide.region_4.7_spmd.sunk | while | flops 304742400 | bytes 2886424 | solution.py:41
  96.2 19.2 %while.102 = (s32[]{:T(128)}, f32[1024,128]{1,0:T(8,128)S(1)}, f32[8,128]{1,0:T(8,128)S(1)}, bf16[8,768,64]{2,1,0:T(8,128)(2,1)}, bf16[1024,64]{1,0:T(8,128)(2,1...) while((s32[]{:T(128)}, f32[1024,128]{1,0:T(8,128)S(1)}, f32[8,128]{1,0:T(8,128)S(1)}, ...), condition=%wide.region_6.6_spmd.clone, body=%wide.region_5.5_spmd.clone.sunk | while | flops 304742400 | bytes 1575523 | solution.py:38
  103.5 2.4 fusion.106
  108.3 2.4 fusion.106
  113.1 2.4 fusion.106
  115.6 19.2 %while.102 = (s32[]{:T(128)}, f32[1024,128]{1,0:T(8,128)S(1)}, f32[8,128]{1,0:T(8,128)S(1)}, bf16[8,768,64]{2,1,0:T(8,128)(2,1)}, bf16[1024,64]{1,0:T(8,128)(2,1...) while((s32[]{:T(128)}, f32[1024,128]{1,0:T(8,128)S(1)}, f32[8,128]{1,0:T(8,128)S(1)}, ...), condition=%wide.region_6.6_spmd.clone, body=%wide.region_5.5_spmd.clone.sunk | while | flops 304742400 | bytes 1575523 | solution.py:38
  118.0 2.4 fusion.106
  122.8 2.4 fusion.106
  127.6 2.4 fusion.106
  132.5 2.4 fusion.106
  135.1 23.4 %all_to_all.20 = f32[16,136,128]{2,1,0:T(8,128)S(1)} all-to-all(f32[16,136,128]{2,1,0:T(8,128)S(1)} %maximum_maximum_fusion.2), channel_id=1, replica_groups=mesh['blk'=8,'dom'=16] {'dom'}, dimensions={0} | all-to-all | bytes 2228224 | tf_op jit(solution)/shard_map/all_to_all | solution.py:127
  159.7 40.3 %all-gather.3.cloned.1.call-done = f32[2048,128]{1,0:T(8,128)} async-done(((f32[128,128]{1,0:T(8,128)}), f32[2048,128]{1,0:T(8,128)}) %all-gather.3.cloned.1.call-update) | async-done | bytes 1048592 | tf_op jit(solution)/shard_map/all_gather | solution.py:134
  204.7 25.2 %while.98 = (s32[]{:T(128)}, f32[6,1024,128]{2,1,0:T(8,128)}, bf16[6,1024,64]{2,1,0:T(8,128)(2,1)}, bf16[1,2048,64]{2,1,0:T(8,128)(2,1)S(1)}, bf16[1,2048,128]{2,1,0:T(8,128)(2,1)S(1)}, /*index=5*/s32[]{:T(128)}) while((s32[]{:T(128)}, f32[6,1024,128]{2,1,0:T(8,128)}, bf16[6,1024,64]{2,1,0:T(8,128)(2,1)}, ...), condition=%wide.region_12.13_spmd, body=%wide.region_11.12_spmd.sunk | while | flops 811597824 | bytes 1573957 | solution.py:41
  204.7 4.2 fusion.92
  208.9 4.2 fusion.92
  213.1 4.2 fusion.92
  217.3 4.2 fusion.92
  221.5 4.2 fusion.92
  225.7 4.2 fusion.92
  232.3 42.4 %all_to_all.21 = f32[8,776,128]{2,1,0:T(8,128)S(1)} all-to-all(f32[8,776,128]{2,1,0:T(8,128)S(1)} %maximum_maximum_fusion), channel_id=1, replica_groups=mesh['blk'=8,'dom'=16] {'blk'}, dimensions={0} | all-to-all | bytes 6356992 | tf_op jit(solution)/shard_map/all_to_all | solution.py:142
  279.0 2.7 collective-permute-start.11
  283.2 3.2 collective-permute-start.13
  286.4 3.5 collective-permute-done.9
  293.0 5.3 %collective-permute-done.13 = bf16[784,128]{1,0:T(8,128)(2,1)S(1)} collective-permute-done((bf16[784,128]{1,0:T(8,128)(2,1)S(1)}, bf16[784,128]{1,0:T(8,128)(2,1)S(1)}, u32[]{:S(2)}, u32[]{:S(2)}) %collective-permute-start.13) | collective-permute-done | bytes 200736 | tf_op jit(solution)/shard_map/ppermute | solution.py:60
  300.1 38.7 %while.100 = (s32[]{:T(128)}, f32[2,1024,128]{2,1,0:T(8,128)S(1)}, bf16[2,1024,64]{2,1,0:T(8,128)(2,1)S(1)}, f32[8,128]{1,0:T(8,128)S(1)}, bf16[8,768,64]{2,1,0:...) while((s32[]{:T(128)}, f32[2,1024,128]{2,1,0:T(8,128)S(1)}, ...), condition=%wide.region_20.21_spmd, body=%wide.region_17.20_spmd.sunk | while | flops 304742400 | bytes 2886424 | solution.py:41
  300.2 19.2 %while.103 = (s32[]{:T(128)}, f32[1024,128]{1,0:T(8,128)S(1)}, f32[8,128]{1,0:T(8,128)S(1)}, bf16[8,768,64]{2,1,0:T(8,128)(2,1)}, bf16[1024,64]{1,0:T(8,128)(2,1...) while((s32[]{:T(128)}, f32[1024,128]{1,0:T(8,128)S(1)}, ...), condition=%wide.region_19.19_spmd.clone, body=%wide.region_18.18_spmd.clone.sunk | while | flops 304742400 | bytes 1575523 | solution.py:38
  305.0 2.4 fusion.101
  309.8 2.4 fusion.101
  314.6 2.4 fusion.101
  319.5 19.2 %while.103 = (s32[]{:T(128)}, f32[1024,128]{1,0:T(8,128)S(1)}, f32[8,128]{1,0:T(8,128)S(1)}, bf16[8,768,64]{2,1,0:T(8,128)(2,1)}, bf16[1024,64]{1,0:T(8,128)(2,1...) while((s32[]{:T(128)}, f32[1024,128]{1,0:T(8,128)S(1)}, ...), condition=%wide.region_19.19_spmd.clone, body=%wide.region_18.18_spmd.clone.sunk | while | flops 304742400 | bytes 1575523 | solution.py:38
  324.4 2.4 fusion.101
  329.2 2.4 fusion.101
  334.0 2.4 fusion.101
  339.0 25.5 %all_to_all.22 = f32[16,136,128]{2,1,0:T(8,128)S(1)} all-to-all(f32[16,136,128]{2,1,0:T(8,128)S(1)} %maximum_maximum_fusion.3), channel_id=1, replica_groups=mesh['blk'=8,'dom'=16] {'dom'}, dimensions={0} | all-to-all | bytes 2228224 | tf_op jit(solution)/shard_map/all_to_all | solution.py:127
  365.3 40.7 %all-gather.5.cloned.1.call-done = f32[2048,128]{1,0:T(8,128)} async-done(((f32[128,128]{1,0:T(8,128)}), f32[2048,128]{1,0:T(8,128)}) %all-gather.5.cloned.1.call-update) | async-done | bytes 1048592 | tf_op jit(solution)/shard_map/all_gather | solution.py:134
  409.9 22.4 %while.101 = (s32[]{:T(128)}, f32[6,1024,128]{2,1,0:T(8,128)S(1)}, bf16[6,1024,64]{2,1,0:T(8,128)(2,1)}, bf16[1,2048,64]{2,1,0:T(8,128)(2,1)}, bf16[1,2048,128]{2,1,0:T(8,128)(2,1)}, /*index=5*/s32[]{:T(128)}) while((s32[]{:T(128)}, f32[6,1024,128]{2,1,0:T(8,128)S(1)}, bf16[6,1024,64]{2,1,0:T(8,128)(2,1)}, bf16[1,2048,64]{2,1,0:T(8,128)(2,1)}, ...), condition=%wide.region_25.26_spmd, body=%wide.region_24.25_spmd.sunk | while | flops 811597824 | bytes 1836101 | solution.py:41
  409.9 3.7 fusion.96
  413.6 3.7 fusion.96
  417.3 3.7 fusion.96
  421.1 3.7 fusion.96
  424.8 3.7 fusion.96
  428.5 3.7 fusion.96
  432.6 42.4 %all_to_all.23 = f32[8,776,128]{2,1,0:T(8,128)S(1)} all-to-all(f32[8,776,128]{2,1,0:T(8,128)S(1)} %maximum_maximum_fusion.1), channel_id=1, replica_groups=mesh['blk'=8,'dom'=16] {'blk'}, dimensions={0} | all-to-all | bytes 6356992 | tf_op jit(solution)/shard_map/all_to_all | solution.py:142
  (186 shorter events, 85.3 us)
Async XLA Ops:
  7.2 192.8 %all-gather.3.cloned.1.call-start = ((), (), s32[]{:S(2)}) async-start(), calls=%async_computation.4 | async-start | bytes 1114112 | tf_op jit(solution)/shard_map/all_gather | solution.py:134
  12.3 40.0 %collective-permute-start = (bf16[784,192]{1,0:T(8,128)(2,1)}, bf16[784,192]{1,0:T(8,128)(2,1)S(1)}, u32[]{:S(2)}, u32[]{:S(2)}) collective-permute-start(bf16[784,192]{1,0:T(8,128)(2,1)} %fusion.63), channel_id=1, source_target_pairs={{0,112},{16,0},{32,16},{48,32},{64,48},{80,64},{96,80},{112,96},{1... | collective-permute-start | bytes 903176 | tf_op jit(solution)/shard_map/ppermute | solution.py:60
  16.7 57.0 %collective-permute-start.1 = (bf16[784,192]{1,0:T(8,128)(2,1)}, bf16[784,192]{1,0:T(8,128)(2,1)S(1)}, u32[]{:S(2)}, u32[]{:S(2)}) collective-permute-start(bf16[784,192]{1,0:T(8,128)(2,1)} %fusion.63), channel_id=1, source_target_pairs={{0,96},{16,112},{32,0},{48,16},{64,32},{80,48},{96,64},{112,80},{1... | collective-permute-start | bytes 903176 | tf_op jit(solution)/shard_map/ppermute | solution.py:60
  17.2 56.6 %collective-permute-start.2 = (bf16[784,192]{1,0:T(8,128)(2,1)}, bf16[784,192]{1,0:T(8,128)(2,1)S(1)}, u32[]{:S(2)}, u32[]{:S(2)}) collective-permute-start(bf16[784,192]{1,0:T(8,128)(2,1)} %fusion.63), channel_id=1, source_target_pairs={{0,80},{16,96},{32,112},{48,0},{64,16},{80,32},{96,48},{112,64},{1... | collective-permute-start | bytes 903176 | tf_op jit(solution)/shard_map/ppermute | solution.py:60
  17.7 56.2 %collective-permute-start.3 = (bf16[784,192]{1,0:T(8,128)(2,1)}, bf16[784,192]{1,0:T(8,128)(2,1)S(1)}, u32[]{:S(2)}, u32[]{:S(2)}) collective-permute-start(bf16[784,192]{1,0:T(8,128)(2,1)} %fusion.63), channel_id=1, source_target_pairs={{0,64},{16,80},{32,96},{48,112},{64,0},{80,16},{96,32},{112,48},{1... | collective-permute-start | bytes 903176 | tf_op jit(solution)/shard_map/ppermute | solution.py:60
  19.0 54.9 %collective-permute-start.4 = (bf16[784,192]{1,0:T(8,128)(2,1)}, bf16[784,192]{1,0:T(8,128)(2,1)S(1)}, u32[]{:S(2)}, u32[]{:S(2)}) collective-permute-start(bf16[784,192]{1,0:T(8,128)(2,1)} %fusion.63), channel_id=1, source_target_pairs={{0,48},{16,64},{32,80},{48,96},{64,112},{80,0},{96,16},{112,32},{1... | collective-permute-start | bytes 903176 | tf_op jit(solution)/shard_map/ppermute | solution.py:60
  52.4 31.0 %collective-permute-start.5 = (bf16[784,192]{1,0:T(8,128)(2,1)}, bf16[784,192]{1,0:T(8,128)(2,1)S(1)}, u32[]{:S(2)}, u32[]{:S(2)}) collective-permute-start(bf16[784,192]{1,0:T(8,128)(2,1)} %fusion.63), channel_id=1, source_target_pairs={{0,32},{16,48},{32,64},{48,80},{64,96},{80,112},{96,0},{112,16},{1... | collective-permute-start | bytes 903176 | tf_op jit(solution)/shard_map/ppermute | solution.py:60
  73.7 18.5 %collective-permute-start.6 = (bf16[784,192]{1,0:T(8,128)(2,1)}, bf16[784,192]{1,0:T(8,128)(2,1)S(1)}, u32[]{:S(2)}, u32[]{:S(2)}) collective-permute-start(bf16[784,192]{1,0:T(8,128)(2,1)} %fusion.63), channel_id=1, source_target_pairs={{0,16},{16,32},{32,48},{48,64},{64,80},{80,96},{96,112},{112,0},{1... | collective-permute-start | bytes 903176 | tf_op jit(solution)/shard_map/ppermute | solution.py:60
  134.9 23.7 %copy-start.2 = (s32[128,128]{1,0:T(8,128)S(1)}, s32[128,128]{1,0:T(8,128)}, u32[]{:S(2)}) copy-start(s32[128,128]{1,0:T(8,128)} %param.19) | copy-start | bytes 196612
  159.3 246.7 %all-gather.5.cloned.1.call-start = ((), (), s32[]{:S(2)}) async-start(), calls=%async_computation.5 | async-start | bytes 1114112 | tf_op jit(solution)/shard_map/all_gather | solution.py:134
  229.9 44.8 %copy-start.1 = (bf16[1,2048,64]{2,1,0:T(8,128)(2,1)}, bf16[1,2048,64]{2,1,0:T(8,128)(2,1)S(1)}, u32[]{:S(2)}) copy-start(bf16[1,2048,64]{2,1,0:T(8,128)(2,1)S(1)} %get-tuple-element.1044) | copy-start | bytes 786436
  274.7 1.0 copy-start
  276.1 5.7 %collective-permute-start.7 = (bf16[784,128]{1,0:T(8,128)(2,1)S(1)}, bf16[784,128]{1,0:T(8,128)(2,1)S(1)}, u32[]{:S(2)}, u32[]{:S(2)}) collective-permute-start(bf16[784,128]{1,0:T(8,128)(2,1)S(1)} %pad_maximum_fusion), channel_id=1, source_target_pairs={{0,112},{16,0},{32,16},{48,32},{64,48},{80,64},{96,80},{112,96},{1... | collective-permute-start | bytes 602120 | tf_op jit(solution)/shard_map/ppermute | solution.py:60
  276.7 6.5 %collective-permute-start.8 = (bf16[784,128]{1,0:T(8,128)(2,1)S(1)}, bf16[784,128]{1,0:T(8,128)(2,1)S(1)}, u32[]{:S(2)}, u32[]{:S(2)}) collective-permute-start(bf16[784,128]{1,0:T(8,128)(2,1)S(1)} %pad_maximum_fusion), channel_id=1, source_target_pairs={{0,96},{16,112},{32,0},{48,16},{64,32},{80,48},{96,64},{112,80},{1... | collective-permute-start | bytes 602120 | tf_op jit(solution)/shard_map/ppermute | solution.py:60
  277.8 12.0 %collective-permute-start.9 = (bf16[784,128]{1,0:T(8,128)(2,1)S(1)}, bf16[784,128]{1,0:T(8,128)(2,1)S(1)}, u32[]{:S(2)}, u32[]{:S(2)}) collective-permute-start(bf16[784,128]{1,0:T(8,128)(2,1)S(1)} %pad_maximum_fusion), channel_id=1, source_target_pairs={{0,80},{16,96},{32,112},{48,0},{64,16},{80,32},{96,48},{112,64},{1... | collective-permute-start | bytes 602120 | tf_op jit(solution)/shard_map/ppermute | solution.py:60
  278.6 11.2 %collective-permute-start.10 = (bf16[784,128]{1,0:T(8,128)(2,1)S(1)}, bf16[784,128]{1,0:T(8,128)(2,1)S(1)}, u32[]{:S(2)}, u32[]{:S(2)}) collective-permute-start(bf16[784,128]{1,0:T(8,128)(2,1)S(1)} %pad_maximum_fusion), channel_id=1, source_target_pairs={{0,64},{16,80},{32,96},{48,112},{64,0},{80,16},{96,32},{112,48},{1... | collective-permute-start | bytes 602120 | tf_op jit(solution)/shard_map/ppermute | solution.py:60
  279.0 11.8 %collective-permute-start.11 = (bf16[784,128]{1,0:T(8,128)(2,1)S(1)}, bf16[784,128]{1,0:T(8,128)(2,1)S(1)}, u32[]{:S(2)}, u32[]{:S(2)}) collective-permute-start(bf16[784,128]{1,0:T(8,128)(2,1)S(1)} %pad_maximum_fusion), channel_id=1, source_target_pairs={{0,48},{16,64},{32,80},{48,96},{64,112},{80,0},{96,16},{112,32},{1... | collective-permute-start | bytes 602120 | tf_op jit(solution)/shard_map/ppermute | solution.py:60
  281.8 11.2 %collective-permute-start.12 = (bf16[784,128]{1,0:T(8,128)(2,1)S(1)}, bf16[784,128]{1,0:T(8,128)(2,1)S(1)}, u32[]{:S(2)}, u32[]{:S(2)}) collective-permute-start(bf16[784,128]{1,0:T(8,128)(2,1)S(1)} %pad_maximum_fusion), channel_id=1, source_target_pairs={{0,32},{16,48},{32,64},{48,80},{64,96},{80,112},{96,0},{112,16},{1... | collective-permute-start | bytes 602120 | tf_op jit(solution)/shard_map/ppermute | solution.py:60
  283.2 15.2 %collective-permute-start.13 = (bf16[784,128]{1,0:T(8,128)(2,1)S(1)}, bf16[784,128]{1,0:T(8,128)(2,1)S(1)}, u32[]{:S(2)}, u32[]{:S(2)}) collective-permute-start(bf16[784,128]{1,0:T(8,128)(2,1)S(1)} %pad_maximum_fusion), channel_id=1, source_target_pairs={{0,16},{16,32},{32,48},{48,64},{64,80},{80,96},{96,112},{112,0},{1... | collective-permute-start | bytes 602120 | tf_op jit(solution)/shard_map/ppermute | solution.py:60
Sparse Core Ops, SparseCore 0:
  159.4 40.5 all-gather.2
  365.4 40.4 all-gather.4

commit v2 on v1

--- a/solution.py
+++ b/solution.py
@@ -94,6 +94,7 @@
     target_logs = warm_start
     target_group = None
     source_logs = None
+    kernel = None
     for iteration in range(ITERS):
         shift = shift_of(target_logs)
         weights = jnp.exp(target_logs - shift).astype(jnp.bfloat16)
@@ -113,13 +114,14 @@
         segment_shift = gathered[:, tgt_rows, :].astype(jnp.float32)
         group_shift = jnp.max(segment_shift, axis=0)
         factors = jnp.exp(segment_shift - group_shift[None, :])
-        partial_value = segment_sums(
-            source_block,
-            target_group.reshape(blk_count, tgt_rows, width),
-            weight_segments,
-            factors,
-            min(block_rows, 1024),
-        )
+        if kernel is None:
+            products = jnp.einsum(
+                "id,sjd->sij", source_block, target_group.reshape(blk_count, tgt_rows, width),
+                preferred_element_type=jnp.float32)
+            kernel = jnp.exp((products - 1.0) / entropic).astype(jnp.bfloat16)
+        per_segment = jnp.einsum(
+            "sij,sjc->sic", kernel, weight_segments, preferred_element_type=jnp.float32)
+        partial_value = jnp.sum(per_segment * factors[:, None, :], axis=0)
         pieces = jnp.concatenate(
             [partial_value.reshape(dom_count, src_rows, columns),
              jnp.broadcast_to(group_shift[None, None, :], (dom_count, 1, columns)),
@@ -131,10 +133,14 @@
         shares = jnp.sum(received[:, :src_rows, :] * scale[:, None, :], axis=0)
         source_logs = log_source - target_peak - jnp.log(shares)
 
-        block_logs = lax.all_gather(source_logs, "dom", axis=0, tiled=True)
+        block_logs = lax.all_to_all(
+            jnp.broadcast_to(source_logs[None], (dom_count, src_rows, columns)), "dom", 0, 0, tiled=False
+        ).reshape(block_rows, columns)
         block_peak = jnp.max(block_logs, axis=0)
         source_weights = jnp.exp(block_logs - block_peak).astype(jnp.bfloat16)
-        target_partial = plain_sums(target_group, source_block, source_weights, 1024, block_rows)
+        target_partial = jnp.einsum(
+            "ic,sij->sjc", source_weights, kernel, preferred_element_type=jnp.float32
+        ).reshape(group_rows, columns)
         pieces = jnp.concatenate(
             [target_partial.reshape(blk_count, tgt_rows, columns),
              jnp.broadcast_to(block_peak[None, None, :], (blk_count, 1, columns)),

time: 485 us -> 358 us (0.74)
  matrix products: 123 us -> 62.3 us
  waiting for transfers between devices: 111 us -> 77.1 us
  blocking collectives: 164 us -> 150 us
  between operations: 14.5 us -> 1.19 us
  other arithmetic: 19.9 us -> 11.5 us
  starting transfers between devices: 39.2 us -> 44.8 us
    all_gather x2 -> x0, waiting for transfers between devices: 81 us -> none  [body(): block_logs = lax.all_gather(source_logs, 'dom', axis=0, tiled=True)]
    dot_general x44 -> x5, matrix products: 123 us -> 62.3 us  [the longest x2 25.9 us: body(): jnp.einsum('sij,sjc->sic', kernel, weight_segments, preferred_element_typ...]
    all_to_all x0 -> x2, waiting for transfers between devices: none -> 55.7 us  [the longest x1 38.6 us: body(): received = lax.all_to_all(pieces, 'blk', 0, 0, tiled=False)]
    all_to_all x2 -> x1, blocking collectives: 84.8 us -> 45 us  [body(): received = lax.all_to_all(pieces, 'blk', 0, 0, tiled=False)]
    all_to_all x0 -> x1, blocking collectives: none -> 19.8 us  [body(): lax.all_to_all(jnp.broadcast_to(source_logs[None], (dom_count, src_rows,...]
    all_to_all x0 -> x2, starting transfers between devices: none -> 15.2 us  [the longest x1 11.3 us: body(): received = lax.all_to_all(pieces, 'blk', 0, 0, tiled=False)]
    ppermute x14, starting transfers between devices: 39.2 us -> 29.6 us  [permute_gather(): lax.ppermute(value, axis, [(i, (i + shift) % count) for i in range(count)])]
    ppermute x14, waiting for transfers between devices: 30.1 us -> 21.4 us  [permute_gather(): lax.ppermute(value, axis, [(i, (i + shift) % count) for i in range(count)])]
  transfers between devices with their start and end apart: 16 -> 16, of which waited for: 9 -> 5; matrix products, arithmetic and copies ran while one was open for 1% -> 1% of each run, Pallas kernels for 0% -> 0%
where the time goes in v2:
time: 358 us; the launch traced here: 356 us
  blocking collectives  150 us (42%)
  waiting for transfers between devices  77.1 us (22%)
  matrix products  62.3 us (17%)
  starting transfers between devices  44.8 us (13%)
  other arithmetic  11.5 us (3%)
  local copies, waits for them, and re-layouts  9.24 us (3%)
    all_to_all x2, blocking collectives, body(): received = lax.all_to_all(pieces, 'dom', 0, 0, tiled=False)  51.3 us
    all_to_all x1, blocking collectives, body(): received = lax.all_to_all(pieces, 'blk', 0, 0, tiled=False)  45 us
    all_to_all x1, waiting for transfers between devices, body(): received = lax.all_to_all(pieces, 'blk', 0, 0, tiled=False)  38.6 us
    all_gather x1, blocking collectives, body(): lax.all_gather(normalized(source_emb), 'dom', axis=0, tiled=True)  33.5 us
    ppermute x14, starting transfers between devices, permute_gather(): lax.ppermute(value, axis, [(i, (i + shift) % count) for i in range(count)])  29.6 us
    dot_general x2, matrix products, body(): jnp.einsum('sij,sjc->sic', kernel, weight_segments, preferred_element_typ...  25.9 us
    dot_general x2, matrix products, body(): jnp.einsum('ic,sij->sjc', source_weights, kernel, preferred_element_type=...  23.3 us
    ppermute x14, waiting for transfers between devices, permute_gather(): lax.ppermute(value, axis, [(i, (i + shift) % count) for i in range(count)])  21.4 us
  transfers between devices with their start and end apart: 16, of which 5 were waited for; matrix products, arithmetic and copies ran while one was open for 1% of the time, Pallas kernels for 0%

profile of v2, /device:TPU:1, one launch (start us, length us, event | category | flops | bytes accessed | tf_op | source)
XLA Modules:
  0.0 355.7 jit_solution(4869274487374984788)
XLA Ops:
  0.6 1.2 copy.19
  1.8 1.1 reduce_max.100
  2.9 0.9 fusion.20
  4.0 0.9 fusion.21
  5.1 2.1 collective-permute-start.6
  7.2 2.5 collective-permute-start.5
  9.7 2.2 collective-permute-start.4
  11.9 1.1 collective-permute-start.1
  13.0 1.5 collective-permute-start
  14.5 0.7 fusion.23
  15.2 0.7 fusion.24
  15.9 33.5 %all_gather.3 = bf16[2048,64]{0,1:T(8,128)(2,1)S(1)} all-gather(bf16[128,64]{0,1:T(8,128)(2,1)S(1)} %fusion.24), channel_id=1, replica_groups=mesh['blk'=8,'dom'=16] {'dom'}, dimensions={0}, use_global_device_ids=true | all-gather | bytes 278528 | tf_op jit(solution)/shard_map/all_gather | solution.py:85
  49.6 0.7 collective-permute-start.3
  50.4 9.8 %collective-permute-done.2 = bf16[784,192]{0,1:T(8,128)(2,1)S(1)} collective-permute-done((bf16[784,192]{0,1:T(8,128)(2,1)S(1)}, bf16[784,192]{0,1:T(8,128)(2,1)S(1)}, u32[]{:S(2)}, u32[]{:S(2)}) %collective-permute-start.2) | collective-permute-done | bytes 301088 | tf_op jit(solution)/shard_map/ppermute | solution.py:60
  61.1 2.3 copy-done.4
  63.5 0.3 exponential_reduce_fusion
  63.8 13.2 %exponential_convert_fusion = bf16[8,768,2048]{2,1,0:T(8,128)(2,1)} fusion(bf16[16,784,192]{1,2,0:T(8,128)(2,1)} %copy-done.4, s32[]{:T(128)S(6)} %select_n.20, bf16[2048,64]{0,1:T(8,128)(2,1)S(1)} %all_gather.3), kind=kOutput, calls=%fused_computation | convolution fusion | flops 1648361472 | bytes 26214404 | tf_op jit(solution)/shard_map/id,sjd->sij/dot_general | solution.py:118
  76.9 13.0 %multiply_reduce_fusion.1 = f32[2048,128]{1,0:T(8,128)S(1)} fusion(f32[8,128]{1,0:T(8,128)S(1)} %exponential_reduce_fusion, bf16[8,768,2048]{2,1,0:T(8,128)(2,1)} %exponential_convert_fusion, bf16[16,784,192]{1,2,0:T(8,128)(2,1)} %copy-done.4, s32[]{:T(128)S(6)} %select_n.20, s32[]{:T(128)S(6)} %add.54), kind=kOutput, calls=%fused_computation.6 | convolution fusion | flops 3225157632 | bytes 27791368 | tf_op jit(solution)/shard_map/sij,sjc->sic/dot_general | solution.py:122
  90.1 23.7 %all_to_all.30 = f32[16,136,128]{2,1,0:T(8,128)S(1)} all-to-all(f32[16,136,128]{2,1,0:T(8,128)S(1)} %maximum_maximum_fusion.2), channel_id=1, replica_groups=mesh['blk'=8,'dom'=16] {'dom'}, dimensions={0} | all-to-all | bytes 2228224 | tf_op jit(solution)/shard_map/all_to_all | solution.py:129
  114.0 1.2 broadcast_in_dim.13
  115.2 3.9 %all-to-all-start.1 = ((f32[16,128,128]{2,1,0:T(8,128)}), f32[16,128,128]{2,1,0:T(8,128)S(1)}, u32[]{:S(2)}, u32[]{:S(2)}) async-start(f32[16,128,128]{2,1,0:T(8,128)} %broadcast_in_dim.13), calls=%async_computation.1 | async-start | bytes 2097152 | tf_op jit(solution)/shard_map/all_to_all | solution.py:136
  119.1 17.1 %all-to-all-done.1 = f32[16,128,128]{2,1,0:T(8,128)S(1)} async-done(((f32[16,128,128]{2,1,0:T(8,128)}), f32[16,128,128]{2,1,0:T(8,128)S(1)}, u32[]{:S(2)}, u32[]{:S(2)}) %all-to-all-start.1) | async-done | bytes 1048608 | tf_op jit(solution)/shard_map/all_to_all | solution.py:136
  136.2 0.3 reduce_max.104
  136.7 11.6 %fusion.2 = f32[8,768,128]{2,1,0:T(8,128)S(1)} fusion(bf16[8,768,2048]{2,1,0:T(8,128)(2,1)} %exponential_convert_fusion, bf16[2048,128]{1,0:T(8,128)(2,1)S(1)} %fusion.13), kind=kOutput, calls=%fused_computation.3 | convolution fusion | flops 3221225472 | bytes 28835840 | tf_op jit(solution)/shard_map/ic,sij->sjc/dot_general | solution.py:141
  148.3 2.0 maximum_maximum_fusion
  150.4 11.3 %all-to-all-start.2 = ((f32[8,776,128]{2,1,0:T(8,128)}), f32[8,776,128]{2,1,0:T(8,128)S(1)}, u32[]{:S(2)}, u32[]{:S(2)}) async-start(f32[8,776,128]{2,1,0:T(8,128)} %maximum_maximum_fusion), calls=%async_computation.2 | async-start | bytes 6356992 | tf_op jit(solution)/shard_map/all_to_all | solution.py:148
  161.8 38.6 %all-to-all-done.2 = f32[8,776,128]{2,1,0:T(8,128)S(1)} async-done(((f32[8,776,128]{2,1,0:T(8,128)}), f32[8,776,128]{2,1,0:T(8,128)S(1)}, u32[]{:S(2)}, u32[]{:S(2)}) %all-to-all-start.2) | async-done | bytes 3178528 | tf_op jit(solution)/shard_map/all_to_all | solution.py:148
  200.7 0.7 copy-done
  201.9 8.2 %collective-permute-start.7 = (bf16[784,128]{1,0:T(8,128)(2,1)S(1)}, bf16[784,128]{1,0:T(8,128)(2,1)S(1)}, u32[]{:S(2)}, u32[]{:S(2)}) collective-permute-start(bf16[784,128]{1,0:T(8,128)(2,1)S(1)} %maximum_maximum_fusion.4), channel_id=1, source_target_pairs={{0,112},{16,0},{32,16},{48,32},{64,48},{80,64},{96,80},{112,96},{1... | collective-permute-start | bytes 602120 | tf_op jit(solution)/shard_map/ppermute | solution.py:60
  210.1 0.3 collective-permute-start.12
  210.4 2.3 collective-permute-start.11
  212.7 1.3 collective-permute-start.10
  214.0 3.3 collective-permute-start.8
  217.3 5.5 %collective-permute-done.8 = bf16[784,128]{1,0:T(8,128)(2,1)S(1)} collective-permute-done((bf16[784,128]{1,0:T(8,128)(2,1)S(1)}, bf16[784,128]{1,0:T(8,128)(2,1)S(1)}, u32[]{:S(2)}, u32[]{:S(2)}) %collective-permute-start.8) | collective-permute-done | bytes 200736 | tf_op jit(solution)/shard_map/ppermute | solution.py:60
  222.8 4.2 %collective-permute-start.9 = (bf16[784,128]{1,0:T(8,128)(2,1)S(1)}, bf16[784,128]{1,0:T(8,128)(2,1)S(1)}, u32[]{:S(2)}, u32[]{:S(2)}) collective-permute-start(bf16[784,128]{1,0:T(8,128)(2,1)S(1)} %maximum_maximum_fusion.4), channel_id=1, source_target_pairs={{0,80},{16,96},{32,112},{48,0},{64,16},{80,32},{96,48},{112,64},{1... | collective-permute-start | bytes 602120 | tf_op jit(solution)/shard_map/ppermute | solution.py:60
  227.0 6.0 %collective-permute-done.9 = bf16[784,128]{1,0:T(8,128)(2,1)S(1)} collective-permute-done((bf16[784,128]{1,0:T(8,128)(2,1)S(1)}, bf16[784,128]{1,0:T(8,128)(2,1)S(1)}, u32[]{:S(2)}, u32[]{:S(2)}) %collective-permute-start.9) | collective-permute-done | bytes 200736 | tf_op jit(solution)/shard_map/ppermute | solution.py:60
  233.2 0.2 bitcast_dynamic-update-slice_fusion.16
  233.7 0.2 bitcast_dynamic-update-slice_fusion.17
  234.0 1.7 copy-done.5
  235.7 12.9 %multiply_reduce_fusion = f32[2048,128]{1,0:T(8,128)S(1)} fusion(f32[8,128]{1,0:T(8,128)S(1)} %bitcast.102, bf16[8,768,2048]{2,1,0:T(8,128)(2,1)} %exponential_convert_fusion, bf16[16,784,128]{2,1,0:T(8,128)(2,1)} %copy-done.5, s32[]{:T(128)S(6)} %select_n.20), kind=kOutput, calls=%fused_computation.5 | convolution fusion | flops 3225157632 | bytes 27791364 | tf_op jit(solution)/shard_map/sij,sjc->sic/dot_general | solution.py:122
  248.8 27.6 %all_to_all.31 = f32[16,136,128]{2,1,0:T(8,128)S(1)} all-to-all(f32[16,136,128]{2,1,0:T(8,128)S(1)} %maximum_maximum_fusion.3), channel_id=1, replica_groups=mesh['blk'=8,'dom'=16] {'dom'}, dimensions={0} | all-to-all | bytes 2228224 | tf_op jit(solution)/shard_map/all_to_all | solution.py:129
  276.7 19.8 %all_to_all.32 = f32[16,128,128]{2,1,0:T(8,128)S(1)} all-to-all(f32[16,128,128]{2,1,0:T(8,128)S(1)} %broadcast_in_dim.16), channel_id=1, replica_groups=mesh['blk'=8,'dom'=16] {'dom'}, dimensions={0} | all-to-all | bytes 2097152 | tf_op jit(solution)/shard_map/all_to_all | solution.py:136
  296.5 0.3 reduce_max.110
  296.9 11.6 %fusion = f32[8,768,128]{2,1,0:T(8,128)S(1)} fusion(bf16[8,768,2048]{2,1,0:T(8,128)(2,1)} %exponential_convert_fusion, bf16[2048,128]{1,0:T(8,128)(2,1)S(1)} %fusion.11), kind=kOutput, calls=%fused_computation.1 | convolution fusion | flops 3221225472 | bytes 28835840 | tf_op jit(solution)/shard_map/ic,sij->sjc/dot_general | solution.py:141
  308.6 0.3 maximum_maximum_fusion.1
  308.8 45.0 %all_to_all.33 = f32[8,776,128]{2,1,0:T(8,128)S(1)} all-to-all(f32[8,776,128]{2,1,0:T(8,128)S(1)} %maximum_maximum_fusion.1), channel_id=1, replica_groups=mesh['blk'=8,'dom'=16] {'blk'}, dimensions={0} | all-to-all | bytes 6356992 | tf_op jit(solution)/shard_map/all_to_all | solution.py:148
  354.1 0.7 copy-done.1
  354.8 0.9 log_subtract_fusion
  (97 shorter events, 4.1 us)
Async XLA Ops:
  5.1 55.3 %collective-permute-start.6 = (bf16[784,192]{0,1:T(8,128)(2,1)S(1)}, bf16[784,192]{0,1:T(8,128)(2,1)S(1)}, u32[]{:S(2)}, u32[]{:S(2)}) collective-permute-start(bf16[784,192]{0,1:T(8,128)(2,1)S(1)} %fusion.18), channel_id=1, source_target_pairs={{0,16},{16,32},{32,48},{48,64},{64,80},{80,96},{96,112},{112,0},{1... | collective-permute-start | bytes 903176 | tf_op jit(solution)/shard_map/ppermute | solution.py:60
  7.2 53.1 %collective-permute-start.5 = (bf16[784,192]{0,1:T(8,128)(2,1)S(1)}, bf16[784,192]{0,1:T(8,128)(2,1)S(1)}, u32[]{:S(2)}, u32[]{:S(2)}) collective-permute-start(bf16[784,192]{0,1:T(8,128)(2,1)S(1)} %fusion.18), channel_id=1, source_target_pairs={{0,32},{16,48},{32,64},{48,80},{64,96},{80,112},{96,0},{112,16},{1... | collective-permute-start | bytes 903176 | tf_op jit(solution)/shard_map/ppermute | solution.py:60
  9.7 50.6 %collective-permute-start.4 = (bf16[784,192]{0,1:T(8,128)(2,1)S(1)}, bf16[784,192]{0,1:T(8,128)(2,1)S(1)}, u32[]{:S(2)}, u32[]{:S(2)}) collective-permute-start(bf16[784,192]{0,1:T(8,128)(2,1)S(1)} %fusion.18), channel_id=1, source_target_pairs={{0,48},{16,64},{32,80},{48,96},{64,112},{80,0},{96,16},{112,32},{1... | collective-permute-start | bytes 903176 | tf_op jit(solution)/shard_map/ppermute | solution.py:60
  11.9 37.7 %collective-permute-start.1 = (bf16[784,192]{0,1:T(8,128)(2,1)S(1)}, bf16[784,192]{0,1:T(8,128)(2,1)S(1)}, u32[]{:S(2)}, u32[]{:S(2)}) collective-permute-start(bf16[784,192]{0,1:T(8,128)(2,1)S(1)} %fusion.18), channel_id=1, source_target_pairs={{0,96},{16,112},{32,0},{48,16},{64,32},{80,48},{96,64},{112,80},{1... | collective-permute-start | bytes 903176 | tf_op jit(solution)/shard_map/ppermute | solution.py:60
  13.0 36.5 %collective-permute-start = (bf16[784,192]{0,1:T(8,128)(2,1)S(1)}, bf16[784,192]{0,1:T(8,128)(2,1)S(1)}, u32[]{:S(2)}, u32[]{:S(2)}) collective-permute-start(bf16[784,192]{0,1:T(8,128)(2,1)S(1)} %fusion.18), channel_id=1, source_target_pairs={{0,112},{16,0},{32,16},{48,32},{64,48},{80,64},{96,80},{112,96},{1... | collective-permute-start | bytes 903176 | tf_op jit(solution)/shard_map/ppermute | solution.py:60
  49.5 10.7 %collective-permute-start.2 = (bf16[784,192]{0,1:T(8,128)(2,1)S(1)}, bf16[784,192]{0,1:T(8,128)(2,1)S(1)}, u32[]{:S(2)}, u32[]{:S(2)}) collective-permute-start(bf16[784,192]{0,1:T(8,128)(2,1)S(1)} %fusion.18), channel_id=1, source_target_pairs={{0,80},{16,96},{32,112},{48,0},{64,16},{80,32},{96,48},{112,64},{1... | collective-permute-start | bytes 903176 | tf_op jit(solution)/shard_map/ppermute | solution.py:60
  49.6 10.6 %collective-permute-start.3 = (bf16[784,192]{0,1:T(8,128)(2,1)S(1)}, bf16[784,192]{0,1:T(8,128)(2,1)S(1)}, u32[]{:S(2)}, u32[]{:S(2)}) collective-permute-start(bf16[784,192]{0,1:T(8,128)(2,1)S(1)} %fusion.18), channel_id=1, source_target_pairs={{0,64},{16,80},{32,96},{48,112},{64,0},{80,16},{96,32},{112,48},{1... | collective-permute-start | bytes 903176 | tf_op jit(solution)/shard_map/ppermute | solution.py:60
  61.0 2.5 copy-start.4
  89.9 24.1 %copy-start.2 = (s32[128,128]{1,0:T(8,128)S(1)}, s32[128,128]{1,0:T(8,128)}, u32[]{:S(2)}) copy-start(s32[128,128]{1,0:T(8,128)} %param.7) | copy-start | bytes 196612
  115.2 21.1 %all-to-all-start.1 = ((f32[16,128,128]{2,1,0:T(8,128)}), f32[16,128,128]{2,1,0:T(8,128)S(1)}, u32[]{:S(2)}, u32[]{:S(2)}) async-start(f32[16,128,128]{2,1,0:T(8,128)} %broadcast_in_dim.13), calls=%async_computation.1 | async-start | bytes 2097152 | tf_op jit(solution)/shard_map/all_to_all | solution.py:136
  150.4 50.0 %all-to-all-start.2 = ((f32[8,776,128]{2,1,0:T(8,128)}), f32[8,776,128]{2,1,0:T(8,128)S(1)}, u32[]{:S(2)}, u32[]{:S(2)}) async-start(f32[8,776,128]{2,1,0:T(8,128)} %maximum_maximum_fusion), calls=%async_computation.2 | async-start | bytes 6356992 | tf_op jit(solution)/shard_map/all_to_all | solution.py:148
  200.4 1.0 copy-start
  201.9 12.1 %collective-permute-start.7 = (bf16[784,128]{1,0:T(8,128)(2,1)S(1)}, bf16[784,128]{1,0:T(8,128)(2,1)S(1)}, u32[]{:S(2)}, u32[]{:S(2)}) collective-permute-start(bf16[784,128]{1,0:T(8,128)(2,1)S(1)} %maximum_maximum_fusion.4), channel_id=1, source_target_pairs={{0,112},{16,0},{32,16},{48,32},{64,48},{80,64},{96,80},{112,96},{1... | collective-permute-start | bytes 602120 | tf_op jit(solution)/shard_map/ppermute | solution.py:60
  210.1 23.1 %collective-permute-start.13 = (bf16[784,128]{1,0:T(8,128)(2,1)S(1)}, bf16[784,128]{1,0:T(8,128)(2,1)S(1)}, u32[]{:S(2)}, u32[]{:S(2)}) collective-permute-start(bf16[784,128]{1,0:T(8,128)(2,1)S(1)} %maximum_maximum_fusion.4), channel_id=1, source_target_pairs={{0,16},{16,32},{32,48},{48,64},{64,80},{80,96},{96,112},{112,0},{1... | collective-permute-start | bytes 602120 | tf_op jit(solution)/shard_map/ppermute | solution.py:60
  210.1 23.0 %collective-permute-start.12 = (bf16[784,128]{1,0:T(8,128)(2,1)S(1)}, bf16[784,128]{1,0:T(8,128)(2,1)S(1)}, u32[]{:S(2)}, u32[]{:S(2)}) collective-permute-start(bf16[784,128]{1,0:T(8,128)(2,1)S(1)} %maximum_maximum_fusion.4), channel_id=1, source_target_pairs={{0,32},{16,48},{32,64},{48,80},{64,96},{80,112},{96,0},{112,16},{1... | collective-permute-start | bytes 602120 | tf_op jit(solution)/shard_map/ppermute | solution.py:60
  210.4 22.7 %collective-permute-start.11 = (bf16[784,128]{1,0:T(8,128)(2,1)S(1)}, bf16[784,128]{1,0:T(8,128)(2,1)S(1)}, u32[]{:S(2)}, u32[]{:S(2)}) collective-permute-start(bf16[784,128]{1,0:T(8,128)(2,1)S(1)} %maximum_maximum_fusion.4), channel_id=1, source_target_pairs={{0,48},{16,64},{32,80},{48,96},{64,112},{80,0},{96,16},{112,32},{1... | collective-permute-start | bytes 602120 | tf_op jit(solution)/shard_map/ppermute | solution.py:60
  212.7 20.3 %collective-permute-start.10 = (bf16[784,128]{1,0:T(8,128)(2,1)S(1)}, bf16[784,128]{1,0:T(8,128)(2,1)S(1)}, u32[]{:S(2)}, u32[]{:S(2)}) collective-permute-start(bf16[784,128]{1,0:T(8,128)(2,1)S(1)} %maximum_maximum_fusion.4), channel_id=1, source_target_pairs={{0,64},{16,80},{32,96},{48,112},{64,0},{80,16},{96,32},{112,48},{1... | collective-permute-start | bytes 602120 | tf_op jit(solution)/shard_map/ppermute | solution.py:60
  214.0 8.8 %collective-permute-start.8 = (bf16[784,128]{1,0:T(8,128)(2,1)S(1)}, bf16[784,128]{1,0:T(8,128)(2,1)S(1)}, u32[]{:S(2)}, u32[]{:S(2)}) collective-permute-start(bf16[784,128]{1,0:T(8,128)(2,1)S(1)} %maximum_maximum_fusion.4), channel_id=1, source_target_pairs={{0,96},{16,112},{32,0},{48,16},{64,32},{80,48},{96,64},{112,80},{1... | collective-permute-start | bytes 602120 | tf_op jit(solution)/shard_map/ppermute | solution.py:60
  222.8 10.2 %collective-permute-start.9 = (bf16[784,128]{1,0:T(8,128)(2,1)S(1)}, bf16[784,128]{1,0:T(8,128)(2,1)S(1)}, u32[]{:S(2)}, u32[]{:S(2)}) collective-permute-start(bf16[784,128]{1,0:T(8,128)(2,1)S(1)} %maximum_maximum_fusion.4), channel_id=1, source_target_pairs={{0,80},{16,96},{32,112},{48,0},{64,16},{80,32},{96,48},{112,64},{1... | collective-permute-start | bytes 602120 | tf_op jit(solution)/shard_map/ppermute | solution.py:60
  233.9 1.8 copy-start.5
  276.6 31.9 %copy-start.3 = (f32[128,128]{1,0:T(8,128)}, f32[128,128]{1,0:T(8,128)S(1)}, u32[]{:S(2)}) copy-start(f32[128,128]{1,0:T(8,128)S(1)} %log_subtract_fusion.2) | copy-start | bytes 196612
  353.8 1.0 copy-start.1

commit v3 on v1

--- a/solution.py
+++ b/solution.py
@@ -91,60 +91,73 @@
     src_piece_rows = padded_rows(src_rows + 1, 8)
     tgt_piece_rows = padded_rows(tgt_rows + 1, 8)
 
-    target_logs = warm_start
+    halves = 2
+    half = columns // halves
+    target_logs = [warm_start[:, h * half:(h + 1) * half] for h in range(halves)]
+    log_targets = [log_target[:, h * half:(h + 1) * half] for h in range(halves)]
+    log_sources = [log_source[:, h * half:(h + 1) * half] for h in range(halves)]
+    source_logs = [None] * halves
     target_group = None
-    source_logs = None
+    kernel = None
     for iteration in range(ITERS):
-        shift = shift_of(target_logs)
-        weights = jnp.exp(target_logs - shift).astype(jnp.bfloat16)
-        payload = jnp.concatenate(
-            [weights, shift.astype(jnp.bfloat16)[None, :],
-             jnp.zeros((tgt_payload_rows - tgt_rows - 1, columns), jnp.bfloat16)], axis=0)
-        if target_group is None:
-            emb_rows = jnp.concatenate(
-                [own_targets, jnp.zeros((tgt_payload_rows - tgt_rows, width), jnp.bfloat16)], axis=0)
-            payload = jnp.concatenate([emb_rows, payload], axis=1)
-            gathered = permute_gather(payload, "blk", blk_count)
-            target_group = gathered[:, :tgt_rows, :width].reshape(group_rows, width)
-            gathered = gathered[:, :, width:]
-        else:
-            gathered = permute_gather(payload, "blk", blk_count)
-        weight_segments = gathered[:, :tgt_rows, :]
-        segment_shift = gathered[:, tgt_rows, :].astype(jnp.float32)
-        group_shift = jnp.max(segment_shift, axis=0)
-        factors = jnp.exp(segment_shift - group_shift[None, :])
-        partial_value = segment_sums(
-            source_block,
-            target_group.reshape(blk_count, tgt_rows, width),
-            weight_segments,
-            factors,
-            min(block_rows, 1024),
-        )
-        pieces = jnp.concatenate(
-            [partial_value.reshape(dom_count, src_rows, columns),
-             jnp.broadcast_to(group_shift[None, None, :], (dom_count, 1, columns)),
-             jnp.zeros((dom_count, src_piece_rows - src_rows - 1, columns), jnp.float32)], axis=1)
-        received = lax.all_to_all(pieces, "dom", 0, 0, tiled=False)
-        group_shifts = received[:, src_rows, :]
-        target_peak = jnp.max(group_shifts, axis=0)
-        scale = jnp.exp(group_shifts - target_peak[None, :])
-        shares = jnp.sum(received[:, :src_rows, :] * scale[:, None, :], axis=0)
-        source_logs = log_source - target_peak - jnp.log(shares)
+        for h in range(halves):
+            shift = shift_of(target_logs[h])
+            weights = jnp.exp(target_logs[h] - shift).astype(jnp.bfloat16)
+            payload = jnp.concatenate(
+                [weights, shift.astype(jnp.bfloat16)[None, :],
+                 jnp.zeros((tgt_payload_rows - tgt_rows - 1, half), jnp.bfloat16)], axis=0)
+            if target_group is None:
+                emb_rows = jnp.concatenate(
+                    [own_targets, jnp.zeros((tgt_payload_rows - tgt_rows, width), jnp.bfloat16)], axis=0)
+                payload = jnp.concatenate([emb_rows, payload], axis=1)
+                gathered = permute_gather(payload, "blk", blk_count)
+                target_group = gathered[:, :tgt_rows, :width].reshape(group_rows, width)
+                gathered = gathered[:, :, width:]
+            else:
+                gathered = permute_gather(payload, "blk", blk_count)
+            weight_segments = gathered[:, :tgt_rows, :]
+            segment_shift = gathered[:, tgt_rows, :].astype(jnp.float32)
+            group_shift = jnp.max(segment_shift, axis=0)
+            factors = jnp.exp(segment_shift - group_shift[None, :])
+            if kernel is None:
+                products = jnp.einsum(
+                    "id,sjd->sij", source_block, target_group.reshape(blk_count, tgt_rows, width),
+                    preferred_element_type=jnp.float32)
+                kernel = jnp.exp((products - 1.0) / entropic).astype(jnp.bfloat16)
+            per_segment = jnp.einsum(
+                "sij,sjc->sic", kernel, weight_segments, preferred_element_type=jnp.float32)
+            partial_value = jnp.sum(per_segment * factors[:, None, :], axis=0)
+            pieces = jnp.concatenate(
+                [partial_value.reshape(dom_count, src_rows, half),
+                 jnp.broadcast_to(group_shift[None, None, :], (dom_count, 1, half)),
+                 jnp.zeros((dom_count, src_piece_rows - src_rows - 1, half), jnp.float32)], axis=1)
+            received = lax.all_to_all(pieces, "dom", 0, 0, tiled=False)
+            group_shifts = received[:, src_rows, :]
+            target_peak = jnp.max(group_shifts, axis=0)
+            scale = jnp.exp(group_shifts - target_peak[None, :])
+            shares = jnp.sum(received[:, :src_rows, :] * scale[:, None, :], axis=0)
+            source_logs[h] = log_sources[h] - target_peak - jnp.log(shares)
 
-        block_logs = lax.all_gather(source_logs, "dom", axis=0, tiled=True)
-        block_peak = jnp.max(block_logs, axis=0)
-        source_weights = jnp.exp(block_logs - block_peak).astype(jnp.bfloat16)
-        target_partial = plain_sums(target_group, source_block, source_weights, 1024, block_rows)
-        pieces = jnp.concatenate(
-            [target_partial.reshape(blk_count, tgt_rows, columns),
-             jnp.broadcast_to(block_peak[None, None, :], (blk_count, 1, columns)),
-             jnp.zeros((blk_count, tgt_piece_rows - tgt_rows - 1, columns), jnp.float32)], axis=1)
-        received = lax.all_to_all(pieces, "blk", 0, 0, tiled=False)
-        block_peaks = received[:, tgt_rows, :]
-        source_peak = jnp.max(block_peaks, axis=0)
-        scale = jnp.exp(block_peaks - source_peak[None, :])
-        target_sums = jnp.sum(received[:, :tgt_rows, :] * scale[:, None, :], axis=0)
-        target_logs = log_target - source_peak - jnp.log(target_sums)
+            block_logs = lax.all_to_all(
+                jnp.broadcast_to(source_logs[h][None], (dom_count, src_rows, half)), "dom", 0, 0, tiled=False
+            ).reshape(block_rows, half)
+            block_peak = jnp.max(block_logs, axis=0)
+            source_weights = jnp.exp(block_logs - block_peak).astype(jnp.bfloat16)
+            target_partial = jnp.einsum(
+                "ic,sij->sjc", source_weights, kernel, preferred_element_type=jnp.float32
+            ).reshape(group_rows, half)
+            pieces = jnp.concatenate(
+                [target_partial.reshape(blk_count, tgt_rows, half),
+                 jnp.broadcast_to(block_peak[None, None, :], (blk_count, 1, half)),
+                 jnp.zeros((blk_count, tgt_piece_rows - tgt_rows - 1, half), jnp.float32)], axis=1)
+            received = lax.all_to_all(pieces, "blk", 0, 0, tiled=False)
+            block_peaks = received[:, tgt_rows, :]
+            source_peak = jnp.max(block_peaks, axis=0)
+            scale = jnp.exp(block_peaks - source_peak[None, :])
+            target_sums = jnp.sum(received[:, :tgt_rows, :] * scale[:, None, :], axis=0)
+            target_logs[h] = log_targets[h] - source_peak - jnp.log(target_sums)
+    source_logs = jnp.concatenate(source_logs, axis=1)
+    target_logs = jnp.concatenate(target_logs, axis=1)
     return (source_logs, target_logs)
 
 

time: 485 us -> 526 us (1.085)
  starting transfers between devices: 39.2 us -> 76.5 us
  waiting for transfers between devices: 111 us -> 128 us
  between operations: 14.5 us -> 1.87 us
  matrix products: 123 us -> 114 us
    all_to_all x0 -> x7, waiting for transfers between devices: none -> 84.5 us  [the longest x2 39.8 us: body(): received = lax.all_to_all(pieces, 'blk', 0, 0, tiled=False)]
    all_gather x2 -> x0, waiting for transfers between devices: 81 us -> none  [body(): block_logs = lax.all_gather(source_logs, 'dom', axis=0, tiled=True)]
    all_to_all x0 -> x7, starting transfers between devices: none -> 30.7 us  [the longest x3 14.1 us: body(): lax.all_to_all(jnp.broadcast_to(source_logs[h][None], (dom_count, src_row...]
    all_to_all x2, blocking collectives: 84.8 us -> 54.8 us  [body(): received = lax.all_to_all(pieces, 'blk', 0, 0, tiled=False)]
    all_to_all x2, blocking collectives: 48.8 us -> 65.8 us  [body(): received = lax.all_to_all(pieces, 'dom', 0, 0, tiled=False)]
    all_to_all x0 -> x1, blocking collectives: none -> 14.7 us  [body(): lax.all_to_all(jnp.broadcast_to(source_logs[h][None], (dom_count, src_row...]
    ppermute x14 -> x28, waiting for transfers between devices: 30.1 us -> 43.6 us  [permute_gather(): lax.ppermute(value, axis, [(i, (i + shift) % count) for i in range(count)])]
    dot_general x44 -> x9, matrix products: 123 us -> 114 us  [the longest x4 51.4 us: body(): jnp.einsum('sij,sjc->sic', kernel, weight_segments, preferred_element_typ...]
  transfers between devices with their start and end apart: 16 -> 35, of which waited for: 9 -> 18; matrix products, arithmetic and copies ran while one was open for 1% -> 7% of each run, Pallas kernels for 0% -> 0%
where the time goes in v3:
time: 526 us; the launch traced here: 519 us
  blocking collectives  163 us (31%)
  waiting for transfers between devices  128 us (24%)
  matrix products  114 us (22%)
  starting transfers between devices  76.5 us (15%)
  other arithmetic  23.9 us (5%)
  local copies, waits for them, and re-layouts  11 us (2%)
    all_to_all x2, blocking collectives, body(): received = lax.all_to_all(pieces, 'dom', 0, 0, tiled=False)  65.8 us
    all_to_all x2, blocking collectives, body(): received = lax.all_to_all(pieces, 'blk', 0, 0, tiled=False)  54.8 us
    dot_general x4, matrix products, body(): jnp.einsum('sij,sjc->sic', kernel, weight_segments, preferred_element_typ...  51.4 us
    dot_general x4, matrix products, body(): jnp.einsum('ic,sij->sjc', source_weights, kernel, preferred_element_type=...  49.8 us
    ppermute x28, starting transfers between devices, permute_gather(): lax.ppermute(value, axis, [(i, (i + shift) % count) for i in range(count)])  45.8 us
    ppermute x28, waiting for transfers between devices, permute_gather(): lax.ppermute(value, axis, [(i, (i + shift) % count) for i in range(count)])  43.6 us
    all_to_all x2, waiting for transfers between devices, body(): received = lax.all_to_all(pieces, 'blk', 0, 0, tiled=False)  39.8 us
    all_to_all x2, waiting for transfers between devices, body(): received = lax.all_to_all(pieces, 'dom', 0, 0, tiled=False)  33.5 us
  transfers between devices with their start and end apart: 35, of which 18 were waited for; matrix products, arithmetic and copies ran while one was open for 7% of the time, Pallas kernels for 0%

profile of v3, /device:TPU:1, one launch (start us, length us, event | category | flops | bytes accessed | tf_op | source)
XLA Modules:
  0.0 518.9 jit_solution(1978807933837232504)
XLA Ops:
  5.6 4.3 collective-permute-start
  12.7 2.1 collective-permute-start.14
  14.9 27.9 %all_gather.3 = bf16[2048,64]{0,1:T(8,128)(2,1)S(1)} all-gather(bf16[128,64]{0,1:T(8,128)(2,1)S(1)} %fusion.50), channel_id=1, replica_groups=mesh['blk'=8,'dom'=16] {'dom'}, dimensions={0}, use_global_device_ids=true | all-gather | bytes 278528 | tf_op jit(solution)/shard_map/all_gather | solution.py:85
  42.8 3.8 collective-permute-start.15
  46.6 3.3 collective-permute-done.15
  49.8 7.2 %collective-permute-start.16 = (bf16[784,64]{0,1:T(8,128)(2,1)S(1)}, bf16[784,64]{0,1:T(8,128)(2,1)S(1)}, u32[]{:S(2)}, u32[]{:S(2)}) collective-permute-start(bf16[784,64]{0,1:T(8,128)(2,1)S(1)} %pad_maximum_fusion.2), channel_id=1, source_target_pairs={{0,80},{16,96},{32,112},{48,0},{64,16},{80,32},{96,48},{112,64},{1... | collective-permute-start | bytes 301064 | tf_op jit(solution)/shard_map/ppermute | solution.py:60
  57.1 5.2 %collective-permute-done.16 = bf16[784,64]{0,1:T(8,128)(2,1)S(1)} collective-permute-done((bf16[784,64]{0,1:T(8,128)(2,1)S(1)}, bf16[784,64]{0,1:T(8,128)(2,1)S(1)}, u32[]{:S(2)}, u32[]{:S(2)}) %collective-permute-start.16) | collective-permute-done | bytes 100384 | tf_op jit(solution)/shard_map/ppermute | solution.py:60
  62.9 3.1 collective-permute-done.17
  65.9 2.4 collective-permute-start.18
  68.3 2.2 collective-permute-done.18
  71.6 4.9 collective-permute-done.19
  76.5 6.3 %collective-permute-done.20 = bf16[784,64]{0,1:T(8,128)(2,1)S(1)} collective-permute-done((bf16[784,64]{0,1:T(8,128)(2,1)S(1)}, bf16[784,64]{0,1:T(8,128)(2,1)S(1)}, u32[]{:S(2)}, u32[]{:S(2)}) %collective-permute-start.20) | collective-permute-done | bytes 100384 | tf_op jit(solution)/shard_map/ppermute | solution.py:60
  85.7 3.7 collective-permute-done.4
  89.4 2.5 collective-permute-done.5
  92.0 2.7 collective-permute-done.6
  97.2 13.2 %exponential_convert_fusion = bf16[8,768,2048]{2,1,0:T(8,128)(2,1)} fusion(bf16[16,784,128]{1,2,0:T(8,128)(2,1)} %copy-done, s32[]{:T(128)S(6)} %select_n.21, bf16[2048,64]{0,1:T(8,128)(2,1)S(1)} %all_gather.3), kind=kOutput, calls=%fused_computation | convolution fusion | flops 1648361472 | bytes 26214404 | tf_op jit(solution)/shard_map/id,sjd->sij/dot_general | solution.py:123
  110.4 12.9 %multiply_reduce_fusion.3 = f32[2048,64]{0,1:T(8,128)S(1)} fusion(bf16[8,768,2048]{2,1,0:T(8,128)(2,1)} %exponential_convert_fusion, f32[8,64]{1,0:T(8,128)S(1)} %exponential_reduce_fusion.7, bf16[16,784,128]{1,2,0:T(8,128)(2,1)} %copy-done, s32[]{:T(128)S(6)} %select_n.21, s32[]{:T(128)S(6)} %add.76), kind=kOutput, calls=%fused_computation.12 | convolution fusion | flops 1612578816 | bytes 26478600 | tf_op jit(solution)/shard_map/sij,sjc->sic/dot_general | solution.py:127
  123.4 12.8 %multiply_reduce_fusion.1 = f32[2048,64]{0,1:T(8,128)S(1)} fusion(bf16[8,768,2048]{2,1,0:T(8,128)(2,1)} %exponential_convert_fusion, f32[8,64]{1,0:T(8,128)S(1)} %exponential_reduce_fusion.4, bf16[8,784,64]{1,2,0:T(8,128)(2,1)S(1)} %fusion.13), kind=kOutput, calls=%fused_computation.10 | convolution fusion | flops 1612578816 | bytes 26480640 | tf_op jit(solution)/shard_map/sij,sjc->sic/dot_general | solution.py:127
  137.9 31.2 %all_to_all.60 = f32[16,136,64]{1,2,0:T(8,128)S(1)} all-to-all(f32[16,136,64]{1,2,0:T(8,128)S(1)} %get-tuple-element.46), channel_id=1, replica_groups=mesh['blk'=8,'dom'=16] {'dom'}, dimensions={0} | all-to-all | bytes 1114112 | tf_op jit(solution)/shard_map/all_to_all | solution.py:134
  169.1 4.7 all-to-all-start.4
  174.3 16.7 %all-to-all-done.4 = f32[16,136,64]{1,2,0:T(8,128)S(1)} async-done(((f32[16,136,64]{1,2,0:T(8,128)}), f32[16,136,64]{1,2,0:T(8,128)S(1)}, u32[]{:S(2)}, u32[]{:S(2)}) %all-to-all-start.4) | async-done | bytes 557088 | tf_op jit(solution)/shard_map/all_to_all | solution.py:134
  192.8 4.4 all-to-all-start.1
  197.2 11.2 %all-to-all-done.1 = f32[16,128,64]{1,2,0:T(8,128)S(1)} async-done(((f32[16,128,64]{1,2,0:T(8,128)}), f32[16,128,64]{1,2,0:T(8,128)S(1)}, u32[]{:S(2)}, u32[]{:S(2)}) %all-to-all-start.1) | async-done | bytes 524320 | tf_op jit(solution)/shard_map/all_to_all | solution.py:141
  209.3 4.8 all-to-all-start.5
  214.2 12.4 %fusion.6 = f32[8,768,64]{1,2,0:T(8,128)S(1)} fusion(bf16[8,768,2048]{2,1,0:T(8,128)(2,1)} %exponential_convert_fusion, f32[64]{0:T(128)S(1)} %reduce_max.204, f32[16,128,64]{1,2,0:T(8,128)S(1)} %all-to-all-done.1), kind=kOutput, calls=%fused_computation.7 | convolution fusion | flops 1610874880 | bytes 27263232 | tf_op jit(solution)/shard_map/ic,sij->sjc/dot_general | solution.py:146
  226.8 12.4 %fusion.4 = f32[8,768,64]{1,2,0:T(8,128)S(1)} fusion(bf16[8,768,2048]{2,1,0:T(8,128)(2,1)} %exponential_convert_fusion, f32[64]{0:T(128)S(1)} %reduce_max.214, f32[16,128,64]{1,2,0:T(8,128)S(1)} %all-to-all-done.5), kind=kOutput, calls=%fused_computation.5 | convolution fusion | flops 1610874880 | bytes 27263232 | tf_op jit(solution)/shard_map/ic,sij->sjc/dot_general | solution.py:146
  241.1 27.5 %all_to_all.61 = f32[8,776,64]{1,2,0:T(8,128)} all-to-all(f32[8,776,64]{1,2,0:T(8,128)S(1)} %get-tuple-element.41), channel_id=1, replica_groups=mesh['blk'=8,'dom'=16] {'blk'}, dimensions={0} | all-to-all | bytes 3178496 | tf_op jit(solution)/shard_map/all_to_all | solution.py:153
  268.6 3.6 all-to-all-start.2
  276.3 20.1 %all-to-all-done.2 = f32[8,776,64]{1,2,0:T(8,128)S(1)} async-done(((f32[8,776,64]{1,2,0:T(8,128)}), f32[8,776,64]{1,2,0:T(8,128)S(1)}, u32[]{:S(2)}, u32[]{:S(2)}) %all-to-all-start.2) | async-done | bytes 1589280 | tf_op jit(solution)/shard_map/all_to_all | solution.py:153
  297.7 2.3 collective-permute-start.21
  303.0 3.9 collective-permute-start.7
  307.0 2.3 collective-permute-done.7
  310.0 3.6 collective-permute-start.27
  315.9 2.6 collective-permute-start.11
  320.7 4.6 collective-permute-done.12
  325.4 2.6 collective-permute-done.13
  329.2 12.8 %multiply_reduce_fusion = f32[2048,64]{0,1:T(8,128)S(1)} fusion(bf16[8,768,2048]{2,1,0:T(8,128)(2,1)} %exponential_convert_fusion, f32[8,64]{1,0:T(8,128)S(1)} %exponential_reduce_fusion.2, bf16[8,784,64]{1,2,0:T(8,128)(2,1)S(1)} %get-tuple-element.47), kind=kOutput, calls=%fused_computation.9 | convolution fusion | flops 1612578816 | bytes 26480640 | tf_op jit(solution)/shard_map/sij,sjc->sic/dot_general | solution.py:127
  342.4 12.8 %multiply_reduce_fusion.2 = f32[2048,64]{0,1:T(8,128)S(1)} fusion(bf16[8,768,2048]{2,1,0:T(8,128)(2,1)} %exponential_convert_fusion, f32[8,64]{1,0:T(8,128)S(1)} %exponential_reduce_fusion.5, bf16[8,784,64]{1,2,0:T(8,128)(2,1)S(1)} %get-tuple-element.48), kind=kOutput, calls=%fused_computation.11 | convolution fusion | flops 1612578816 | bytes 26480640 | tf_op jit(solution)/shard_map/sij,sjc->sic/dot_general | solution.py:127
  356.8 34.6 %all_to_all.62 = f32[16,136,64]{1,2,0:T(8,128)S(1)} all-to-all(f32[16,136,64]{1,2,0:T(8,128)S(1)} %get-tuple-element.44), channel_id=1, replica_groups=mesh['blk'=8,'dom'=16] {'dom'}, dimensions={0} | all-to-all | bytes 1114112 | tf_op jit(solution)/shard_map/all_to_all | solution.py:134
  391.4 4.7 all-to-all-start.3
  396.5 16.8 %all-to-all-done.3 = f32[16,136,64]{1,2,0:T(8,128)S(1)} async-done(((f32[16,136,64]{1,2,0:T(8,128)}), f32[16,136,64]{1,2,0:T(8,128)S(1)}, u32[]{:S(2)}, u32[]{:S(2)}) %all-to-all-start.3) | async-done | bytes 557088 | tf_op jit(solution)/shard_map/all_to_all | solution.py:134
  414.3 14.7 %all_to_all.63 = f32[16,128,64]{1,2,0:T(8,128)S(1)} all-to-all(f32[16,128,64]{1,2,0:T(8,128)S(1)} %broadcast_in_dim.34), channel_id=1, replica_groups=mesh['blk'=8,'dom'=16] {'dom'}, dimensions={0} | all-to-all | bytes 1048576 | tf_op jit(solution)/shard_map/all_to_all | solution.py:141
  429.9 5.0 all-to-all-start.8
  435.0 12.4 %fusion = f32[8,768,64]{1,2,0:T(8,128)S(1)} fusion(bf16[8,768,2048]{2,1,0:T(8,128)(2,1)} %exponential_convert_fusion, f32[64]{0:T(128)S(1)} %reduce_max.222, f32[16,128,64]{1,2,0:T(8,128)S(1)} %all_to_all.63), kind=kOutput, calls=%fused_computation.1 | convolution fusion | flops 1610874880 | bytes 27263232 | tf_op jit(solution)/shard_map/ic,sij->sjc/dot_general | solution.py:146
  447.6 12.4 %fusion.2 = f32[8,768,64]{1,2,0:T(8,128)S(1)} fusion(bf16[8,768,2048]{2,1,0:T(8,128)(2,1)} %exponential_convert_fusion, f32[64]{0:T(128)S(1)} %reduce_max.220, f32[16,128,64]{1,2,0:T(8,128)S(1)} %all-to-all-done.8), kind=kOutput, calls=%fused_computation.3 | convolution fusion | flops 1610874880 | bytes 27263232 | tf_op jit(solution)/shard_map/ic,sij->sjc/dot_general | solution.py:146
  461.8 27.3 %all_to_all.64 = f32[8,776,64]{1,2,0:T(8,128)} all-to-all(f32[8,776,64]{1,2,0:T(8,128)S(1)} %get-tuple-element.40), channel_id=1, replica_groups=mesh['blk'=8,'dom'=16] {'blk'}, dimensions={0} | all-to-all | bytes 3178496 | tf_op jit(solution)/shard_map/all_to_all | solution.py:153
  489.1 3.6 all-to-all-start.9
  497.3 19.6 %all-to-all-done.9 = f32[8,776,64]{1,2,0:T(8,128)S(1)} async-done(((f32[8,776,64]{1,2,0:T(8,128)}), f32[8,776,64]{1,2,0:T(8,128)S(1)}, u32[]{:S(2)}, u32[]{:S(2)}) %all-to-all-start.9) | async-done | bytes 1589280 | tf_op jit(solution)/shard_map/all_to_all | solution.py:153
  (190 shorter events, 48.8 us)
Async XLA Ops:
  0.6 14.1 %copy-start.3 = (bf16[128,64]{0,1:T(8,128)(2,1)S(1)}, bf16[128,64]{0,1:T(8,128)(2,1)}, u32[]{:S(2)}) copy-start(bf16[128,64]{0,1:T(8,128)(2,1)} %param.7) | copy-start | bytes 49156
  5.6 78.1 %collective-permute-start = (bf16[784,128]{0,1:T(8,128)(2,1)S(1)}, bf16[784,128]{0,1:T(8,128)(2,1)S(1)}, u32[]{:S(2)}, u32[]{:S(2)}) collective-permute-start(bf16[784,128]{0,1:T(8,128)(2,1)S(1)} %fusion.46), channel_id=1, source_target_pairs={{0,112},{16,0},{32,16},{48,32},{64,48},{80,64},{96,80},{112,96},{1... | collective-permute-start | bytes 602120 | tf_op jit(solution)/shard_map/ppermute | solution.py:60
  9.9 74.4 %collective-permute-start.1 = (bf16[784,128]{0,1:T(8,128)(2,1)S(1)}, bf16[784,128]{0,1:T(8,128)(2,1)S(1)}, u32[]{:S(2)}, u32[]{:S(2)}) collective-permute-start(bf16[784,128]{0,1:T(8,128)(2,1)S(1)} %fusion.46), channel_id=1, source_target_pairs={{0,96},{16,112},{32,0},{48,16},{64,32},{80,48},{96,64},{112,80},{1... | collective-permute-start | bytes 602120 | tf_op jit(solution)/shard_map/ppermute | solution.py:60
  10.4 75.2 %collective-permute-start.2 = (bf16[784,128]{0,1:T(8,128)(2,1)S(1)}, bf16[784,128]{0,1:T(8,128)(2,1)S(1)}, u32[]{:S(2)}, u32[]{:S(2)}) collective-permute-start(bf16[784,128]{0,1:T(8,128)(2,1)S(1)} %fusion.46), channel_id=1, source_target_pairs={{0,80},{16,96},{32,112},{48,0},{64,16},{80,32},{96,48},{112,64},{1... | collective-permute-start | bytes 602120 | tf_op jit(solution)/shard_map/ppermute | solution.py:60
  10.9 74.7 %collective-permute-start.3 = (bf16[784,128]{0,1:T(8,128)(2,1)S(1)}, bf16[784,128]{0,1:T(8,128)(2,1)S(1)}, u32[]{:S(2)}, u32[]{:S(2)}) collective-permute-start(bf16[784,128]{0,1:T(8,128)(2,1)S(1)} %fusion.46), channel_id=1, source_target_pairs={{0,64},{16,80},{32,96},{48,112},{64,0},{80,16},{96,32},{112,48},{1... | collective-permute-start | bytes 602120 | tf_op jit(solution)/shard_map/ppermute | solution.py:60
  12.7 30.1 %collective-permute-start.14 = (bf16[784,64]{0,1:T(8,128)(2,1)S(1)}, bf16[784,64]{0,1:T(8,128)(2,1)S(1)}, u32[]{:S(2)}, u32[]{:S(2)}) collective-permute-start(bf16[784,64]{0,1:T(8,128)(2,1)S(1)} %pad_maximum_fusion.2), channel_id=1, source_target_pairs={{0,112},{16,0},{32,16},{48,32},{64,48},{80,64},{96,80},{112,96},{1... | collective-permute-start | bytes 301064 | tf_op jit(solution)/shard_map/ppermute | solution.py:60
  42.8 7.0 %collective-permute-start.15 = (bf16[784,64]{0,1:T(8,128)(2,1)S(1)}, bf16[784,64]{0,1:T(8,128)(2,1)S(1)}, u32[]{:S(2)}, u32[]{:S(2)}) collective-permute-start(bf16[784,64]{0,1:T(8,128)(2,1)S(1)} %pad_maximum_fusion.2), channel_id=1, source_target_pairs={{0,96},{16,112},{32,0},{48,16},{64,32},{80,48},{96,64},{112,80},{1... | collective-permute-start | bytes 301064 | tf_op jit(solution)/shard_map/ppermute | solution.py:60
  49.8 12.5 %collective-permute-start.16 = (bf16[784,64]{0,1:T(8,128)(2,1)S(1)}, bf16[784,64]{0,1:T(8,128)(2,1)S(1)}, u32[]{:S(2)}, u32[]{:S(2)}) collective-permute-start(bf16[784,64]{0,1:T(8,128)(2,1)S(1)} %pad_maximum_fusion.2), channel_id=1, source_target_pairs={{0,80},{16,96},{32,112},{48,0},{64,16},{80,32},{96,48},{112,64},{1... | collective-permute-start | bytes 301064 | tf_op jit(solution)/shard_map/ppermute | solution.py:60
  62.3 3.6 collective-permute-start.17
  65.9 4.5 collective-permute-start.18
  70.5 6.0 %collective-permute-start.19 = (bf16[784,64]{0,1:T(8,128)(2,1)S(1)}, bf16[784,64]{0,1:T(8,128)(2,1)S(1)}, u32[]{:S(2)}, u32[]{:S(2)}) collective-permute-start(bf16[784,64]{0,1:T(8,128)(2,1)S(1)} %pad_maximum_fusion.2), channel_id=1, source_target_pairs={{0,32},{16,48},{32,64},{48,80},{64,96},{80,112},{96,0},{112,16},{1... | collective-permute-start | bytes 301064 | tf_op jit(solution)/shard_map/ppermute | solution.py:60
  76.5 6.3 %collective-permute-start.20 = (bf16[784,64]{0,1:T(8,128)(2,1)S(1)}, bf16[784,64]{0,1:T(8,128)(2,1)S(1)}, u32[]{:S(2)}, u32[]{:S(2)}) collective-permute-start(bf16[784,64]{0,1:T(8,128)(2,1)S(1)} %pad_maximum_fusion.2), channel_id=1, source_target_pairs={{0,16},{16,32},{32,48},{48,64},{64,80},{80,96},{96,112},{112,0},{1... | collective-permute-start | bytes 301064 | tf_op jit(solution)/shard_map/ppermute | solution.py:60
  82.8 6.6 %collective-permute-start.4 = (bf16[784,128]{0,1:T(8,128)(2,1)S(1)}, bf16[784,128]{0,1:T(8,128)(2,1)S(1)}, u32[]{:S(2)}, u32[]{:S(2)}) collective-permute-start(bf16[784,128]{0,1:T(8,128)(2,1)S(1)} %fusion.46), channel_id=1, source_target_pairs={{0,48},{16,64},{32,80},{48,96},{64,112},{80,0},{96,16},{112,32},{1... | collective-permute-start | bytes 602120 | tf_op jit(solution)/shard_map/ppermute | solution.py:60
  83.7 8.3 %collective-permute-start.5 = (bf16[784,128]{0,1:T(8,128)(2,1)S(1)}, bf16[784,128]{0,1:T(8,128)(2,1)S(1)}, u32[]{:S(2)}, u32[]{:S(2)}) collective-permute-start(bf16[784,128]{0,1:T(8,128)(2,1)S(1)} %fusion.46), channel_id=1, source_target_pairs={{0,32},{16,48},{32,64},{48,80},{64,96},{80,112},{96,0},{112,16},{1... | collective-permute-start | bytes 602120 | tf_op jit(solution)/shard_map/ppermute | solution.py:60
  84.3 10.4 %collective-permute-start.6 = (bf16[784,128]{0,1:T(8,128)(2,1)S(1)}, bf16[784,128]{0,1:T(8,128)(2,1)S(1)}, u32[]{:S(2)}, u32[]{:S(2)}) collective-permute-start(bf16[784,128]{0,1:T(8,128)(2,1)S(1)} %fusion.46), channel_id=1, source_target_pairs={{0,16},{16,32},{32,48},{48,64},{64,80},{80,96},{96,112},{112,0},{1... | collective-permute-start | bytes 602120 | tf_op jit(solution)/shard_map/ppermute | solution.py:60
  95.2 1.9 copy-start
  136.5 37.2 %copy-start.2 = (s32[128,128]{1,0:T(8,128)S(1)}, s32[128,128]{1,0:T(8,128)}, u32[]{:S(2)}) copy-start(s32[128,128]{1,0:T(8,128)} %param.9) | copy-start | bytes 196612
  169.1 21.9 %all-to-all-start.4 = ((f32[16,136,64]{1,2,0:T(8,128)}), f32[16,136,64]{1,2,0:T(8,128)S(1)}, u32[]{:S(2)}, u32[]{:S(2)}) async-start(f32[16,136,64]{1,2,0:T(8,128)} %get-tuple-element.45), calls=%async_computation.4 | async-start | bytes 2097152 | tf_op jit(solution)/shard_map/all_to_all | solution.py:134
  192.8 15.6 %all-to-all-start.1 = ((f32[16,128,64]{1,2,0:T(8,128)}), f32[16,128,64]{1,2,0:T(8,128)S(1)}, u32[]{:S(2)}, u32[]{:S(2)}) async-start(f32[16,128,64]{1,2,0:T(8,128)} %broadcast_in_dim.25), calls=%async_computation.1 | async-start | bytes 1048576 | tf_op jit(solution)/shard_map/all_to_all | solution.py:141
  209.3 17.4 %all-to-all-start.5 = ((f32[16,128,64]{1,2,0:T(8,128)}), f32[16,128,64]{1,2,0:T(8,128)S(1)}, u32[]{:S(2)}, u32[]{:S(2)}) async-start(f32[16,128,64]{1,2,0:T(8,128)} %broadcast_in_dim.29), calls=%async_computation.5 | async-start | bytes 1048576 | tf_op jit(solution)/shard_map/all_to_all | solution.py:141
  241.1 31.1 %copy-start.1 = (s32[768,128]{1,0:T(8,128)S(1)}, s32[768,128]{1,0:T(8,128)}, u32[]{:S(2)}) copy-start(s32[768,128]{1,0:T(8,128)} %param.10) | copy-start | bytes 1179652
  268.6 27.8 %all-to-all-start.2 = ((f32[8,776,64]{1,2,0:T(8,128)}), f32[8,776,64]{1,2,0:T(8,128)S(1)}, u32[]{:S(2)}, u32[]{:S(2)}) async-start(f32[8,776,64]{1,2,0:T(8,128)} %get-tuple-element.42), calls=%async_computation.2 | async-start | bytes 3670016 | tf_op jit(solution)/shard_map/all_to_all | solution.py:153
  297.7 5.4 %collective-permute-start.21 = (bf16[784,64]{0,1:T(8,128)(2,1)S(1)}, bf16[784,64]{0,1:T(8,128)(2,1)S(1)}, u32[]{:S(2)}, u32[]{:S(2)}) collective-permute-start(bf16[784,64]{0,1:T(8,128)(2,1)S(1)} %get-tuple-element.38), channel_id=1, source_target_pairs={{0,112},{16,0},{32,16},{48,32},{64,48},{80,64},{96,80},{112,96},{1... | collective-permute-start | bytes 301064 | tf_op jit(solution)/shard_map/ppermute | solution.py:60
  300.0 10.0 %collective-permute-start.22 = (bf16[784,64]{0,1:T(8,128)(2,1)S(1)}, bf16[784,64]{0,1:T(8,128)(2,1)S(1)}, u32[]{:S(2)}, u32[]{:S(2)}) collective-permute-start(bf16[784,64]{0,1:T(8,128)(2,1)S(1)} %get-tuple-element.38), channel_id=1, source_target_pairs={{0,96},{16,112},{32,0},{48,16},{64,32},{80,48},{96,64},{112,80},{1... | collective-permute-start | bytes 301064 | tf_op jit(solution)/shard_map/ppermute | solution.py:60
  300.0 13.6 %collective-permute-start.23 = (bf16[784,64]{0,1:T(8,128)(2,1)S(1)}, bf16[784,64]{0,1:T(8,128)(2,1)S(1)}, u32[]{:S(2)}, u32[]{:S(2)}) collective-permute-start(bf16[784,64]{0,1:T(8,128)(2,1)S(1)} %get-tuple-element.38), channel_id=1, source_target_pairs={{0,80},{16,96},{32,112},{48,0},{64,16},{80,32},{96,48},{112,64},{1... | collective-permute-start | bytes 301064 | tf_op jit(solution)/shard_map/ppermute | solution.py:60
  300.7 14.0 %collective-permute-start.24 = (bf16[784,64]{0,1:T(8,128)(2,1)S(1)}, bf16[784,64]{0,1:T(8,128)(2,1)S(1)}, u32[]{:S(2)}, u32[]{:S(2)}) collective-permute-start(bf16[784,64]{0,1:T(8,128)(2,1)S(1)} %get-tuple-element.38), channel_id=1, source_target_pairs={{0,64},{16,80},{32,96},{48,112},{64,0},{80,16},{96,32},{112,48},{1... | collective-permute-start | bytes 301064 | tf_op jit(solution)/shard_map/ppermute | solution.py:60
  301.9 13.9 %collective-permute-start.25 = (bf16[784,64]{0,1:T(8,128)(2,1)S(1)}, bf16[784,64]{0,1:T(8,128)(2,1)S(1)}, u32[]{:S(2)}, u32[]{:S(2)}) collective-permute-start(bf16[784,64]{0,1:T(8,128)(2,1)S(1)} %get-tuple-element.38), channel_id=1, source_target_pairs={{0,48},{16,64},{32,80},{48,96},{64,112},{80,0},{96,16},{112,32},{1... | collective-permute-start | bytes 301064 | tf_op jit(solution)/shard_map/ppermute | solution.py:60
  303.0 6.2 %collective-permute-start.7 = (bf16[784,64]{0,1:T(8,128)(2,1)S(1)}, bf16[784,64]{0,1:T(8,128)(2,1)S(1)}, u32[]{:S(2)}, u32[]{:S(2)}) collective-permute-start(bf16[784,64]{0,1:T(8,128)(2,1)S(1)} %get-tuple-element.37), channel_id=1, source_target_pairs={{0,112},{16,0},{32,16},{48,32},{64,48},{80,64},{96,80},{112,96},{1... | collective-permute-start | bytes 301064 | tf_op jit(solution)/shard_map/ppermute | solution.py:60
  309.3 6.6 %collective-permute-start.26 = (bf16[784,64]{0,1:T(8,128)(2,1)S(1)}, bf16[784,64]{0,1:T(8,128)(2,1)S(1)}, u32[]{:S(2)}, u32[]{:S(2)}) collective-permute-start(bf16[784,64]{0,1:T(8,128)(2,1)S(1)} %get-tuple-element.38), channel_id=1, source_target_pairs={{0,32},{16,48},{32,64},{48,80},{64,96},{80,112},{96,0},{112,16},{1... | collective-permute-start | bytes 301064 | tf_op jit(solution)/shard_map/ppermute | solution.py:60
  310.0 8.5 %collective-permute-start.27 = (bf16[784,64]{0,1:T(8,128)(2,1)S(1)}, bf16[784,64]{0,1:T(8,128)(2,1)S(1)}, u32[]{:S(2)}, u32[]{:S(2)}) collective-permute-start(bf16[784,64]{0,1:T(8,128)(2,1)S(1)} %get-tuple-element.38), channel_id=1, source_target_pairs={{0,16},{16,32},{32,48},{48,64},{64,80},{80,96},{96,112},{112,0},{1... | collective-permute-start | bytes 301064 | tf_op jit(solution)/shard_map/ppermute | solution.py:60
  313.6 6.7 %collective-permute-start.8 = (bf16[784,64]{0,1:T(8,128)(2,1)S(1)}, bf16[784,64]{0,1:T(8,128)(2,1)S(1)}, u32[]{:S(2)}, u32[]{:S(2)}) collective-permute-start(bf16[784,64]{0,1:T(8,128)(2,1)S(1)} %get-tuple-element.37), channel_id=1, source_target_pairs={{0,96},{16,112},{32,0},{48,16},{64,32},{80,48},{96,64},{112,80},{1... | collective-permute-start | bytes 301064 | tf_op jit(solution)/shard_map/ppermute | solution.py:60
  314.7 5.7 %collective-permute-start.9 = (bf16[784,64]{0,1:T(8,128)(2,1)S(1)}, bf16[784,64]{0,1:T(8,128)(2,1)S(1)}, u32[]{:S(2)}, u32[]{:S(2)}) collective-permute-start(bf16[784,64]{0,1:T(8,128)(2,1)S(1)} %get-tuple-element.37), channel_id=1, source_target_pairs={{0,80},{16,96},{32,112},{48,0},{64,16},{80,32},{96,48},{112,64},{1... | collective-permute-start | bytes 301064 | tf_op jit(solution)/shard_map/ppermute | solution.py:60
  315.7 5.0 collective-permute-start.10
  315.9 4.8 collective-permute-start.11
  318.5 6.9 %collective-permute-start.12 = (bf16[784,64]{0,1:T(8,128)(2,1)S(1)}, bf16[784,64]{0,1:T(8,128)(2,1)S(1)}, u32[]{:S(2)}, u32[]{:S(2)}) collective-permute-start(bf16[784,64]{0,1:T(8,128)(2,1)S(1)} %get-tuple-element.37), channel_id=1, source_target_pairs={{0,32},{16,48},{32,64},{48,80},{64,96},{80,112},{96,0},{112,16},{1... | collective-permute-start | bytes 301064 | tf_op jit(solution)/shard_map/ppermute | solution.py:60
  320.3 7.6 %collective-permute-start.13 = (bf16[784,64]{0,1:T(8,128)(2,1)S(1)}, bf16[784,64]{0,1:T(8,128)(2,1)S(1)}, u32[]{:S(2)}, u32[]{:S(2)}) collective-permute-start(bf16[784,64]{0,1:T(8,128)(2,1)S(1)} %get-tuple-element.37), channel_id=1, source_target_pairs={{0,16},{16,32},{32,48},{48,64},{64,80},{80,96},{96,112},{112,0},{1... | collective-permute-start | bytes 301064 | tf_op jit(solution)/shard_map/ppermute | solution.py:60
  391.4 21.9 %all-to-all-start.3 = ((f32[16,136,64]{1,2,0:T(8,128)}), f32[16,136,64]{1,2,0:T(8,128)S(1)}, u32[]{:S(2)}, u32[]{:S(2)}) async-start(f32[16,136,64]{1,2,0:T(8,128)} %get-tuple-element.43), calls=%async_computation.3 | async-start | bytes 2097152 | tf_op jit(solution)/shard_map/all_to_all | solution.py:134
  429.9 17.6 %all-to-all-start.8 = ((f32[16,128,64]{1,2,0:T(8,128)}), f32[16,128,64]{1,2,0:T(8,128)S(1)}, u32[]{:S(2)}, u32[]{:S(2)}) async-start(f32[16,128,64]{1,2,0:T(8,128)} %broadcast_in_dim.32), calls=%async_computation.8 | async-start | bytes 1048576 | tf_op jit(solution)/shard_map/all_to_all | solution.py:141
  489.1 27.8 %all-to-all-start.9 = ((f32[8,776,64]{1,2,0:T(8,128)}), f32[8,776,64]{1,2,0:T(8,128)S(1)}, u32[]{:S(2)}, u32[]{:S(2)}) async-start(f32[8,776,64]{1,2,0:T(8,128)} %get-tuple-element.39), calls=%async_computation.9 | async-start | bytes 3670016 | tf_op jit(solution)/shard_map/all_to_all | solution.py:153

commit v4 on v2

--- a/solution.py
+++ b/solution.py
@@ -62,6 +62,10 @@
     return jnp.roll(stacked, me + 1, axis=0)
 
 
+def copy_gather(value, axis, count):
+    return lax.all_to_all(jnp.broadcast_to(value[None], (count,) + value.shape), axis, 0, 0, tiled=False)
+
+
 def shift_of(values):
     return jnp.max(values, axis=0).astype(jnp.bfloat16).astype(jnp.float32)
 
@@ -82,7 +86,7 @@
     block_rows = src_rows * dom_count
     group_rows = tgt_rows * blk_count
 
-    source_block = lax.all_gather(normalized(source_emb), "dom", axis=0, tiled=True)
+    source_block = copy_gather(normalized(source_emb), "dom", dom_count).reshape(src_rows * dom_count, source_emb.shape[1])
     own_targets = normalized(target_emb)
     log_target = jnp.log(target_counts.astype(jnp.float32)) - math.log(all_targets)
     log_source = jnp.log(source_counts.astype(jnp.float32)) - math.log(all_sources)
@@ -105,11 +109,11 @@
             emb_rows = jnp.concatenate(
                 [own_targets, jnp.zeros((tgt_payload_rows - tgt_rows, width), jnp.bfloat16)], axis=0)
             payload = jnp.concatenate([emb_rows, payload], axis=1)
-            gathered = permute_gather(payload, "blk", blk_count)
+            gathered = copy_gather(payload, "blk", blk_count)
             target_group = gathered[:, :tgt_rows, :width].reshape(group_rows, width)
             gathered = gathered[:, :, width:]
         else:
-            gathered = permute_gather(payload, "blk", blk_count)
+            gathered = copy_gather(payload, "blk", blk_count)
         weight_segments = gathered[:, :tgt_rows, :]
         segment_shift = gathered[:, tgt_rows, :].astype(jnp.float32)
         group_shift = jnp.max(segment_shift, axis=0)
@@ -133,9 +137,7 @@
         shares = jnp.sum(received[:, :src_rows, :] * scale[:, None, :], axis=0)
         source_logs = log_source - target_peak - jnp.log(shares)
 
-        block_logs = lax.all_to_all(
-            jnp.broadcast_to(source_logs[None], (dom_count, src_rows, columns)), "dom", 0, 0, tiled=False
-        ).reshape(block_rows, columns)
+        block_logs = copy_gather(source_logs, "dom", dom_count).reshape(block_rows, columns)
         block_peak = jnp.max(block_logs, axis=0)
         source_weights = jnp.exp(block_logs - block_peak).astype(jnp.bfloat16)
         target_partial = jnp.einsum(

time: 358 us -> 335 us (0.936)
  blocking collectives: 150 us -> 179 us
  starting transfers between devices: 44.8 us -> 17.5 us
  waiting for transfers between devices: 77.1 us -> 54.9 us
    all_to_all x1 -> x2, blocking collectives: 45 us -> 87.4 us  [body(): received = lax.all_to_all(pieces, 'blk', 0, 0, tiled=False)]
    all_gather x1 -> x0, blocking collectives: 33.5 us -> none  [body(): lax.all_gather(normalized(source_emb), 'dom', axis=0, tiled=True)]
    ppermute x14 -> x0, starting transfers between devices: 29.6 us -> none  [permute_gather(): lax.ppermute(value, axis, [(i, (i + shift) % count) for i in range(count)])]
    all_to_all x1 -> x2, blocking collectives: 19.8 us -> 41.6 us  [copy_gather(): lax.all_to_all(jnp.broadcast_to(value[None], (count,) + value.shape), axi...]
    ppermute x14 -> x0, waiting for transfers between devices: 21.4 us -> none  [permute_gather(): lax.ppermute(value, axis, [(i, (i + shift) % count) for i in range(count)])]
    unnamed x41 -> x7, local copies, waits for them, and re-layouts: 7.56 us -> 0.9 us
    all_to_all x2 -> x3, starting transfers between devices: 15.2 us -> 17.5 us  [copy_gather(): lax.all_to_all(jnp.broadcast_to(value[None], (count,) + value.shape), axi...]
    all_to_all x2 -> x3, waiting for transfers between devices: 55.7 us -> 54.9 us  [copy_gather(): lax.all_to_all(jnp.broadcast_to(value[None], (count,) + value.shape), axi...]
  transfers between devices with their start and end apart: 16 -> 3, of which waited for: 5 -> 3; matrix products, arithmetic and copies ran while one was open for 1% -> 2% of each run, Pallas kernels for 0% -> 0%
where the time goes in v4:
time: 335 us; the launch traced here: 333 us
  blocking collectives  179 us (53%)
  matrix products  63.9 us (19%)
  waiting for transfers between devices  54.9 us (16%)
  starting transfers between devices  17.5 us (5%)
  other arithmetic  11.2 us (3%)
  local copies, waits for them, and re-layouts  5.73 us (2%)
    all_to_all x2, blocking collectives, body(): received = lax.all_to_all(pieces, 'blk', 0, 0, tiled=False)  87.4 us
    all_to_all x3, waiting for transfers between devices, copy_gather(): lax.all_to_all(jnp.broadcast_to(value[None], (count,) + value.shape), axi...  54.9 us
    all_to_all x2, blocking collectives, body(): received = lax.all_to_all(pieces, 'dom', 0, 0, tiled=False)  49.5 us
    all_to_all x2, blocking collectives, copy_gather(): lax.all_to_all(jnp.broadcast_to(value[None], (count,) + value.shape), axi...  41.6 us
    dot_general x2, matrix products, body(): jnp.einsum('sij,sjc->sic', kernel, weight_segments, preferred_element_typ...  28.1 us
    dot_general x2, matrix products, body(): jnp.einsum('ic,sij->sjc', source_weights, kernel, preferred_element_type=...  23.4 us
    all_to_all x3, starting transfers between devices, copy_gather(): lax.all_to_all(jnp.broadcast_to(value[None], (count,) + value.shape), axi...  17.5 us
    dot_general x1, matrix products, body(): jnp.einsum('id,sjd->sij', source_block, target_group.reshape(blk_count, t...  12.4 us
  transfers between devices with their start and end apart: 3, of which 3 were waited for; matrix products, arithmetic and copies ran while one was open for 2% of the time, Pallas kernels for 0%

profile of v4, /device:TPU:1, one launch (start us, length us, event | category | flops | bytes accessed | tf_op | source)
XLA Modules:
  0.0 332.7 jit_solution(15822774994635126311)
XLA Ops:
  0.6 0.7 fusion.22
  1.4 0.7 fusion.23
  2.1 0.8 broadcast_in_dim.19
  2.9 9.4 %all-to-all-start.1 = ((bf16[16,128,64]{1,2,0:T(8,128)(2,1)}), bf16[16,128,64]{1,2,0:T(8,128)(2,1)S(1)}, u32[]{:S(2)}, u32[]{:S(2)}) async-start(bf16[16,128,64]{1,2,0:T(8,128)(2,1)} %broadcast_in_dim.19), calls=%async_computation.1 | async-start | bytes 524288 | tf_op jit(solution)/shard_map/all_to_all | solution.py:66
  12.3 1.1 reduce_max.100
  13.4 0.9 fusion.19
  14.4 0.9 fusion.20
  15.3 0.2 copy.42
  15.5 1.1 exponential_convert_fusion.2
  16.5 0.2 fusion.18
  16.7 0.2 copy.32
  16.9 4.1 %all-to-all-done.1 = bf16[16,128,64]{1,2,0:T(8,128)(2,1)S(1)} async-done(((bf16[16,128,64]{1,2,0:T(8,128)(2,1)}), bf16[16,128,64]{1,2,0:T(8,128)(2,1)S(1)}, u32[]{:S(2)}, u32[]{:S(2)}) %all-to-all-start.1) | async-done | bytes 262176 | tf_op jit(solution)/shard_map/all_to_all | solution.py:66
  21.0 1.9 broadcast_in_dim.18
  22.9 4.1 %all-to-all-start = ((bf16[8,784,192]{1,2,0:T(8,128)(2,1)}), bf16[8,784,192]{1,2,0:T(8,128)(2,1)S(1)}, u32[]{:S(2)}, u32[]{:S(2)}) async-start(bf16[8,784,192]{1,2,0:T(8,128)(2,1)} %broadcast_in_dim.18), calls=%async_computation | async-start | bytes 5505024 | tf_op jit(solution)/shard_map/all_to_all | solution.py:66
  27.1 0.2 copy.33
  27.3 0.1 reshape.119
  27.4 33.7 %all-to-all-done = bf16[8,784,192]{1,2,0:T(8,128)(2,1)S(1)} async-done(((bf16[8,784,192]{1,2,0:T(8,128)(2,1)}), bf16[8,784,192]{1,2,0:T(8,128)(2,1)S(1)}, u32[]{:S(2)}, u32[]{:S(2)}) %all-to-all-start) | async-done | bytes 2408480 | tf_op jit(solution)/shard_map/all_to_all | solution.py:66
  61.2 0.1 slice_reduce_fusion
  61.3 0.3 exponential_reduce_fusion
  61.6 12.4 %exponential_convert_fusion = bf16[8,768,2048]{2,1,0:T(8,128)(2,1)} fusion(bf16[2048,64,1]{0,1,2:T(8,128)(2,1)S(1)} %reshape.119, bf16[8,784,192]{1,2,0:T(8,128)(2,1)S(1)} %all-to-all-done), kind=kOutput, calls=%fused_computation | convolution fusion | flops 1648361472 | bytes 26214400 | tf_op jit(solution)/shard_map/id,sjd->sij/dot_general | solution.py:122
  74.0 14.6 %multiply_reduce_fusion.1 = f32[2048,128]{1,0:T(8,128)} fusion(f32[8,128]{1,0:T(8,128)S(1)} %exponential_reduce_fusion, bf16[8,768,2048]{2,1,0:T(8,128)(2,1)} %exponential_convert_fusion, bf16[8,784,192]{1,2,0:T(8,128)(2,1)S(1)} %all-to-all-done), kind=kOutput, calls=%fused_computation.6 | convolution fusion | flops 3225157632 | bytes 27791360 | tf_op jit(solution)/shard_map/sij,sjc->sic/dot_general | solution.py:126
  88.6 1.4 maximum_maximum_fusion.2
  90.0 22.6 %all_to_all.45 = f32[16,136,128]{2,1,0:T(8,128)S(1)} all-to-all(f32[16,136,128]{2,1,0:T(8,128)S(1)} %maximum_maximum_fusion.2), channel_id=1, replica_groups=mesh['blk'=8,'dom'=16] {'dom'}, dimensions={0} | all-to-all | bytes 2228224 | tf_op jit(solution)/shard_map/all_to_all | solution.py:133
  112.8 1.2 broadcast_in_dim.21
  113.9 3.9 %all-to-all-start.3 = ((f32[16,128,128]{2,1,0:T(8,128)}), f32[16,128,128]{2,1,0:T(8,128)S(1)}, u32[]{:S(2)}, u32[]{:S(2)}) async-start(f32[16,128,128]{2,1,0:T(8,128)} %broadcast_in_dim.21), calls=%async_computation.3 | async-start | bytes 2097152 | tf_op jit(solution)/shard_map/all_to_all | solution.py:66
  117.9 17.1 %all-to-all-done.3 = f32[16,128,128]{2,1,0:T(8,128)S(1)} async-done(((f32[16,128,128]{2,1,0:T(8,128)}), f32[16,128,128]{2,1,0:T(8,128)S(1)}, u32[]{:S(2)}, u32[]{:S(2)}) %all-to-all-start.3) | async-done | bytes 1048608 | tf_op jit(solution)/shard_map/all_to_all | solution.py:66
  135.0 0.3 reduce_max.104
  135.3 0.1 fusion.13
  135.4 11.7 %fusion.2 = f32[8,768,128]{2,1,0:T(8,128)S(1)} fusion(bf16[8,768,2048]{2,1,0:T(8,128)(2,1)} %exponential_convert_fusion, bf16[2048,128]{1,0:T(8,128)(2,1)S(1)} %fusion.13), kind=kOutput, calls=%fused_computation.3 | convolution fusion | flops 3221225472 | bytes 28835840 | tf_op jit(solution)/shard_map/ic,sij->sjc/dot_general | solution.py:143
  147.1 0.3 maximum_maximum_fusion
  147.4 47.7 %all_to_all.46 = f32[8,776,128]{2,1,0:T(8,128)S(1)} all-to-all(f32[8,776,128]{2,1,0:T(8,128)S(1)} %maximum_maximum_fusion), channel_id=1, replica_groups=mesh['blk'=8,'dom'=16] {'blk'}, dimensions={0} | all-to-all | bytes 6356992 | tf_op jit(solution)/shard_map/all_to_all | solution.py:150
  195.2 0.2 fusion.5
  195.4 0.7 copy-done
  196.1 0.2 fusion.21
  196.3 0.2 exponential_convert_fusion.1
  196.5 0.2 broadcast_in_dim.23
  196.7 21.8 %all_to_all.47 = bf16[8,784,128]{2,1,0:T(8,128)(2,1)S(1)} all-to-all(bf16[8,784,128]{2,1,0:T(8,128)(2,1)S(1)} %broadcast_in_dim.23), channel_id=1, replica_groups=mesh['blk'=8,'dom'=16] {'blk'}, dimensions={0} | all-to-all | bytes 3211264 | tf_op jit(solution)/shard_map/all_to_all | solution.py:66
  218.6 13.6 %multiply_reduce_fusion = f32[2048,128]{1,0:T(8,128)S(1)} fusion(f32[8,128]{1,0:T(8,128)S(1)} %bitcast.51, bf16[8,768,2048]{2,1,0:T(8,128)(2,1)} %exponential_convert_fusion, bf16[8,784,128]{2,1,0:T(8,128)(2,1)S(1)} %all_to_all.47), kind=kOutput, calls=%fused_computation.5 | convolution fusion | flops 3225157632 | bytes 27791360 | tf_op jit(solution)/shard_map/sij,sjc->sic/dot_general | solution.py:126
  232.2 0.1 maximum_maximum_fusion.3
  232.3 26.9 %all_to_all.48 = f32[16,136,128]{2,1,0:T(8,128)S(1)} all-to-all(f32[16,136,128]{2,1,0:T(8,128)S(1)} %maximum_maximum_fusion.3), channel_id=1, replica_groups=mesh['blk'=8,'dom'=16] {'dom'}, dimensions={0} | all-to-all | bytes 2228224 | tf_op jit(solution)/shard_map/all_to_all | solution.py:133
  259.5 19.8 %all_to_all.49 = f32[16,128,128]{2,1,0:T(8,128)S(1)} all-to-all(f32[16,128,128]{2,1,0:T(8,128)S(1)} %broadcast_in_dim.25), channel_id=1, replica_groups=mesh['blk'=8,'dom'=16] {'dom'}, dimensions={0} | all-to-all | bytes 2097152 | tf_op jit(solution)/shard_map/all_to_all | solution.py:66
  279.3 0.3 reduce_max.110
  279.6 0.1 fusion.11
  279.7 11.7 %fusion = f32[8,768,128]{2,1,0:T(8,128)S(1)} fusion(bf16[8,768,2048]{2,1,0:T(8,128)(2,1)} %exponential_convert_fusion, bf16[2048,128]{1,0:T(8,128)(2,1)S(1)} %fusion.11), kind=kOutput, calls=%fused_computation.1 | convolution fusion | flops 3221225472 | bytes 28835840 | tf_op jit(solution)/shard_map/ic,sij->sjc/dot_general | solution.py:143
  291.5 0.3 maximum_maximum_fusion.1
  291.8 39.7 %all_to_all.50 = f32[8,776,128]{2,1,0:T(8,128)S(1)} all-to-all(f32[8,776,128]{2,1,0:T(8,128)S(1)} %maximum_maximum_fusion.1), channel_id=1, replica_groups=mesh['blk'=8,'dom'=16] {'blk'}, dimensions={0} | all-to-all | bytes 6356992 | tf_op jit(solution)/shard_map/all_to_all | solution.py:150
  331.5 0.2 fusion.4
  331.8 0.9 log_subtract_fusion
  (37 shorter events, 0.8 us)
Async XLA Ops:
  2.9 18.1 %all-to-all-start.1 = ((bf16[16,128,64]{1,2,0:T(8,128)(2,1)}), bf16[16,128,64]{1,2,0:T(8,128)(2,1)S(1)}, u32[]{:S(2)}, u32[]{:S(2)}) async-start(bf16[16,128,64]{1,2,0:T(8,128)(2,1)} %broadcast_in_dim.19), calls=%async_computation.1 | async-start | bytes 524288 | tf_op jit(solution)/shard_map/all_to_all | solution.py:66
  22.9 38.3 %all-to-all-start = ((bf16[8,784,192]{1,2,0:T(8,128)(2,1)}), bf16[8,784,192]{1,2,0:T(8,128)(2,1)S(1)}, u32[]{:S(2)}, u32[]{:S(2)}) async-start(bf16[8,784,192]{1,2,0:T(8,128)(2,1)} %broadcast_in_dim.18), calls=%async_computation | async-start | bytes 5505024 | tf_op jit(solution)/shard_map/all_to_all | solution.py:66
  88.6 24.1 %copy-start.1 = (s32[128,128]{1,0:T(8,128)S(1)}, s32[128,128]{1,0:T(8,128)}, u32[]{:S(2)}) copy-start(s32[128,128]{1,0:T(8,128)} %param.7) | copy-start | bytes 196612
  113.9 21.1 %all-to-all-start.3 = ((f32[16,128,128]{2,1,0:T(8,128)}), f32[16,128,128]{2,1,0:T(8,128)S(1)}, u32[]{:S(2)}, u32[]{:S(2)}) async-start(f32[16,128,128]{2,1,0:T(8,128)} %broadcast_in_dim.21), calls=%async_computation.3 | async-start | bytes 2097152 | tf_op jit(solution)/shard_map/all_to_all | solution.py:66
  195.1 1.0 copy-start
  259.4 32.0 %copy-start.2 = (f32[128,128]{1,0:T(8,128)}, f32[128,128]{1,0:T(8,128)S(1)}, u32[]{:S(2)}) copy-start(f32[128,128]{1,0:T(8,128)S(1)} %log_subtract_fusion.2) | copy-start | bytes 196612

commit v5 on v4

--- a/solution.py
+++ b/solution.py
@@ -86,13 +86,15 @@
     block_rows = src_rows * dom_count
     group_rows = tgt_rows * blk_count
 
-    source_block = copy_gather(normalized(source_emb), "dom", dom_count).reshape(src_rows * dom_count, source_emb.shape[1])
+    source_block = permute_gather(normalized(source_emb), "dom", dom_count).reshape(
+        src_rows * dom_count, source_emb.shape[1])
     own_targets = normalized(target_emb)
     log_target = jnp.log(target_counts.astype(jnp.float32)) - math.log(all_targets)
     log_source = jnp.log(source_counts.astype(jnp.float32)) - math.log(all_sources)
 
     tgt_payload_rows = padded_rows(tgt_rows + 1, 16)
     src_piece_rows = padded_rows(src_rows + 1, 8)
+    src_payload_rows = padded_rows(src_rows + 1, 16)
     tgt_piece_rows = padded_rows(tgt_rows + 1, 8)
 
     target_logs = warm_start
@@ -137,9 +139,17 @@
         shares = jnp.sum(received[:, :src_rows, :] * scale[:, None, :], axis=0)
         source_logs = log_source - target_peak - jnp.log(shares)
 
-        block_logs = copy_gather(source_logs, "dom", dom_count).reshape(block_rows, columns)
-        block_peak = jnp.max(block_logs, axis=0)
-        source_weights = jnp.exp(block_logs - block_peak).astype(jnp.bfloat16)
+        own_shift = shift_of(source_logs)
+        own_weights = jnp.exp(source_logs - own_shift).astype(jnp.bfloat16)
+        payload = jnp.concatenate(
+            [own_weights, own_shift.astype(jnp.bfloat16)[None, :],
+             jnp.zeros((src_payload_rows - src_rows - 1, columns), jnp.bfloat16)], axis=0)
+        gathered = copy_gather(payload, "dom", dom_count)
+        owner_shift = gathered[:, src_rows, :].astype(jnp.float32)
+        block_peak = jnp.max(owner_shift, axis=0)
+        owner_factor = jnp.exp(owner_shift - block_peak[None, :])
+        source_weights = (gathered[:, :src_rows, :].astype(jnp.float32) * owner_factor[:, None, :]).astype(
+            jnp.bfloat16).reshape(block_rows, columns)
         target_partial = jnp.einsum(
             "ic,sij->sjc", source_weights, kernel, preferred_element_type=jnp.float32
         ).reshape(group_rows, columns)

time: 335 us -> 368 us (1.099)
  starting transfers between devices: 17.5 us -> 69.8 us
  waiting for transfers between devices: 54.9 us -> 41.5 us
    ppermute x0 -> x15, starting transfers between devices: none -> 61.7 us  [permute_gather(): lax.ppermute(value, axis, [(i, (i + shift) % count) for i in range(count)])]
    all_to_all x3 -> x2, waiting for transfers between devices: 54.9 us -> 11.9 us  [copy_gather(): lax.all_to_all(jnp.broadcast_to(value[None], (count,) + value.shape), axi...]
    ppermute x0 -> x15, waiting for transfers between devices: none -> 29.6 us  [permute_gather(): lax.ppermute(value, axis, [(i, (i + shift) % count) for i in range(count)])]
    all_to_all x3 -> x2, starting transfers between devices: 17.5 us -> 8.07 us  [copy_gather(): lax.all_to_all(jnp.broadcast_to(value[None], (count,) + value.shape), axi...]
    all_to_all x2, blocking collectives: 41.6 us -> 37.5 us  [copy_gather(): lax.all_to_all(jnp.broadcast_to(value[None], (count,) + value.shape), axi...]
  transfers between devices with their start and end apart: 3 -> 17, of which waited for: 3 -> 11; matrix products, arithmetic and copies ran while one was open for 2% -> 2% of each run, Pallas kernels for 0% -> 0%
where the time goes in v5:
time: 368 us
  blocking collectives  176 us (48%)
  starting transfers between devices  69.8 us (19%)
  matrix products  63.8 us (17%)
  waiting for transfers between devices  41.5 us (11%)
  other arithmetic  10.9 us (3%)
  local copies, waits for them, and re-layouts  5.03 us (1%)
    all_to_all x2, blocking collectives, body(): received = lax.all_to_all(pieces, 'blk', 0, 0, tiled=False)  87.3 us
    ppermute x15, starting transfers between devices, permute_gather(): lax.ppermute(value, axis, [(i, (i + shift) % count) for i in range(count)])  61.7 us
    all_to_all x2, blocking collectives, body(): received = lax.all_to_all(pieces, 'dom', 0, 0, tiled=False)  50.8 us
    all_to_all x2, blocking collectives, copy_gather(): lax.all_to_all(jnp.broadcast_to(value[None], (count,) + value.shape), axi...  37.5 us
    ppermute x15, waiting for transfers between devices, permute_gather(): lax.ppermute(value, axis, [(i, (i + shift) % count) for i in range(count)])  29.6 us
    dot_general x2, matrix products, body(): jnp.einsum('sij,sjc->sic', kernel, weight_segments, preferred_element_typ...  28 us
    dot_general x2, matrix products, body(): jnp.einsum('ic,sij->sjc', source_weights, kernel, preferred_element_type=...  23.4 us
    dot_general x1, matrix products, body(): jnp.einsum('id,sjd->sij', source_block, target_group.reshape(blk_count, t...  12.4 us
  transfers between devices with their start and end apart: 17, of which 11 were waited for; matrix products, arithmetic and copies ran while one was open for 2% of the time, Pallas kernels for 0%

profile of v5, /device:TPU:1, one launch (start us, length us, event | category | flops | bytes accessed | tf_op | source)
XLA Modules:
  0.0 367.6 jit_solution(2103141699939250008)
XLA Ops:
  0.6 0.7 fusion.16
  1.4 0.7 fusion.17
  2.1 3.0 collective-permute-start.14
  5.1 1.6 collective-permute-start.13
  6.8 2.0 collective-permute-start.12
  8.8 2.3 collective-permute-start.11
  11.1 1.2 collective-permute-start
  12.3 1.1 reduce_max.128
  13.4 0.9 fusion.13
  14.3 0.9 fusion.14
  15.4 1.1 exponential_convert_fusion.2
  16.9 1.9 broadcast_in_dim.16
  18.9 4.3 %all-to-all-start = ((bf16[8,784,192]{1,2,0:T(8,128)(2,1)}), bf16[8,784,192]{1,2,0:T(8,128)(2,1)S(1)}, u32[]{:S(2)}, u32[]{:S(2)}) async-start(bf16[8,784,192]{1,2,0:T(8,128)(2,1)} %broadcast_in_dim.16), calls=%async_computation | async-start | bytes 5505024 | tf_op jit(solution)/shard_map/all_to_all | solution.py:66
  23.2 3.5 collective-permute-start.1
  26.7 1.8 collective-permute-done.1
  28.5 23.9 %collective-permute-start.2 = (bf16[128,64]{0,1:T(8,128)(2,1)S(1)}, bf16[128,64]{0,1:T(8,128)(2,1)S(1)}, u32[]{:S(2)}, u32[]{:S(2)}) collective-permute-start(bf16[128,64]{0,1:T(8,128)(2,1)S(1)} %fusion.17), channel_id=1, source_target_pairs={{0,13},{1,14},{2,15},{3,0},{4,1},{5,2},{6,3},{7,4},{8,5},{9,6},{10... | collective-permute-start | bytes 49160 | tf_op jit(solution)/shard_map/ppermute | solution.py:60
  52.4 3.7 %collective-permute-done.2 = bf16[128,64]{0,1:T(8,128)(2,1)S(1)} collective-permute-done((bf16[128,64]{0,1:T(8,128)(2,1)S(1)}, bf16[128,64]{0,1:T(8,128)(2,1)S(1)}, u32[]{:S(2)}, u32[]{:S(2)}) %collective-permute-start.2) | collective-permute-done | bytes 16416 | tf_op jit(solution)/shard_map/ppermute | solution.py:60
  56.1 4.1 %collective-permute-done.3 = bf16[128,64]{0,1:T(8,128)(2,1)S(1)} collective-permute-done((bf16[128,64]{0,1:T(8,128)(2,1)S(1)}, bf16[128,64]{0,1:T(8,128)(2,1)S(1)}, u32[]{:S(2)}, u32[]{:S(2)}) %collective-permute-start.3) | collective-permute-done | bytes 16416 | tf_op jit(solution)/shard_map/ppermute | solution.py:60
  60.2 2.2 collective-permute-start.4
  62.4 7.7 %collective-permute-done.4 = bf16[128,64]{0,1:T(8,128)(2,1)S(1)} collective-permute-done((bf16[128,64]{0,1:T(8,128)(2,1)S(1)}, bf16[128,64]{0,1:T(8,128)(2,1)S(1)}, u32[]{:S(2)}, u32[]{:S(2)}) %collective-permute-start.4) | collective-permute-done | bytes 16416 | tf_op jit(solution)/shard_map/ppermute | solution.py:60
  70.1 2.4 collective-permute-start.5
  72.5 1.4 collective-permute-done.5
  73.9 2.6 collective-permute-start.6
  76.6 4.0 %collective-permute-done.6 = bf16[128,64]{0,1:T(8,128)(2,1)S(1)} collective-permute-done((bf16[128,64]{0,1:T(8,128)(2,1)S(1)}, bf16[128,64]{0,1:T(8,128)(2,1)S(1)}, u32[]{:S(2)}, u32[]{:S(2)}) %collective-permute-start.6) | collective-permute-done | bytes 16416 | tf_op jit(solution)/shard_map/ppermute | solution.py:60
  80.6 1.6 collective-permute-start.7
  82.2 2.5 collective-permute-done.7
  84.7 4.1 %collective-permute-start.8 = (bf16[128,64]{0,1:T(8,128)(2,1)S(1)}, bf16[128,64]{0,1:T(8,128)(2,1)S(1)}, u32[]{:S(2)}, u32[]{:S(2)}) collective-permute-start(bf16[128,64]{0,1:T(8,128)(2,1)S(1)} %fusion.17), channel_id=1, source_target_pairs={{0,7},{1,8},{2,9},{3,10},{4,11},{5,12},{6,13},{7,14},{8,15},{9,0},... | collective-permute-start | bytes 49160 | tf_op jit(solution)/shard_map/ppermute | solution.py:60
  88.8 1.5 collective-permute-done.8
  90.3 4.7 %collective-permute-start.9 = (bf16[128,64]{0,1:T(8,128)(2,1)S(1)}, bf16[128,64]{0,1:T(8,128)(2,1)S(1)}, u32[]{:S(2)}, u32[]{:S(2)}) collective-permute-start(bf16[128,64]{0,1:T(8,128)(2,1)S(1)} %fusion.17), channel_id=1, source_target_pairs={{0,6},{1,7},{2,8},{3,9},{4,10},{5,11},{6,12},{7,13},{8,14},{9,15},... | collective-permute-start | bytes 49160 | tf_op jit(solution)/shard_map/ppermute | solution.py:60
  95.0 0.9 collective-permute-done.9
  95.9 6.5 %collective-permute-start.10 = (bf16[128,64]{0,1:T(8,128)(2,1)S(1)}, bf16[128,64]{0,1:T(8,128)(2,1)S(1)}, u32[]{:S(2)}, u32[]{:S(2)}) collective-permute-start(bf16[128,64]{0,1:T(8,128)(2,1)S(1)} %fusion.17), channel_id=1, source_target_pairs={{0,5},{1,6},{2,7},{3,8},{4,9},{5,10},{6,11},{7,12},{8,13},{9,14},{... | collective-permute-start | bytes 49160 | tf_op jit(solution)/shard_map/ppermute | solution.py:60
  102.3 2.0 collective-permute-done.10
  105.5 12.4 %exponential_convert_fusion = bf16[8,768,2048]{2,1,0:T(8,128)(2,1)} fusion(bf16[2048,64,1]{0,1,2:T(8,128)(2,1)S(1)} %reshape.160, bf16[8,784,192]{1,2,0:T(8,128)(2,1)S(1)} %all-to-all-done), kind=kOutput, calls=%fused_computation | convolution fusion | flops 1648361472 | bytes 26214400 | tf_op jit(solution)/shard_map/id,sjd->sij/dot_general | solution.py:124
  117.9 14.6 %multiply_reduce_fusion.1 = f32[2048,128]{1,0:T(8,128)} fusion(f32[8,128]{1,0:T(8,128)S(1)} %exponential_reduce_fusion, bf16[8,768,2048]{2,1,0:T(8,128)(2,1)} %exponential_convert_fusion, bf16[8,784,192]{1,2,0:T(8,128)(2,1)S(1)} %all-to-all-done), kind=kOutput, calls=%fused_computation.6 | convolution fusion | flops 3225157632 | bytes 27791360 | tf_op jit(solution)/shard_map/sij,sjc->sic/dot_general | solution.py:128
  132.5 1.4 maximum_maximum_fusion.2
  133.9 24.0 %all_to_all.40 = f32[16,136,128]{2,1,0:T(8,128)S(1)} all-to-all(f32[16,136,128]{2,1,0:T(8,128)S(1)} %maximum_maximum_fusion.2), channel_id=1, replica_groups=mesh['blk'=8,'dom'=16] {'dom'}, dimensions={0} | all-to-all | bytes 2228224 | tf_op jit(solution)/shard_map/all_to_all | solution.py:135
  158.1 0.9 broadcast_in_dim.18
  159.0 3.8 %all-to-all-start.2 = ((bf16[16,144,128]{2,1,0:T(8,128)(2,1)}), bf16[16,144,128]{2,1,0:T(8,128)(2,1)S(1)}, u32[]{:S(2)}, u32[]{:S(2)}) async-start(bf16[16,144,128]{2,1,0:T(8,128)(2,1)} %broadcast_in_dim.18), calls=%async_computation.2 | async-start | bytes 1179648 | tf_op jit(solution)/shard_map/all_to_all | solution.py:66
  162.9 11.9 %all-to-all-done.2 = bf16[16,144,128]{2,1,0:T(8,128)(2,1)S(1)} async-done(((bf16[16,144,128]{2,1,0:T(8,128)(2,1)}), bf16[16,144,128]{2,1,0:T(8,128)(2,1)S(1)}, u32[]{:S(2)}, u32[]{:S(2)}) %all-to-all-start.2) | async-done | bytes 589856 | tf_op jit(solution)/shard_map/all_to_all | solution.py:66
  175.0 11.7 %fusion.2 = f32[8,768,128]{2,1,0:T(8,128)S(1)} fusion(bf16[2048,128,1]{1,0,2:T(8,128)(2,1)S(1)} %bitcast.92, bf16[8,768,2048]{2,1,0:T(8,128)(2,1)} %exponential_convert_fusion), kind=kOutput, calls=%fused_computation.3 | convolution fusion | flops 3221225472 | bytes 28835840 | tf_op jit(solution)/shard_map/ic,sij->sjc/dot_general | solution.py:153
  187.0 46.2 %all_to_all.41 = f32[8,776,128]{2,1,0:T(8,128)S(1)} all-to-all(f32[8,776,128]{2,1,0:T(8,128)S(1)} %maximum_maximum_fusion), channel_id=1, replica_groups=mesh['blk'=8,'dom'=16] {'blk'}, dimensions={0} | all-to-all | bytes 6356992 | tf_op jit(solution)/shard_map/all_to_all | solution.py:160
  234.9 21.8 %all_to_all.42 = bf16[8,784,128]{2,1,0:T(8,128)(2,1)S(1)} all-to-all(bf16[8,784,128]{2,1,0:T(8,128)(2,1)S(1)} %broadcast_in_dim.20), channel_id=1, replica_groups=mesh['blk'=8,'dom'=16] {'blk'}, dimensions={0} | all-to-all | bytes 3211264 | tf_op jit(solution)/shard_map/all_to_all | solution.py:66
  256.7 13.5 %multiply_reduce_fusion = f32[2048,128]{1,0:T(8,128)S(1)} fusion(f32[8,128]{1,0:T(8,128)S(1)} %bitcast.101, bf16[8,768,2048]{2,1,0:T(8,128)(2,1)} %exponential_convert_fusion, bf16[8,784,128]{2,1,0:T(8,128)(2,1)S(1)} %all_to_all.42), kind=kOutput, calls=%fused_computation.5 | convolution fusion | flops 3225157632 | bytes 27791360 | tf_op jit(solution)/shard_map/sij,sjc->sic/dot_general | solution.py:128
  270.4 26.8 %all_to_all.43 = f32[16,136,128]{2,1,0:T(8,128)S(1)} all-to-all(f32[16,136,128]{2,1,0:T(8,128)S(1)} %maximum_maximum_fusion.3), channel_id=1, replica_groups=mesh['blk'=8,'dom'=16] {'dom'}, dimensions={0} | all-to-all | bytes 2228224 | tf_op jit(solution)/shard_map/all_to_all | solution.py:135
  297.5 15.6 %all_to_all.44 = bf16[16,144,128]{2,1,0:T(8,128)(2,1)S(1)} all-to-all(bf16[16,144,128]{2,1,0:T(8,128)(2,1)S(1)} %broadcast_in_dim.22), channel_id=1, replica_groups=mesh['blk'=8,'dom'=16] {'dom'}, dimensions={0} | all-to-all | bytes 1179648 | tf_op jit(solution)/shard_map/all_to_all | solution.py:66
  313.4 11.7 %fusion = f32[8,768,128]{2,1,0:T(8,128)S(1)} fusion(bf16[2048,128,1]{1,0,2:T(8,128)(2,1)S(1)} %bitcast.91, bf16[8,768,2048]{2,1,0:T(8,128)(2,1)} %exponential_convert_fusion), kind=kOutput, calls=%fused_computation.1 | convolution fusion | flops 3221225472 | bytes 28835840 | tf_op jit(solution)/shard_map/ic,sij->sjc/dot_general | solution.py:153
  325.4 41.0 %all_to_all.45 = f32[8,776,128]{2,1,0:T(8,128)S(1)} all-to-all(f32[8,776,128]{2,1,0:T(8,128)S(1)} %maximum_maximum_fusion.1), channel_id=1, replica_groups=mesh['blk'=8,'dom'=16] {'blk'}, dimensions={0} | all-to-all | bytes 6356992 | tf_op jit(solution)/shard_map/all_to_all | solution.py:160
  366.7 0.9 log_subtract_fusion
  (109 shorter events, 5.4 us)
Async XLA Ops:
  2.1 102.3 %collective-permute-start.14 = (bf16[128,64]{0,1:T(8,128)(2,1)S(1)}, bf16[128,64]{0,1:T(8,128)(2,1)S(1)}, u32[]{:S(2)}, u32[]{:S(2)}) collective-permute-start(bf16[128,64]{0,1:T(8,128)(2,1)S(1)} %fusion.17), channel_id=1, source_target_pairs={{0,1},{1,2},{2,3},{3,4},{4,5},{5,6},{6,7},{7,8},{8,9},{9,10},{10,1... | collective-permute-start | bytes 49160 | tf_op jit(solution)/shard_map/ppermute | solution.py:60
  5.1 99.3 %collective-permute-start.13 = (bf16[128,64]{0,1:T(8,128)(2,1)S(1)}, bf16[128,64]{0,1:T(8,128)(2,1)S(1)}, u32[]{:S(2)}, u32[]{:S(2)}) collective-permute-start(bf16[128,64]{0,1:T(8,128)(2,1)S(1)} %fusion.17), channel_id=1, source_target_pairs={{0,2},{1,3},{2,4},{3,5},{4,6},{5,7},{6,8},{7,9},{8,10},{9,11},{10,... | collective-permute-start | bytes 49160 | tf_op jit(solution)/shard_map/ppermute | solution.py:60
  6.8 97.6 %collective-permute-start.12 = (bf16[128,64]{0,1:T(8,128)(2,1)S(1)}, bf16[128,64]{0,1:T(8,128)(2,1)S(1)}, u32[]{:S(2)}, u32[]{:S(2)}) collective-permute-start(bf16[128,64]{0,1:T(8,128)(2,1)S(1)} %fusion.17), channel_id=1, source_target_pairs={{0,3},{1,4},{2,5},{3,6},{4,7},{5,8},{6,9},{7,10},{8,11},{9,12},{10... | collective-permute-start | bytes 49160 | tf_op jit(solution)/shard_map/ppermute | solution.py:60
  8.8 95.6 %collective-permute-start.11 = (bf16[128,64]{0,1:T(8,128)(2,1)S(1)}, bf16[128,64]{0,1:T(8,128)(2,1)S(1)}, u32[]{:S(2)}, u32[]{:S(2)}) collective-permute-start(bf16[128,64]{0,1:T(8,128)(2,1)S(1)} %fusion.17), channel_id=1, source_target_pairs={{0,4},{1,5},{2,6},{3,7},{4,8},{5,9},{6,10},{7,11},{8,12},{9,13},{1... | collective-permute-start | bytes 49160 | tf_op jit(solution)/shard_map/ppermute | solution.py:60
  11.1 12.1 %collective-permute-start = (bf16[128,64]{0,1:T(8,128)(2,1)S(1)}, bf16[128,64]{0,1:T(8,128)(2,1)S(1)}, u32[]{:S(2)}, u32[]{:S(2)}) collective-permute-start(bf16[128,64]{0,1:T(8,128)(2,1)S(1)} %fusion.17), channel_id=1, source_target_pairs={{0,15},{1,0},{2,1},{3,2},{4,3},{5,4},{6,5},{7,6},{8,7},{9,8},{10,9... | collective-permute-start | bytes 49160 | tf_op jit(solution)/shard_map/ppermute | solution.py:60
  18.9 85.6 %copy-start.3 = (bf16[128,64]{0,1:T(8,128)(2,1)S(1)}, bf16[128,64]{0,1:T(8,128)(2,1)}, u32[]{:S(2)}) copy-start(bf16[128,64]{0,1:T(8,128)(2,1)} %param.5) | copy-start | bytes 49156
  18.9 86.2 %all-to-all-start = ((bf16[8,784,192]{1,2,0:T(8,128)(2,1)}), bf16[8,784,192]{1,2,0:T(8,128)(2,1)S(1)}, u32[]{:S(2)}, u32[]{:S(2)}) async-start(bf16[8,784,192]{1,2,0:T(8,128)(2,1)} %broadcast_in_dim.16), calls=%async_computation | async-start | bytes 5505024 | tf_op jit(solution)/shard_map/all_to_all | solution.py:66
  23.2 5.3 %collective-permute-start.1 = (bf16[128,64]{0,1:T(8,128)(2,1)S(1)}, bf16[128,64]{0,1:T(8,128)(2,1)S(1)}, u32[]{:S(2)}, u32[]{:S(2)}) collective-permute-start(bf16[128,64]{0,1:T(8,128)(2,1)S(1)} %fusion.17), channel_id=1, source_target_pairs={{0,14},{1,15},{2,0},{3,1},{4,2},{5,3},{6,4},{7,5},{8,6},{9,7},{10,... | collective-permute-start | bytes 49160 | tf_op jit(solution)/shard_map/ppermute | solution.py:60
  28.5 27.6 %collective-permute-start.2 = (bf16[128,64]{0,1:T(8,128)(2,1)S(1)}, bf16[128,64]{0,1:T(8,128)(2,1)S(1)}, u32[]{:S(2)}, u32[]{:S(2)}) collective-permute-start(bf16[128,64]{0,1:T(8,128)(2,1)S(1)} %fusion.17), channel_id=1, source_target_pairs={{0,13},{1,14},{2,15},{3,0},{4,1},{5,2},{6,3},{7,4},{8,5},{9,6},{10... | collective-permute-start | bytes 49160 | tf_op jit(solution)/shard_map/ppermute | solution.py:60
  56.1 4.1 %collective-permute-start.3 = (bf16[128,64]{0,1:T(8,128)(2,1)S(1)}, bf16[128,64]{0,1:T(8,128)(2,1)S(1)}, u32[]{:S(2)}, u32[]{:S(2)}) collective-permute-start(bf16[128,64]{0,1:T(8,128)(2,1)S(1)} %fusion.17), channel_id=1, source_target_pairs={{0,12},{1,13},{2,14},{3,15},{4,0},{5,1},{6,2},{7,3},{8,4},{9,5},{1... | collective-permute-start | bytes 49160 | tf_op jit(solution)/shard_map/ppermute | solution.py:60
  60.2 9.9 %collective-permute-start.4 = (bf16[128,64]{0,1:T(8,128)(2,1)S(1)}, bf16[128,64]{0,1:T(8,128)(2,1)S(1)}, u32[]{:S(2)}, u32[]{:S(2)}) collective-permute-start(bf16[128,64]{0,1:T(8,128)(2,1)S(1)} %fusion.17), channel_id=1, source_target_pairs={{0,11},{1,12},{2,13},{3,14},{4,15},{5,0},{6,1},{7,2},{8,3},{9,4},{... | collective-permute-start | bytes 49160 | tf_op jit(solution)/shard_map/ppermute | solution.py:60
  70.1 3.8 %collective-permute-start.5 = (bf16[128,64]{0,1:T(8,128)(2,1)S(1)}, bf16[128,64]{0,1:T(8,128)(2,1)S(1)}, u32[]{:S(2)}, u32[]{:S(2)}) collective-permute-start(bf16[128,64]{0,1:T(8,128)(2,1)S(1)} %fusion.17), channel_id=1, source_target_pairs={{0,10},{1,11},{2,12},{3,13},{4,14},{5,15},{6,0},{7,1},{8,2},{9,3},... | collective-permute-start | bytes 49160 | tf_op jit(solution)/shard_map/ppermute | solution.py:60
  73.9 6.7 %collective-permute-start.6 = (bf16[128,64]{0,1:T(8,128)(2,1)S(1)}, bf16[128,64]{0,1:T(8,128)(2,1)S(1)}, u32[]{:S(2)}, u32[]{:S(2)}) collective-permute-start(bf16[128,64]{0,1:T(8,128)(2,1)S(1)} %fusion.17), channel_id=1, source_target_pairs={{0,9},{1,10},{2,11},{3,12},{4,13},{5,14},{6,15},{7,0},{8,1},{9,2},... | collective-permute-start | bytes 49160 | tf_op jit(solution)/shard_map/ppermute | solution.py:60
  80.6 4.1 %collective-permute-start.7 = (bf16[128,64]{0,1:T(8,128)(2,1)S(1)}, bf16[128,64]{0,1:T(8,128)(2,1)S(1)}, u32[]{:S(2)}, u32[]{:S(2)}) collective-permute-start(bf16[128,64]{0,1:T(8,128)(2,1)S(1)} %fusion.17), channel_id=1, source_target_pairs={{0,8},{1,9},{2,10},{3,11},{4,12},{5,13},{6,14},{7,15},{8,0},{9,1},... | collective-permute-start | bytes 49160 | tf_op jit(solution)/shard_map/ppermute | solution.py:60
  84.7 5.6 %collective-permute-start.8 = (bf16[128,64]{0,1:T(8,128)(2,1)S(1)}, bf16[128,64]{0,1:T(8,128)(2,1)S(1)}, u32[]{:S(2)}, u32[]{:S(2)}) collective-permute-start(bf16[128,64]{0,1:T(8,128)(2,1)S(1)} %fusion.17), channel_id=1, source_target_pairs={{0,7},{1,8},{2,9},{3,10},{4,11},{5,12},{6,13},{7,14},{8,15},{9,0},... | collective-permute-start | bytes 49160 | tf_op jit(solution)/shard_map/ppermute | solution.py:60
  90.3 5.6 %collective-permute-start.9 = (bf16[128,64]{0,1:T(8,128)(2,1)S(1)}, bf16[128,64]{0,1:T(8,128)(2,1)S(1)}, u32[]{:S(2)}, u32[]{:S(2)}) collective-permute-start(bf16[128,64]{0,1:T(8,128)(2,1)S(1)} %fusion.17), channel_id=1, source_target_pairs={{0,6},{1,7},{2,8},{3,9},{4,10},{5,11},{6,12},{7,13},{8,14},{9,15},... | collective-permute-start | bytes 49160 | tf_op jit(solution)/shard_map/ppermute | solution.py:60
  95.9 8.5 %collective-permute-start.10 = (bf16[128,64]{0,1:T(8,128)(2,1)S(1)}, bf16[128,64]{0,1:T(8,128)(2,1)S(1)}, u32[]{:S(2)}, u32[]{:S(2)}) collective-permute-start(bf16[128,64]{0,1:T(8,128)(2,1)S(1)} %fusion.17), channel_id=1, source_target_pairs={{0,5},{1,6},{2,7},{3,8},{4,9},{5,10},{6,11},{7,12},{8,13},{9,14},{... | collective-permute-start | bytes 49160 | tf_op jit(solution)/shard_map/ppermute | solution.py:60
  132.4 25.5 %copy-start.1 = (s32[128,128]{1,0:T(8,128)S(1)}, s32[128,128]{1,0:T(8,128)}, u32[]{:S(2)}) copy-start(s32[128,128]{1,0:T(8,128)} %param.7) | copy-start | bytes 196612
  159.0 15.8 %all-to-all-start.2 = ((bf16[16,144,128]{2,1,0:T(8,128)(2,1)}), bf16[16,144,128]{2,1,0:T(8,128)(2,1)S(1)}, u32[]{:S(2)}, u32[]{:S(2)}) async-start(bf16[16,144,128]{2,1,0:T(8,128)(2,1)} %broadcast_in_dim.18), calls=%async_computation.2 | async-start | bytes 1179648 | tf_op jit(solution)/shard_map/all_to_all | solution.py:66
  233.3 1.0 copy-start
  297.4 27.7 %copy-start.2 = (f32[128,128]{1,0:T(8,128)}, f32[128,128]{1,0:T(8,128)S(1)}, u32[]{:S(2)}) copy-start(f32[128,128]{1,0:T(8,128)S(1)} %get-tuple-element.3) | copy-start | bytes 196612

commit v6 on v5

--- a/solution.py
+++ b/solution.py
@@ -86,9 +86,14 @@
     block_rows = src_rows * dom_count
     group_rows = tgt_rows * blk_count
 
-    source_block = permute_gather(normalized(source_emb), "dom", dom_count).reshape(
+    source_block = copy_gather(normalized(source_emb), "dom", dom_count).reshape(
         src_rows * dom_count, source_emb.shape[1])
-    own_targets = normalized(target_emb)
+    target_group = copy_gather(normalized(target_emb), "blk", blk_count).reshape(
+        tgt_rows * blk_count, target_emb.shape[1])
+    products = jnp.einsum(
+        "id,sjd->sij", source_block, target_group.reshape(blk_count, tgt_rows, source_emb.shape[1]),
+        preferred_element_type=jnp.float32)
+    kernel = jnp.exp((products - 1.0) / entropic).astype(jnp.bfloat16)
     log_target = jnp.log(target_counts.astype(jnp.float32)) - math.log(all_targets)
     log_source = jnp.log(source_counts.astype(jnp.float32)) - math.log(all_sources)
 
@@ -98,33 +103,18 @@
     tgt_piece_rows = padded_rows(tgt_rows + 1, 8)
 
     target_logs = warm_start
-    target_group = None
     source_logs = None
-    kernel = None
     for iteration in range(ITERS):
         shift = shift_of(target_logs)
         weights = jnp.exp(target_logs - shift).astype(jnp.bfloat16)
         payload = jnp.concatenate(
             [weights, shift.astype(jnp.bfloat16)[None, :],
              jnp.zeros((tgt_payload_rows - tgt_rows - 1, columns), jnp.bfloat16)], axis=0)
-        if target_group is None:
-            emb_rows = jnp.concatenate(
-                [own_targets, jnp.zeros((tgt_payload_rows - tgt_rows, width), jnp.bfloat16)], axis=0)
-            payload = jnp.concatenate([emb_rows, payload], axis=1)
-            gathered = copy_gather(payload, "blk", blk_count)
-            target_group = gathered[:, :tgt_rows, :width].reshape(group_rows, width)
-            gathered = gathered[:, :, width:]
-        else:
-            gathered = copy_gather(payload, "blk", blk_count)
+        gathered = copy_gather(payload, "blk", blk_count)
         weight_segments = gathered[:, :tgt_rows, :]
         segment_shift = gathered[:, tgt_rows, :].astype(jnp.float32)
         group_shift = jnp.max(segment_shift, axis=0)
         factors = jnp.exp(segment_shift - group_shift[None, :])
-        if kernel is None:
-            products = jnp.einsum(
-                "id,sjd->sij", source_block, target_group.reshape(blk_count, tgt_rows, width),
-                preferred_element_type=jnp.float32)
-            kernel = jnp.exp((products - 1.0) / entropic).astype(jnp.bfloat16)
         per_segment = jnp.einsum(
             "sij,sjc->sic", kernel, weight_segments, preferred_element_type=jnp.float32)
         partial_value = jnp.sum(per_segment * factors[:, None, :], axis=0)

time: 368 us -> 307 us (0.83)
  starting transfers between devices: 69.8 us -> 21 us
  blocking collectives: 176 us -> 168 us
  other arithmetic: 10.9 us -> 7.15 us
    ppermute x15 -> x0, starting transfers between devices: 61.7 us -> none  [permute_gather(): lax.ppermute(value, axis, [(i, (i + shift) % count) for i in range(count)])]
    ppermute x15 -> x0, waiting for transfers between devices: 29.6 us -> none  [permute_gather(): lax.ppermute(value, axis, [(i, (i + shift) % count) for i in range(count)])]
    all_to_all x2 -> x4, waiting for transfers between devices: 11.9 us -> 40.6 us  [copy_gather(): lax.all_to_all(jnp.broadcast_to(value[None], (count,) + value.shape), axi...]
    all_to_all x2 -> x4, starting transfers between devices: 8.07 us -> 21 us  [copy_gather(): lax.all_to_all(jnp.broadcast_to(value[None], (count,) + value.shape), axi...]
    all_to_all x2, blocking collectives: 87.3 us -> 80.8 us  [body(): received = lax.all_to_all(pieces, 'blk', 0, 0, tiled=False)]
  transfers between devices with their start and end apart: 17 -> 4, of which waited for: 11 -> 4; matrix products, arithmetic and copies ran while one was open for 2% -> 5% of each run, Pallas kernels for 0% -> 0%
where the time goes in v6:
time: 307 us; the launch traced here: 306 us
  blocking collectives  168 us (55%)
  matrix products  62.8 us (20%)
  waiting for transfers between devices  40.6 us (13%)
  starting transfers between devices  21 us (7%)
  other arithmetic  7.15 us (2%)
  local copies, waits for them, and re-layouts  5.59 us (2%)
    all_to_all x2, blocking collectives, body(): received = lax.all_to_all(pieces, 'blk', 0, 0, tiled=False)  80.8 us
    all_to_all x2, blocking collectives, body(): received = lax.all_to_all(pieces, 'dom', 0, 0, tiled=False)  49.6 us
    all_to_all x4, waiting for transfers between devices, copy_gather(): lax.all_to_all(jnp.broadcast_to(value[None], (count,) + value.shape), axi...  40.6 us
    all_to_all x2, blocking collectives, copy_gather(): lax.all_to_all(jnp.broadcast_to(value[None], (count,) + value.shape), axi...  37.5 us
    dot_general x2, matrix products, body(): jnp.einsum('sij,sjc->sic', kernel, weight_segments, preferred_element_typ...  26.9 us
    dot_general x2, matrix products, body(): jnp.einsum('ic,sij->sjc', source_weights, kernel, preferred_element_type=...  23.4 us
    all_to_all x4, starting transfers between devices, copy_gather(): lax.all_to_all(jnp.broadcast_to(value[None], (count,) + value.shape), axi...  21 us
    dot_general x1, matrix products, body(): jnp.einsum('id,sjd->sij', source_block, target_group.reshape(blk_count, t...  12.4 us
  transfers between devices with their start and end apart: 4, of which 4 were waited for; matrix products, arithmetic and copies ran while one was open for 5% of the time, Pallas kernels for 0%

profile of v6, /device:TPU:1, one launch (start us, length us, event | category | flops | bytes accessed | tf_op | source)
XLA Modules:
  0.0 305.8 jit_solution(16252174445158965016)
XLA Ops:
  0.6 0.8 fusion.13
  1.4 0.7 fusion.14
  2.2 0.8 broadcast_in_dim.21
  2.9 9.4 %all-to-all-start.1 = ((bf16[16,128,64]{1,2,0:T(8,128)(2,1)}), bf16[16,128,64]{1,2,0:T(8,128)(2,1)S(1)}, u32[]{:S(2)}, u32[]{:S(2)}) async-start(bf16[16,128,64]{1,2,0:T(8,128)(2,1)} %broadcast_in_dim.21), calls=%async_computation.1 | async-start | bytes 524288 | tf_op jit(solution)/shard_map/all_to_all | solution.py:66
  12.4 0.9 fusion.10
  13.3 0.9 fusion.11
  14.2 6.8 %all-to-all-done.1 = bf16[16,128,64]{1,2,0:T(8,128)(2,1)S(1)} async-done(((bf16[16,128,64]{1,2,0:T(8,128)(2,1)}), bf16[16,128,64]{1,2,0:T(8,128)(2,1)S(1)}, u32[]{:S(2)}, u32[]{:S(2)}) %all-to-all-start.1) | async-done | bytes 262176 | tf_op jit(solution)/shard_map/all_to_all | solution.py:66
  21.1 0.9 broadcast_in_dim.20
  22.0 4.1 %all-to-all-start = ((bf16[8,768,64]{1,2,0:T(8,128)(2,1)}), bf16[8,768,64]{1,2,0:T(8,128)(2,1)S(1)}, u32[]{:S(2)}, u32[]{:S(2)}) async-start(bf16[8,768,64]{1,2,0:T(8,128)(2,1)} %broadcast_in_dim.20), calls=%async_computation | async-start | bytes 1572864 | tf_op jit(solution)/shard_map/all_to_all | solution.py:66
  26.1 0.1 reduce_max.128
  26.3 0.1 pad.20.clone
  26.5 0.2 copy.12
  26.6 0.1 reshape.162
  26.8 12.4 %all-to-all-done = bf16[8,768,64]{1,2,0:T(8,128)(2,1)S(1)} async-done(((bf16[8,768,64]{1,2,0:T(8,128)(2,1)}), bf16[8,768,64]{1,2,0:T(8,128)(2,1)S(1)}, u32[]{:S(2)}, u32[]{:S(2)}) %all-to-all-start) | async-done | bytes 786464 | tf_op jit(solution)/shard_map/all_to_all | solution.py:66
  39.2 1.5 broadcast_in_dim.22
  40.7 3.6 %all-to-all-start.2 = ((bf16[8,784,128]{2,1,0:T(8,128)(2,1)}), bf16[8,784,128]{2,1,0:T(8,128)(2,1)S(1)}, u32[]{:S(2)}, u32[]{:S(2)}) async-start(bf16[8,784,128]{2,1,0:T(8,128)(2,1)} %broadcast_in_dim.22), calls=%async_computation.2 | async-start | bytes 3211264 | tf_op jit(solution)/shard_map/all_to_all | solution.py:66
  44.2 12.4 %exponential_convert_fusion = bf16[8,768,2048]{2,1,0:T(8,128)(2,1)} fusion(bf16[8,768,64]{1,2,0:T(8,128)(2,1)S(1)} %all-to-all-done, bf16[2048,64,1]{0,1,2:T(8,128)(2,1)S(1)} %reshape.162), kind=kOutput, calls=%fused_computation | convolution fusion | flops 1648361472 | bytes 26214400 | tf_op jit(solution)/shard_map/id,sjd->sij/dot_general | solution.py:93
  56.6 9.4 %all-to-all-done.2 = bf16[8,784,128]{2,1,0:T(8,128)(2,1)S(1)} async-done(((bf16[8,784,128]{2,1,0:T(8,128)(2,1)}), bf16[8,784,128]{2,1,0:T(8,128)(2,1)S(1)}, u32[]{:S(2)}, u32[]{:S(2)}) %all-to-all-start.2) | async-done | bytes 1605664 | tf_op jit(solution)/shard_map/all_to_all | solution.py:66
  66.1 13.5 %multiply_reduce_fusion.1 = f32[2048,128]{1,0:T(8,128)S(1)} fusion(f32[8,128]{1,0:T(8,128)S(1)} %bitcast.55, bf16[8,768,2048]{2,1,0:T(8,128)(2,1)} %exponential_convert_fusion, bf16[8,784,128]{2,1,0:T(8,128)(2,1)S(1)} %all-to-all-done.2), kind=kOutput, calls=%fused_computation.6 | convolution fusion | flops 3225157632 | bytes 27791360 | tf_op jit(solution)/shard_map/sij,sjc->sic/dot_general | solution.py:118
  79.6 0.1 maximum_maximum_fusion.2
  79.7 22.6 %all_to_all.50 = f32[16,136,128]{2,1,0:T(8,128)S(1)} all-to-all(f32[16,136,128]{2,1,0:T(8,128)S(1)} %maximum_maximum_fusion.2), channel_id=1, replica_groups=mesh['blk'=8,'dom'=16] {'dom'}, dimensions={0} | all-to-all | bytes 2228224 | tf_op jit(solution)/shard_map/all_to_all | solution.py:125
  102.4 0.1 fusion.9
  102.6 0.9 broadcast_in_dim.24
  103.5 3.8 %all-to-all-start.4 = ((bf16[16,144,128]{2,1,0:T(8,128)(2,1)}), bf16[16,144,128]{2,1,0:T(8,128)(2,1)S(1)}, u32[]{:S(2)}, u32[]{:S(2)}) async-start(bf16[16,144,128]{2,1,0:T(8,128)(2,1)} %broadcast_in_dim.24), calls=%async_computation.4 | async-start | bytes 1179648 | tf_op jit(solution)/shard_map/all_to_all | solution.py:66
  107.3 0.1 pad.14.clone
  107.4 11.9 %all-to-all-done.4 = bf16[16,144,128]{2,1,0:T(8,128)(2,1)S(1)} async-done(((bf16[16,144,128]{2,1,0:T(8,128)(2,1)}), bf16[16,144,128]{2,1,0:T(8,128)(2,1)S(1)}, u32[]{:S(2)}, u32[]{:S(2)}) %all-to-all-start.4) | async-done | bytes 589856 | tf_op jit(solution)/shard_map/all_to_all | solution.py:66
  119.4 0.1 multiply_convert_fusion.1
  119.5 11.7 %fusion.2 = f32[8,768,128]{2,1,0:T(8,128)S(1)} fusion(bf16[2048,128,1]{1,0,2:T(8,128)(2,1)S(1)} %bitcast.46, bf16[8,768,2048]{2,1,0:T(8,128)(2,1)} %exponential_convert_fusion), kind=kOutput, calls=%fused_computation.3 | convolution fusion | flops 3221225472 | bytes 28835840 | tf_op jit(solution)/shard_map/ic,sij->sjc/dot_general | solution.py:143
  131.2 0.3 maximum_maximum_fusion
  131.5 39.7 %all_to_all.51 = f32[8,776,128]{2,1,0:T(8,128)S(1)} all-to-all(f32[8,776,128]{2,1,0:T(8,128)S(1)} %maximum_maximum_fusion), channel_id=1, replica_groups=mesh['blk'=8,'dom'=16] {'blk'}, dimensions={0} | all-to-all | bytes 6356992 | tf_op jit(solution)/shard_map/all_to_all | solution.py:150
  171.3 0.2 fusion.5
  171.5 0.7 copy-done
  172.3 0.2 fusion.12
  172.4 0.2 exponential_convert_fusion.1
  172.6 0.2 broadcast_in_dim.26
  172.9 21.8 %all_to_all.52 = bf16[8,784,128]{2,1,0:T(8,128)(2,1)S(1)} all-to-all(bf16[8,784,128]{2,1,0:T(8,128)(2,1)S(1)} %broadcast_in_dim.26), channel_id=1, replica_groups=mesh['blk'=8,'dom'=16] {'blk'}, dimensions={0} | all-to-all | bytes 3211264 | tf_op jit(solution)/shard_map/all_to_all | solution.py:66
  194.8 13.5 %multiply_reduce_fusion = f32[2048,128]{1,0:T(8,128)S(1)} fusion(f32[8,128]{1,0:T(8,128)S(1)} %bitcast.56, bf16[8,768,2048]{2,1,0:T(8,128)(2,1)} %exponential_convert_fusion, bf16[8,784,128]{2,1,0:T(8,128)(2,1)S(1)} %all_to_all.52), kind=kOutput, calls=%fused_computation.5 | convolution fusion | flops 3225157632 | bytes 27791360 | tf_op jit(solution)/shard_map/sij,sjc->sic/dot_general | solution.py:118
  208.3 0.1 maximum_maximum_fusion.3
  208.4 27.0 %all_to_all.53 = f32[16,136,128]{2,1,0:T(8,128)S(1)} all-to-all(f32[16,136,128]{2,1,0:T(8,128)S(1)} %maximum_maximum_fusion.3), channel_id=1, replica_groups=mesh['blk'=8,'dom'=16] {'dom'}, dimensions={0} | all-to-all | bytes 2228224 | tf_op jit(solution)/shard_map/all_to_all | solution.py:125
  235.5 0.1 fusion.8
  235.7 0.1 broadcast_in_dim.28
  235.8 15.6 %all_to_all.54 = bf16[16,144,128]{2,1,0:T(8,128)(2,1)S(1)} all-to-all(bf16[16,144,128]{2,1,0:T(8,128)(2,1)S(1)} %broadcast_in_dim.28), channel_id=1, replica_groups=mesh['blk'=8,'dom'=16] {'dom'}, dimensions={0} | all-to-all | bytes 1179648 | tf_op jit(solution)/shard_map/all_to_all | solution.py:66
  251.5 0.1 multiply_convert_fusion
  251.6 11.7 %fusion = f32[8,768,128]{2,1,0:T(8,128)S(1)} fusion(bf16[2048,128,1]{1,0,2:T(8,128)(2,1)S(1)} %bitcast.45, bf16[8,768,2048]{2,1,0:T(8,128)(2,1)} %exponential_convert_fusion), kind=kOutput, calls=%fused_computation.1 | convolution fusion | flops 3221225472 | bytes 28835840 | tf_op jit(solution)/shard_map/ic,sij->sjc/dot_general | solution.py:143
  263.3 0.3 maximum_maximum_fusion.1
  263.6 41.0 %all_to_all.55 = f32[8,776,128]{2,1,0:T(8,128)S(1)} all-to-all(f32[8,776,128]{2,1,0:T(8,128)S(1)} %maximum_maximum_fusion.1), channel_id=1, replica_groups=mesh['blk'=8,'dom'=16] {'blk'}, dimensions={0} | all-to-all | bytes 6356992 | tf_op jit(solution)/shard_map/all_to_all | solution.py:150
  304.7 0.2 fusion.4
  304.9 0.9 log_subtract_fusion
  (50 shorter events, 0.8 us)
Async XLA Ops:
  0.6 25.5 %copy-start.1 = (f32[768,128]{1,0:T(8,128)S(1)}, f32[768,128]{1,0:T(8,128)}, u32[]{:S(2)}) copy-start(f32[768,128]{1,0:T(8,128)} %param.9) | copy-start | bytes 1179652
  2.9 18.1 %all-to-all-start.1 = ((bf16[16,128,64]{1,2,0:T(8,128)(2,1)}), bf16[16,128,64]{1,2,0:T(8,128)(2,1)S(1)}, u32[]{:S(2)}, u32[]{:S(2)}) async-start(bf16[16,128,64]{1,2,0:T(8,128)(2,1)} %broadcast_in_dim.21), calls=%async_computation.1 | async-start | bytes 524288 | tf_op jit(solution)/shard_map/all_to_all | solution.py:66
  22.0 17.2 %all-to-all-start = ((bf16[8,768,64]{1,2,0:T(8,128)(2,1)}), bf16[8,768,64]{1,2,0:T(8,128)(2,1)S(1)}, u32[]{:S(2)}, u32[]{:S(2)}) async-start(bf16[8,768,64]{1,2,0:T(8,128)(2,1)} %broadcast_in_dim.20), calls=%async_computation | async-start | bytes 1572864 | tf_op jit(solution)/shard_map/all_to_all | solution.py:66
  40.7 25.4 %all-to-all-start.2 = ((bf16[8,784,128]{2,1,0:T(8,128)(2,1)}), bf16[8,784,128]{2,1,0:T(8,128)(2,1)S(1)}, u32[]{:S(2)}, u32[]{:S(2)}) async-start(bf16[8,784,128]{2,1,0:T(8,128)(2,1)} %broadcast_in_dim.22), calls=%async_computation.2 | async-start | bytes 3211264 | tf_op jit(solution)/shard_map/all_to_all | solution.py:66
  79.6 22.9 %copy-start.2 = (s32[128,128]{1,0:T(8,128)S(1)}, s32[128,128]{1,0:T(8,128)}, u32[]{:S(2)}) copy-start(s32[128,128]{1,0:T(8,128)} %param.7) | copy-start | bytes 196612
  103.5 15.8 %all-to-all-start.4 = ((bf16[16,144,128]{2,1,0:T(8,128)(2,1)}), bf16[16,144,128]{2,1,0:T(8,128)(2,1)S(1)}, u32[]{:S(2)}, u32[]{:S(2)}) async-start(bf16[16,144,128]{2,1,0:T(8,128)(2,1)} %broadcast_in_dim.24), calls=%async_computation.4 | async-start | bytes 1179648 | tf_op jit(solution)/shard_map/all_to_all | solution.py:66
  171.3 1.0 copy-start
  235.6 27.7 %copy-start.3 = (f32[128,128]{1,0:T(8,128)}, f32[128,128]{1,0:T(8,128)S(1)}, u32[]{:S(2)}) copy-start(f32[128,128]{1,0:T(8,128)S(1)} %get-tuple-element.3) | copy-start | bytes 196612

commit v7 on v6

--- a/solution.py
+++ b/solution.py
@@ -110,7 +110,10 @@
         payload = jnp.concatenate(
             [weights, shift.astype(jnp.bfloat16)[None, :],
              jnp.zeros((tgt_payload_rows - tgt_rows - 1, columns), jnp.bfloat16)], axis=0)
-        gathered = copy_gather(payload, "blk", blk_count)
+        if iteration == 0:
+            gathered = lax.all_gather(payload, "blk", axis=0, tiled=False)
+        else:
+            gathered = copy_gather(payload, "blk", blk_count)
         weight_segments = gathered[:, :tgt_rows, :]
         segment_shift = gathered[:, tgt_rows, :].astype(jnp.float32)
         group_shift = jnp.max(segment_shift, axis=0)

time: 307 us -> 316 us (1.029)
  between operations: 0.96 us -> 14.3 us
  other arithmetic: 7.15 us -> 11.2 us
  waiting for transfers between devices: 40.6 us -> 37.1 us
  starting transfers between devices: 21 us -> 17.6 us
    all_to_all x4 -> x3, waiting for transfers between devices: 40.6 us -> 37.1 us  [copy_gather(): lax.all_to_all(jnp.broadcast_to(value[None], (count,) + value.shape), axi...]
    all_to_all x4 -> x3, starting transfers between devices: 21 us -> 17.6 us  [copy_gather(): lax.all_to_all(jnp.broadcast_to(value[None], (count,) + value.shape), axi...]
  transfers between devices with their start and end apart: 4 -> 4, of which waited for: 4 -> 3; matrix products, arithmetic and copies ran while one was open for 5% -> 6% of each run, Pallas kernels for 0% -> 0%
where the time goes in v7:
time: 316 us; the launch traced here: 315 us
  blocking collectives  169 us (53%)
  matrix products  62 us (20%)
  waiting for transfers between devices  37.1 us (12%)
  starting transfers between devices  17.6 us (6%)
  between operations  14.3 us (5%)
  other arithmetic  11.2 us (4%)
  local copies, waits for them, and re-layouts  4.14 us (1%)
    all_to_all x2, blocking collectives, body(): received = lax.all_to_all(pieces, 'blk', 0, 0, tiled=False)  81.2 us
    all_to_all x2, blocking collectives, body(): received = lax.all_to_all(pieces, 'dom', 0, 0, tiled=False)  50.3 us
    all_to_all x2, blocking collectives, copy_gather(): lax.all_to_all(jnp.broadcast_to(value[None], (count,) + value.shape), axi...  37.5 us
    all_to_all x3, waiting for transfers between devices, copy_gather(): lax.all_to_all(jnp.broadcast_to(value[None], (count,) + value.shape), axi...  37.1 us
    dot_general x2, matrix products, body(): jnp.einsum('sij,sjc->sic', kernel, weight_segments, preferred_element_typ...  26.4 us
    dot_general x2, matrix products, body(): jnp.einsum('ic,sij->sjc', source_weights, kernel, preferred_element_type=...  23.3 us
    all_to_all x3, starting transfers between devices, copy_gather(): lax.all_to_all(jnp.broadcast_to(value[None], (count,) + value.shape), axi...  17.6 us
    dot_general x1, matrix products, body(): jnp.einsum('id,sjd->sij', source_block, target_group.reshape(blk_count, t...  12.4 us
  transfers between devices with their start and end apart: 4, of which 3 were waited for; matrix products, arithmetic and copies ran while one was open for 6% of the time, Pallas kernels for 0%

profile of v7, /device:TPU:1, one launch (start us, length us, event | category | flops | bytes accessed | tf_op | source)
XLA Modules:
  0.0 315.4 jit_solution(15276106703707761222)
XLA Ops:
  7.2 1.1 reduce_max.128
  8.3 1.1 exponential_convert_fusion.2
  9.4 0.7 pad_maximum_fusion.1
  10.1 0.7 fusion.13
  10.9 0.7 fusion.14
  11.6 0.8 broadcast_in_dim.19
  12.4 9.4 %all-to-all-start.1 = ((bf16[16,128,64]{1,2,0:T(8,128)(2,1)}), bf16[16,128,64]{1,2,0:T(8,128)(2,1)S(1)}, u32[]{:S(2)}, u32[]{:S(2)}) async-start(bf16[16,128,64]{1,2,0:T(8,128)(2,1)} %broadcast_in_dim.19), calls=%async_computation.1 | async-start | bytes 524288 | tf_op jit(solution)/shard_map/all_to_all | solution.py:66
  21.8 0.9 fusion.10
  22.8 0.9 fusion.11
  23.7 9.2 %all-to-all-done.1 = bf16[16,128,64]{1,2,0:T(8,128)(2,1)S(1)} async-done(((bf16[16,128,64]{1,2,0:T(8,128)(2,1)}), bf16[16,128,64]{1,2,0:T(8,128)(2,1)S(1)}, u32[]{:S(2)}, u32[]{:S(2)}) %all-to-all-start.1) | async-done | bytes 262176 | tf_op jit(solution)/shard_map/all_to_all | solution.py:66
  32.9 0.9 broadcast_in_dim.18
  33.9 4.3 %all-to-all-start = ((bf16[8,768,64]{1,2,0:T(8,128)(2,1)}), bf16[8,768,64]{1,2,0:T(8,128)(2,1)S(1)}, u32[]{:S(2)}, u32[]{:S(2)}) async-start(bf16[8,768,64]{1,2,0:T(8,128)(2,1)} %broadcast_in_dim.18), calls=%async_computation | async-start | bytes 1572864 | tf_op jit(solution)/shard_map/all_to_all | solution.py:66
  38.2 0.1 pad.20.clone
  38.3 0.2 copy.12
  38.4 0.1 reshape.162
  38.6 15.9 %all-to-all-done = bf16[8,768,64]{1,2,0:T(8,128)(2,1)S(1)} async-done(((bf16[8,768,64]{1,2,0:T(8,128)(2,1)}), bf16[8,768,64]{1,2,0:T(8,128)(2,1)S(1)}, u32[]{:S(2)}, u32[]{:S(2)}) %all-to-all-start) | async-done | bytes 786464 | tf_op jit(solution)/shard_map/all_to_all | solution.py:66
  54.5 12.4 %exponential_convert_fusion = bf16[8,768,2048]{2,1,0:T(8,128)(2,1)} fusion(bf16[8,768,64]{1,2,0:T(8,128)(2,1)S(1)} %all-to-all-done, bf16[2048,64,1]{0,1,2:T(8,128)(2,1)S(1)} %reshape.162), kind=kOutput, calls=%fused_computation | convolution fusion | flops 1648361472 | bytes 26214400 | tf_op jit(solution)/shard_map/id,sjd->sij/dot_general | solution.py:93
  66.9 0.7 slice_reduce_fusion.5
  67.6 0.7 subtract_exponential_fusion.7
  68.4 12.9 %multiply_reduce_fusion.1 = f32[2048,128]{1,0:T(8,128)S(1)} fusion(f32[8,128]{1,0:T(8,128)S(1)} %bitcast.56, bf16[8,768,2048]{2,1,0:T(8,128)(2,1)} %exponential_convert_fusion, bf16[8,784,128]{2,1,0:T(8,128)(2,1)} %bitcast.64), kind=kOutput, calls=%fused_computation.6 | convolution fusion | flops 3225157632 | bytes 27791360 | tf_op jit(solution)/shard_map/sij,sjc->sic/dot_general | solution.py:121
  81.3 0.1 maximum_maximum_fusion.2
  81.5 23.5 %all_to_all.45 = f32[16,136,128]{2,1,0:T(8,128)S(1)} all-to-all(f32[16,136,128]{2,1,0:T(8,128)S(1)} %maximum_maximum_fusion.2), channel_id=1, replica_groups=mesh['blk'=8,'dom'=16] {'dom'}, dimensions={0} | all-to-all | bytes 2228224 | tf_op jit(solution)/shard_map/all_to_all | solution.py:128
  105.0 0.1 fusion.9
  105.2 0.9 broadcast_in_dim.21
  106.2 3.8 %all-to-all-start.3 = ((bf16[16,144,128]{2,1,0:T(8,128)(2,1)}), bf16[16,144,128]{2,1,0:T(8,128)(2,1)S(1)}, u32[]{:S(2)}, u32[]{:S(2)}) async-start(bf16[16,144,128]{2,1,0:T(8,128)(2,1)} %broadcast_in_dim.21), calls=%async_computation.3 | async-start | bytes 1179648 | tf_op jit(solution)/shard_map/all_to_all | solution.py:66
  110.0 11.9 %all-to-all-done.3 = bf16[16,144,128]{2,1,0:T(8,128)(2,1)S(1)} async-done(((bf16[16,144,128]{2,1,0:T(8,128)(2,1)}), bf16[16,144,128]{2,1,0:T(8,128)(2,1)S(1)}, u32[]{:S(2)}, u32[]{:S(2)}) %all-to-all-start.3) | async-done | bytes 589856 | tf_op jit(solution)/shard_map/all_to_all | solution.py:66
  122.0 0.1 multiply_convert_fusion.1
  122.1 11.6 %fusion.2 = f32[8,768,128]{2,1,0:T(8,128)S(1)} fusion(bf16[2048,128,1]{1,0,2:T(8,128)(2,1)S(1)} %bitcast.47, bf16[8,768,2048]{2,1,0:T(8,128)(2,1)} %exponential_convert_fusion), kind=kOutput, calls=%fused_computation.3 | convolution fusion | flops 3221225472 | bytes 28835840 | tf_op jit(solution)/shard_map/ic,sij->sjc/dot_general | solution.py:146
  133.8 0.3 maximum_maximum_fusion
  134.1 40.2 %all_to_all.46 = f32[8,776,128]{2,1,0:T(8,128)S(1)} all-to-all(f32[8,776,128]{2,1,0:T(8,128)S(1)} %maximum_maximum_fusion), channel_id=1, replica_groups=mesh['blk'=8,'dom'=16] {'blk'}, dimensions={0} | all-to-all | bytes 6356992 | tf_op jit(solution)/shard_map/all_to_all | solution.py:153
  174.3 0.2 fusion.5
  174.5 0.7 copy-done
  175.3 0.2 fusion.12
  175.4 0.2 exponential_convert_fusion.1
  175.6 0.2 broadcast_in_dim.23
  175.9 21.8 %all_to_all.47 = bf16[8,784,128]{2,1,0:T(8,128)(2,1)S(1)} all-to-all(bf16[8,784,128]{2,1,0:T(8,128)(2,1)S(1)} %broadcast_in_dim.23), channel_id=1, replica_groups=mesh['blk'=8,'dom'=16] {'blk'}, dimensions={0} | all-to-all | bytes 3211264 | tf_op jit(solution)/shard_map/all_to_all | solution.py:66
  197.7 13.5 %multiply_reduce_fusion = f32[2048,128]{1,0:T(8,128)S(1)} fusion(f32[8,128]{1,0:T(8,128)S(1)} %bitcast.57, bf16[8,768,2048]{2,1,0:T(8,128)(2,1)} %exponential_convert_fusion, bf16[8,784,128]{2,1,0:T(8,128)(2,1)S(1)} %all_to_all.47), kind=kOutput, calls=%fused_computation.5 | convolution fusion | flops 3225157632 | bytes 27791360 | tf_op jit(solution)/shard_map/sij,sjc->sic/dot_general | solution.py:121
  211.2 0.1 maximum_maximum_fusion.3
  211.4 26.8 %all_to_all.48 = f32[16,136,128]{2,1,0:T(8,128)S(1)} all-to-all(f32[16,136,128]{2,1,0:T(8,128)S(1)} %maximum_maximum_fusion.3), channel_id=1, replica_groups=mesh['blk'=8,'dom'=16] {'dom'}, dimensions={0} | all-to-all | bytes 2228224 | tf_op jit(solution)/shard_map/all_to_all | solution.py:128
  238.2 0.1 fusion.8
  238.4 0.1 broadcast_in_dim.25
  238.5 15.6 %all_to_all.49 = bf16[16,144,128]{2,1,0:T(8,128)(2,1)S(1)} all-to-all(bf16[16,144,128]{2,1,0:T(8,128)(2,1)S(1)} %broadcast_in_dim.25), channel_id=1, replica_groups=mesh['blk'=8,'dom'=16] {'dom'}, dimensions={0} | all-to-all | bytes 1179648 | tf_op jit(solution)/shard_map/all_to_all | solution.py:66
  254.2 0.1 multiply_convert_fusion
  254.4 11.6 %fusion = f32[8,768,128]{2,1,0:T(8,128)S(1)} fusion(bf16[2048,128,1]{1,0,2:T(8,128)(2,1)S(1)} %bitcast.46, bf16[8,768,2048]{2,1,0:T(8,128)(2,1)} %exponential_convert_fusion), kind=kOutput, calls=%fused_computation.1 | convolution fusion | flops 3221225472 | bytes 28835840 | tf_op jit(solution)/shard_map/ic,sij->sjc/dot_general | solution.py:146
  266.1 0.3 maximum_maximum_fusion.1
  266.3 41.0 %all_to_all.50 = f32[8,776,128]{2,1,0:T(8,128)S(1)} all-to-all(f32[8,776,128]{2,1,0:T(8,128)S(1)} %maximum_maximum_fusion.1), channel_id=1, replica_groups=mesh['blk'=8,'dom'=16] {'blk'}, dimensions={0} | all-to-all | bytes 6356992 | tf_op jit(solution)/shard_map/all_to_all | solution.py:153
  307.4 0.2 fusion.4
  307.6 0.9 log_subtract_fusion
  (48 shorter events, 0.8 us)
Async XLA Ops:
  7.2 59.7 %all-gather.3.cloned.1.call-start = ((), (), s32[]{:S(2)}) async-start(), calls=%async_computation.9 | async-start | bytes 1806336 | tf_op jit(solution)/shard_map/all_gather | solution.py:114
  12.4 20.6 %all-to-all-start.1 = ((bf16[16,128,64]{1,2,0:T(8,128)(2,1)}), bf16[16,128,64]{1,2,0:T(8,128)(2,1)S(1)}, u32[]{:S(2)}, u32[]{:S(2)}) async-start(bf16[16,128,64]{1,2,0:T(8,128)(2,1)} %broadcast_in_dim.19), calls=%async_computation.1 | async-start | bytes 524288 | tf_op jit(solution)/shard_map/all_to_all | solution.py:66
  33.9 20.7 %all-to-all-start = ((bf16[8,768,64]{1,2,0:T(8,128)(2,1)}), bf16[8,768,64]{1,2,0:T(8,128)(2,1)S(1)}, u32[]{:S(2)}, u32[]{:S(2)}) async-start(bf16[8,768,64]{1,2,0:T(8,128)(2,1)} %broadcast_in_dim.18), calls=%async_computation | async-start | bytes 1572864 | tf_op jit(solution)/shard_map/all_to_all | solution.py:66
  81.3 23.8 %copy-start.1 = (s32[128,128]{1,0:T(8,128)S(1)}, s32[128,128]{1,0:T(8,128)}, u32[]{:S(2)}) copy-start(s32[128,128]{1,0:T(8,128)} %param.7) | copy-start | bytes 196612
  106.2 15.8 %all-to-all-start.3 = ((bf16[16,144,128]{2,1,0:T(8,128)(2,1)}), bf16[16,144,128]{2,1,0:T(8,128)(2,1)S(1)}, u32[]{:S(2)}, u32[]{:S(2)}) async-start(bf16[16,144,128]{2,1,0:T(8,128)(2,1)} %broadcast_in_dim.21), calls=%async_computation.3 | async-start | bytes 1179648 | tf_op jit(solution)/shard_map/all_to_all | solution.py:66
  174.3 1.0 copy-start
  238.4 27.6 %copy-start.2 = (f32[128,128]{1,0:T(8,128)}, f32[128,128]{1,0:T(8,128)S(1)}, u32[]{:S(2)}) copy-start(f32[128,128]{1,0:T(8,128)S(1)} %get-tuple-element.3) | copy-start | bytes 196612
Sparse Core Ops, SparseCore 0:
  10.2 44.1 all-gather.2

commit v8 on v6

--- a/solution.py
+++ b/solution.py
@@ -121,8 +121,8 @@
         pieces = jnp.concatenate(
             [partial_value.reshape(dom_count, src_rows, columns),
              jnp.broadcast_to(group_shift[None, None, :], (dom_count, 1, columns)),
-             jnp.zeros((dom_count, src_piece_rows - src_rows - 1, columns), jnp.float32)], axis=1)
-        received = lax.all_to_all(pieces, "dom", 0, 0, tiled=False)
+             jnp.zeros((dom_count, src_payload_rows - src_rows - 1, columns), jnp.float32)], axis=1)
+        received = lax.all_to_all(pieces.astype(jnp.bfloat16), "dom", 0, 0, tiled=False).astype(jnp.float32)
         group_shifts = received[:, src_rows, :]
         target_peak = jnp.max(group_shifts, axis=0)
         scale = jnp.exp(group_shifts - target_peak[None, :])
@@ -146,8 +146,8 @@
         pieces = jnp.concatenate(
             [target_partial.reshape(blk_count, tgt_rows, columns),
              jnp.broadcast_to(block_peak[None, None, :], (blk_count, 1, columns)),
-             jnp.zeros((blk_count, tgt_piece_rows - tgt_rows - 1, columns), jnp.float32)], axis=1)
-        received = lax.all_to_all(pieces, "blk", 0, 0, tiled=False)
+             jnp.zeros((blk_count, tgt_payload_rows - tgt_rows - 1, columns), jnp.float32)], axis=1)
+        received = lax.all_to_all(pieces.astype(jnp.bfloat16), "blk", 0, 0, tiled=False).astype(jnp.float32)
         block_peaks = received[:, tgt_rows, :]
         source_peak = jnp.max(block_peaks, axis=0)
         scale = jnp.exp(block_peaks - source_peak[None, :])

time: 307 us -> 262 us (0.85)
  blocking collectives: 168 us -> 123 us
    all_to_all x4, blocking collectives: 130 us -> 85.2 us  [the longest x2 47 us: body(): lax.all_to_all(pieces.astype(jnp.bfloat16), 'blk', 0, 0, tiled=False)]
  transfers between devices with their start and end apart: 4 -> 4, of which waited for: 4 -> 4; matrix products, arithmetic and copies ran while one was open for 5% -> 6% of each run, Pallas kernels for 0% -> 0%
where the time goes in v8:
time: 262 us
  blocking collectives  123 us (47%)
  matrix products  63 us (24%)
  waiting for transfers between devices  40.5 us (15%)
  starting transfers between devices  21 us (8%)
  other arithmetic  8.02 us (3%)
  local copies, waits for them, and re-layouts  5.39 us (2%)
    all_to_all x2, blocking collectives, body(): lax.all_to_all(pieces.astype(jnp.bfloat16), 'blk', 0, 0, tiled=False)  47 us
    all_to_all x4, waiting for transfers between devices, copy_gather(): lax.all_to_all(jnp.broadcast_to(value[None], (count,) + value.shape), axi...  40.5 us
    all_to_all x2, blocking collectives, body(): lax.all_to_all(pieces.astype(jnp.bfloat16), 'dom', 0, 0, tiled=False)  38.2 us
    all_to_all x2, blocking collectives, copy_gather(): lax.all_to_all(jnp.broadcast_to(value[None], (count,) + value.shape), axi...  37.5 us
    dot_general x2, matrix products, body(): jnp.einsum('sij,sjc->sic', kernel, weight_segments, preferred_element_typ...  27 us
    dot_general x2, matrix products, body(): jnp.einsum('ic,sij->sjc', source_weights, kernel, preferred_element_type=...  23.5 us
    all_to_all x4, starting transfers between devices, copy_gather(): lax.all_to_all(jnp.broadcast_to(value[None], (count,) + value.shape), axi...  21 us
    dot_general x1, matrix products, body(): jnp.einsum('id,sjd->sij', source_block, target_group.reshape(blk_count, t...  12.4 us
  transfers between devices with their start and end apart: 4, of which 4 were waited for; matrix products, arithmetic and copies ran while one was open for 6% of the time, Pallas kernels for 0%

profile of v8, /device:TPU:1, one launch (start us, length us, event | category | flops | bytes accessed | tf_op | source)
XLA Modules:
  0.0 261.5 jit_solution(15308275974054498994)
XLA Ops:
  0.6 0.8 fusion.19
  1.4 0.7 fusion.20
  2.2 0.8 broadcast_in_dim.21
  2.9 9.4 %all-to-all-start.1 = ((bf16[16,128,64]{1,2,0:T(8,128)(2,1)}), bf16[16,128,64]{1,2,0:T(8,128)(2,1)S(1)}, u32[]{:S(2)}, u32[]{:S(2)}) async-start(bf16[16,128,64]{1,2,0:T(8,128)(2,1)} %broadcast_in_dim.21), calls=%async_computation.1 | async-start | bytes 524288 | tf_op jit(solution)/shard_map/all_to_all | solution.py:66
  12.4 0.9 fusion.16
  13.3 0.9 fusion.17
  14.2 6.8 %all-to-all-done.1 = bf16[16,128,64]{1,2,0:T(8,128)(2,1)S(1)} async-done(((bf16[16,128,64]{1,2,0:T(8,128)(2,1)}), bf16[16,128,64]{1,2,0:T(8,128)(2,1)S(1)}, u32[]{:S(2)}, u32[]{:S(2)}) %all-to-all-start.1) | async-done | bytes 262176 | tf_op jit(solution)/shard_map/all_to_all | solution.py:66
  21.1 0.9 broadcast_in_dim.20
  22.0 4.1 %all-to-all-start = ((bf16[8,768,64]{1,2,0:T(8,128)(2,1)}), bf16[8,768,64]{1,2,0:T(8,128)(2,1)S(1)}, u32[]{:S(2)}, u32[]{:S(2)}) async-start(bf16[8,768,64]{1,2,0:T(8,128)(2,1)} %broadcast_in_dim.20), calls=%async_computation | async-start | bytes 1572864 | tf_op jit(solution)/shard_map/all_to_all | solution.py:66
  26.1 0.1 reduce_max.128
  26.5 0.2 copy.12
  26.6 0.1 reshape.164
  26.8 12.4 %all-to-all-done = bf16[8,768,64]{1,2,0:T(8,128)(2,1)S(1)} async-done(((bf16[8,768,64]{1,2,0:T(8,128)(2,1)}), bf16[8,768,64]{1,2,0:T(8,128)(2,1)S(1)}, u32[]{:S(2)}, u32[]{:S(2)}) %all-to-all-start) | async-done | bytes 786464 | tf_op jit(solution)/shard_map/all_to_all | solution.py:66
  39.2 1.5 broadcast_in_dim.22
  40.7 3.6 %all-to-all-start.2 = ((bf16[8,784,128]{2,1,0:T(8,128)(2,1)}), bf16[8,784,128]{2,1,0:T(8,128)(2,1)S(1)}, u32[]{:S(2)}, u32[]{:S(2)}) async-start(bf16[8,784,128]{2,1,0:T(8,128)(2,1)} %broadcast_in_dim.22), calls=%async_computation.2 | async-start | bytes 3211264 | tf_op jit(solution)/shard_map/all_to_all | solution.py:66
  44.2 12.4 %exponential_convert_fusion = bf16[8,768,2048]{2,1,0:T(8,128)(2,1)} fusion(bf16[8,768,64]{1,2,0:T(8,128)(2,1)S(1)} %all-to-all-done, bf16[2048,64,1]{0,1,2:T(8,128)(2,1)S(1)} %reshape.164), kind=kOutput, calls=%fused_computation | convolution fusion | flops 1648361472 | bytes 26214400 | tf_op jit(solution)/shard_map/id,sjd->sij/dot_general | solution.py:93
  56.6 9.4 %all-to-all-done.2 = bf16[8,784,128]{2,1,0:T(8,128)(2,1)S(1)} async-done(((bf16[8,784,128]{2,1,0:T(8,128)(2,1)}), bf16[8,784,128]{2,1,0:T(8,128)(2,1)S(1)}, u32[]{:S(2)}, u32[]{:S(2)}) %all-to-all-start.2) | async-done | bytes 1605664 | tf_op jit(solution)/shard_map/all_to_all | solution.py:66
  66.1 13.5 %multiply_reduce_fusion.1 = bf16[2048,128]{1,0:T(8,128)(2,1)S(1)} fusion(f32[8,128]{1,0:T(8,128)S(1)} %bitcast.59, bf16[8,768,2048]{2,1,0:T(8,128)(2,1)} %exponential_convert_fusion, bf16[8,784,128]{2,1,0:T(8,128)(2,1)S(1)} %all-to-all-done.2), kind=kOutput, calls=%fused_computation.6 | convolution fusion | flops 3225157632 | bytes 27267072 | tf_op jit(solution)/shard_map/sij,sjc->sic/dot_general | solution.py:118
  79.6 0.2 maximum_maximum_fusion.2
  79.8 17.0 %all_to_all.50 = bf16[16,144,128]{2,1,0:T(8,128)(2,1)S(1)} all-to-all(bf16[16,144,128]{2,1,0:T(8,128)(2,1)S(1)} %maximum_maximum_fusion.2), channel_id=1, replica_groups=mesh['blk'=8,'dom'=16] {'dom'}, dimensions={0} | all-to-all | bytes 1179648 | tf_op jit(solution)/shard_map/all_to_all | solution.py:125
  96.9 0.1 fusion.15
  97.1 0.9 broadcast_in_dim.24
  98.1 3.8 %all-to-all-start.4 = ((bf16[16,144,128]{2,1,0:T(8,128)(2,1)}), bf16[16,144,128]{2,1,0:T(8,128)(2,1)S(1)}, u32[]{:S(2)}, u32[]{:S(2)}) async-start(bf16[16,144,128]{2,1,0:T(8,128)(2,1)} %broadcast_in_dim.24), calls=%async_computation.4 | async-start | bytes 1179648 | tf_op jit(solution)/shard_map/all_to_all | solution.py:66
  102.0 11.9 %all-to-all-done.4 = bf16[16,144,128]{2,1,0:T(8,128)(2,1)S(1)} async-done(((bf16[16,144,128]{2,1,0:T(8,128)(2,1)}), bf16[16,144,128]{2,1,0:T(8,128)(2,1)S(1)}, u32[]{:S(2)}, u32[]{:S(2)}) %all-to-all-start.4) | async-done | bytes 589856 | tf_op jit(solution)/shard_map/all_to_all | solution.py:66
  113.9 0.1 multiply_convert_fusion.1
  114.1 11.8 %fusion.6 = bf16[8,768,128]{2,1,0:T(8,128)(2,1)S(1)} fusion(bf16[2048,128,1]{1,0,2:T(8,128)(2,1)S(1)} %bitcast.50, bf16[8,768,2048]{2,1,0:T(8,128)(2,1)} %exponential_convert_fusion), kind=kOutput, calls=%fused_computation.11 | convolution fusion | flops 3222011904 | bytes 27262976 | tf_op jit(solution)/shard_map/ic,sij->sjc/dot_general | solution.py:143
  125.9 0.4 maximum_maximum_fusion
  126.2 22.9 %all_to_all.51 = bf16[8,784,128]{2,1,0:T(8,128)(2,1)S(1)} all-to-all(bf16[8,784,128]{2,1,0:T(8,128)(2,1)S(1)} %maximum_maximum_fusion), channel_id=1, replica_groups=mesh['blk'=8,'dom'=16] {'blk'}, dimensions={0} | all-to-all | bytes 3211264 | tf_op jit(solution)/shard_map/all_to_all | solution.py:150
  149.1 0.2 convert_element_type.197
  149.4 0.2 fusion.5
  149.6 0.5 copy-done
  150.1 0.2 fusion.18
  150.3 0.2 exponential_convert_fusion.1
  150.5 0.2 broadcast_in_dim.26
  150.7 21.8 %all_to_all.52 = bf16[8,784,128]{2,1,0:T(8,128)(2,1)S(1)} all-to-all(bf16[8,784,128]{2,1,0:T(8,128)(2,1)S(1)} %broadcast_in_dim.26), channel_id=1, replica_groups=mesh['blk'=8,'dom'=16] {'blk'}, dimensions={0} | all-to-all | bytes 3211264 | tf_op jit(solution)/shard_map/all_to_all | solution.py:66
  172.6 13.5 %multiply_reduce_fusion = bf16[2048,128]{1,0:T(8,128)(2,1)S(1)} fusion(f32[8,128]{1,0:T(8,128)S(1)} %bitcast.60, bf16[8,768,2048]{2,1,0:T(8,128)(2,1)} %exponential_convert_fusion, bf16[8,784,128]{2,1,0:T(8,128)(2,1)S(1)} %all_to_all.52), kind=kOutput, calls=%fused_computation.5 | convolution fusion | flops 3225157632 | bytes 27267072 | tf_op jit(solution)/shard_map/sij,sjc->sic/dot_general | solution.py:118
  186.1 0.2 maximum_maximum_fusion.3
  186.3 21.2 %all_to_all.53 = bf16[16,144,128]{2,1,0:T(8,128)(2,1)S(1)} all-to-all(bf16[16,144,128]{2,1,0:T(8,128)(2,1)S(1)} %maximum_maximum_fusion.3), channel_id=1, replica_groups=mesh['blk'=8,'dom'=16] {'dom'}, dimensions={0} | all-to-all | bytes 1179648 | tf_op jit(solution)/shard_map/all_to_all | solution.py:125
  207.6 0.1 convert_element_type.203
  207.7 0.1 fusion.14
  208.0 15.6 %all_to_all.54 = bf16[16,144,128]{2,1,0:T(8,128)(2,1)S(1)} all-to-all(bf16[16,144,128]{2,1,0:T(8,128)(2,1)S(1)} %broadcast_in_dim.28), channel_id=1, replica_groups=mesh['blk'=8,'dom'=16] {'dom'}, dimensions={0} | all-to-all | bytes 1179648 | tf_op jit(solution)/shard_map/all_to_all | solution.py:66
  223.7 0.1 multiply_convert_fusion
  223.8 11.8 %fusion.9 = bf16[8,768,128]{2,1,0:T(8,128)(2,1)S(1)} fusion(bf16[2048,128,1]{1,0,2:T(8,128)(2,1)S(1)} %bitcast.49, bf16[8,768,2048]{2,1,0:T(8,128)(2,1)} %exponential_convert_fusion), kind=kOutput, calls=%fused_computation.12 | convolution fusion | flops 3222011904 | bytes 27262976 | tf_op jit(solution)/shard_map/ic,sij->sjc/dot_general | solution.py:143
  235.6 0.4 maximum_maximum_fusion.1
  236.0 24.2 %all_to_all.55 = bf16[8,784,128]{2,1,0:T(8,128)(2,1)S(1)} all-to-all(bf16[8,784,128]{2,1,0:T(8,128)(2,1)S(1)} %maximum_maximum_fusion.1), channel_id=1, replica_groups=mesh['blk'=8,'dom'=16] {'blk'}, dimensions={0} | all-to-all | bytes 3211264 | tf_op jit(solution)/shard_map/all_to_all | solution.py:150
  260.1 0.2 convert_element_type.211
  260.4 0.2 fusion.4
  260.6 0.9 log_subtract_fusion
  (54 shorter events, 1.1 us)
Async XLA Ops:
  0.6 25.5 %copy-start.1 = (f32[768,128]{1,0:T(8,128)S(1)}, f32[768,128]{1,0:T(8,128)}, u32[]{:S(2)}) copy-start(f32[768,128]{1,0:T(8,128)} %param.9) | copy-start | bytes 1179652
  2.9 18.1 %all-to-all-start.1 = ((bf16[16,128,64]{1,2,0:T(8,128)(2,1)}), bf16[16,128,64]{1,2,0:T(8,128)(2,1)S(1)}, u32[]{:S(2)}, u32[]{:S(2)}) async-start(bf16[16,128,64]{1,2,0:T(8,128)(2,1)} %broadcast_in_dim.21), calls=%async_computation.1 | async-start | bytes 524288 | tf_op jit(solution)/shard_map/all_to_all | solution.py:66
  22.0 17.2 %all-to-all-start = ((bf16[8,768,64]{1,2,0:T(8,128)(2,1)}), bf16[8,768,64]{1,2,0:T(8,128)(2,1)S(1)}, u32[]{:S(2)}, u32[]{:S(2)}) async-start(bf16[8,768,64]{1,2,0:T(8,128)(2,1)} %broadcast_in_dim.20), calls=%async_computation | async-start | bytes 1572864 | tf_op jit(solution)/shard_map/all_to_all | solution.py:66
  40.7 25.4 %all-to-all-start.2 = ((bf16[8,784,128]{2,1,0:T(8,128)(2,1)}), bf16[8,784,128]{2,1,0:T(8,128)(2,1)S(1)}, u32[]{:S(2)}, u32[]{:S(2)}) async-start(bf16[8,784,128]{2,1,0:T(8,128)(2,1)} %broadcast_in_dim.22), calls=%async_computation.2 | async-start | bytes 3211264 | tf_op jit(solution)/shard_map/all_to_all | solution.py:66
  79.6 17.4 %copy-start.2 = (s32[128,128]{1,0:T(8,128)S(1)}, s32[128,128]{1,0:T(8,128)}, u32[]{:S(2)}) copy-start(s32[128,128]{1,0:T(8,128)} %param.7) | copy-start | bytes 196612
  98.1 15.8 %all-to-all-start.4 = ((bf16[16,144,128]{2,1,0:T(8,128)(2,1)}), bf16[16,144,128]{2,1,0:T(8,128)(2,1)S(1)}, u32[]{:S(2)}, u32[]{:S(2)}) async-start(bf16[16,144,128]{2,1,0:T(8,128)(2,1)} %broadcast_in_dim.24), calls=%async_computation.4 | async-start | bytes 1179648 | tf_op jit(solution)/shard_map/all_to_all | solution.py:66
  149.1 1.0 copy-start
  207.8 27.8 %copy-start.3 = (f32[128,128]{1,0:T(8,128)}, f32[128,128]{1,0:T(8,128)S(1)}, u32[]{:S(2)}) copy-start(f32[128,128]{1,0:T(8,128)S(1)} %get-tuple-element.3) | copy-start | bytes 196612

commit v9 on v8

--- a/solution.py
+++ b/solution.py
@@ -115,9 +115,9 @@
         segment_shift = gathered[:, tgt_rows, :].astype(jnp.float32)
         group_shift = jnp.max(segment_shift, axis=0)
         factors = jnp.exp(segment_shift - group_shift[None, :])
-        per_segment = jnp.einsum(
-            "sij,sjc->sic", kernel, weight_segments, preferred_element_type=jnp.float32)
-        partial_value = jnp.sum(per_segment * factors[:, None, :], axis=0)
+        scaled_segments = (weight_segments.astype(jnp.float32) * factors[:, None, :]).astype(jnp.bfloat16)
+        partial_value = jnp.einsum(
+            "sij,sjc->ic", kernel, scaled_segments, preferred_element_type=jnp.float32)
         pieces = jnp.concatenate(
             [partial_value.reshape(dom_count, src_rows, columns),
              jnp.broadcast_to(group_shift[None, None, :], (dom_count, 1, columns)),

time: 262 us -> 260 us (level)
  matrix products: 63 us -> 59.4 us
    dot_general x2, matrix products: 27 us -> 23.5 us  [body(): jnp.einsum('sij,sjc->ic', kernel, scaled_segments, preferred_element_type...]
where the time goes in v9:
time: 260 us; the launch traced here: 259 us
  blocking collectives  123 us (47%)
  matrix products  59.4 us (23%)
  waiting for transfers between devices  40.5 us (16%)
  starting transfers between devices  21.1 us (8%)
  other arithmetic  8 us (3%)
  local copies, waits for them, and re-layouts  6.23 us (2%)
    all_to_all x2, blocking collectives, body(): lax.all_to_all(pieces.astype(jnp.bfloat16), 'blk', 0, 0, tiled=False)  47 us
    all_to_all x4, waiting for transfers between devices, copy_gather(): lax.all_to_all(jnp.broadcast_to(value[None], (count,) + value.shape), axi...  40.5 us
    all_to_all x2, blocking collectives, body(): lax.all_to_all(pieces.astype(jnp.bfloat16), 'dom', 0, 0, tiled=False)  38.2 us
    all_to_all x2, blocking collectives, copy_gather(): lax.all_to_all(jnp.broadcast_to(value[None], (count,) + value.shape), axi...  37.5 us
    dot_general x2, matrix products, body(): jnp.einsum('ic,sij->sjc', source_weights, kernel, preferred_element_type=...  23.5 us
    dot_general x2, matrix products, body(): jnp.einsum('sij,sjc->ic', kernel, scaled_segments, preferred_element_type...  23.5 us
    all_to_all x4, starting transfers between devices, copy_gather(): lax.all_to_all(jnp.broadcast_to(value[None], (count,) + value.shape), axi...  21.1 us
    dot_general x1, matrix products, body(): jnp.einsum('id,sjd->sij', source_block, target_group.reshape(blk_count, t...  12.4 us
  transfers between devices with their start and end apart: 4, of which 4 were waited for; matrix products, arithmetic and copies ran while one was open for 6% of the time, Pallas kernels for 0%

profile of v9, /device:TPU:1, one launch (start us, length us, event | category | flops | bytes accessed | tf_op | source)
XLA Modules:
  0.0 258.9 jit_solution(8593242403175339282)
XLA Ops:
  0.6 0.7 fusion.14
  1.4 0.7 fusion.15
  2.1 0.8 broadcast_in_dim.21
  2.9 9.6 %all-to-all-start.1 = ((bf16[16,128,64]{1,2,0:T(8,128)(2,1)}), bf16[16,128,64]{1,2,0:T(8,128)(2,1)S(1)}, u32[]{:S(2)}, u32[]{:S(2)}) async-start(bf16[16,128,64]{1,2,0:T(8,128)(2,1)} %broadcast_in_dim.21), calls=%async_computation.1 | async-start | bytes 524288 | tf_op jit(solution)/shard_map/all_to_all | solution.py:66
  12.4 0.9 fusion.11
  13.4 0.9 fusion.12
  14.3 6.8 %all-to-all-done.1 = bf16[16,128,64]{1,2,0:T(8,128)(2,1)S(1)} async-done(((bf16[16,128,64]{1,2,0:T(8,128)(2,1)}), bf16[16,128,64]{1,2,0:T(8,128)(2,1)S(1)}, u32[]{:S(2)}, u32[]{:S(2)}) %all-to-all-start.1) | async-done | bytes 262176 | tf_op jit(solution)/shard_map/all_to_all | solution.py:66
  21.1 0.9 broadcast_in_dim.20
  22.1 4.1 %all-to-all-start = ((bf16[8,768,64]{1,2,0:T(8,128)(2,1)}), bf16[8,768,64]{1,2,0:T(8,128)(2,1)S(1)}, u32[]{:S(2)}, u32[]{:S(2)}) async-start(bf16[8,768,64]{1,2,0:T(8,128)(2,1)} %broadcast_in_dim.20), calls=%async_computation | async-start | bytes 1572864 | tf_op jit(solution)/shard_map/all_to_all | solution.py:66
  26.2 0.1 reduce_max.128
  26.5 0.2 copy.9
  26.7 0.1 reshape.164
  26.8 12.4 %all-to-all-done = bf16[8,768,64]{1,2,0:T(8,128)(2,1)S(1)} async-done(((bf16[8,768,64]{1,2,0:T(8,128)(2,1)}), bf16[8,768,64]{1,2,0:T(8,128)(2,1)S(1)}, u32[]{:S(2)}, u32[]{:S(2)}) %all-to-all-start) | async-done | bytes 786464 | tf_op jit(solution)/shard_map/all_to_all | solution.py:66
  39.3 1.5 broadcast_in_dim.22
  40.7 3.6 %all-to-all-start.2 = ((bf16[8,784,128]{2,1,0:T(8,128)(2,1)}), bf16[8,784,128]{2,1,0:T(8,128)(2,1)S(1)}, u32[]{:S(2)}, u32[]{:S(2)}) async-start(bf16[8,784,128]{2,1,0:T(8,128)(2,1)} %broadcast_in_dim.22), calls=%async_computation.2 | async-start | bytes 3211264 | tf_op jit(solution)/shard_map/all_to_all | solution.py:66
  44.3 12.4 %fusion = bf16[8,2048,768]{1,2,0:T(8,128)(2,1)} fusion(bf16[8,768,64]{1,2,0:T(8,128)(2,1)S(1)} %all-to-all-done, bf16[2048,64,1]{0,1,2:T(8,128)(2,1)S(1)} %reshape.164), kind=kOutput, calls=%fused_computation.1 | convolution fusion | flops 1648361472 | bytes 26214400 | tf_op jit(solution)/shard_map/id,sjd->sij/dot_general | solution.py:93
  56.7 9.4 %all-to-all-done.2 = bf16[8,784,128]{2,1,0:T(8,128)(2,1)S(1)} async-done(((bf16[8,784,128]{2,1,0:T(8,128)(2,1)}), bf16[8,784,128]{2,1,0:T(8,128)(2,1)S(1)}, u32[]{:S(2)}, u32[]{:S(2)}) %all-to-all-start.2) | async-done | bytes 1605664 | tf_op jit(solution)/shard_map/all_to_all | solution.py:66
  66.1 11.7 %fusion.3 = bf16[2048,128]{1,0:T(8,128)(2,1)S(1)} fusion(bf16[8,2048,768]{1,2,0:T(8,128)(2,1)} %fusion, bf16[8,784,128]{2,1,0:T(8,128)(2,1)S(1)} %all-to-all-done.2, f32[8,128]{1,0:T(8,128)S(1)} %bitcast.58), kind=kOutput, calls=%fused_computation.10 | convolution fusion | flops 3223846912 | bytes 27267072 | tf_op jit(solution)/shard_map/sij,sjc->ic/dot_general | solution.py:119
  77.9 0.2 maximum_maximum_fusion.2
  78.1 17.0 %all_to_all.50 = bf16[16,144,128]{2,1,0:T(8,128)(2,1)S(1)} all-to-all(bf16[16,144,128]{2,1,0:T(8,128)(2,1)S(1)} %maximum_maximum_fusion.2), channel_id=1, replica_groups=mesh['blk'=8,'dom'=16] {'dom'}, dimensions={0} | all-to-all | bytes 1179648 | tf_op jit(solution)/shard_map/all_to_all | solution.py:125
  95.2 0.1 fusion.10
  95.3 0.6 copy-done.2
  96.0 0.9 broadcast_in_dim.24
  96.9 3.8 %all-to-all-start.4 = ((bf16[16,144,128]{2,1,0:T(8,128)(2,1)}), bf16[16,144,128]{2,1,0:T(8,128)(2,1)S(1)}, u32[]{:S(2)}, u32[]{:S(2)}) async-start(bf16[16,144,128]{2,1,0:T(8,128)(2,1)} %broadcast_in_dim.24), calls=%async_computation.4 | async-start | bytes 1179648 | tf_op jit(solution)/shard_map/all_to_all | solution.py:66
  100.8 11.9 %all-to-all-done.4 = bf16[16,144,128]{2,1,0:T(8,128)(2,1)S(1)} async-done(((bf16[16,144,128]{2,1,0:T(8,128)(2,1)}), bf16[16,144,128]{2,1,0:T(8,128)(2,1)S(1)}, u32[]{:S(2)}, u32[]{:S(2)}) %all-to-all-start.4) | async-done | bytes 589856 | tf_op jit(solution)/shard_map/all_to_all | solution.py:66
  112.8 0.1 multiply_convert_fusion.5
  112.9 11.8 %convolution_convert_fusion.1 = bf16[8,768,128]{2,1,0:T(8,128)(2,1)S(1)} fusion(bf16[8,2048,768]{1,2,0:T(8,128)(2,1)} %fusion, bf16[2048,128,1]{1,0,2:T(8,128)(2,1)S(1)} %bitcast.51), kind=kOutput, calls=%fused_computation.13 | convolution fusion | flops 3222011904 | bytes 27262976 | tf_op jit(solution)/shard_map/ic,sij->sjc/dot_general | solution.py:143
  124.7 0.4 maximum_maximum_fusion
  125.1 22.9 %all_to_all.51 = bf16[8,784,128]{2,1,0:T(8,128)(2,1)S(1)} all-to-all(bf16[8,784,128]{2,1,0:T(8,128)(2,1)S(1)} %maximum_maximum_fusion), channel_id=1, replica_groups=mesh['blk'=8,'dom'=16] {'blk'}, dimensions={0} | all-to-all | bytes 3211264 | tf_op jit(solution)/shard_map/all_to_all | solution.py:150
  148.0 0.2 convert_element_type.211
  148.2 0.2 fusion.2
  148.4 0.8 copy-done
  149.2 0.2 fusion.13
  149.4 0.2 exponential_convert_fusion.1
  149.6 0.2 broadcast_in_dim.26
  149.8 21.8 %all_to_all.52 = bf16[8,784,128]{2,1,0:T(8,128)(2,1)S(1)} all-to-all(bf16[8,784,128]{2,1,0:T(8,128)(2,1)S(1)} %broadcast_in_dim.26), channel_id=1, replica_groups=mesh['blk'=8,'dom'=16] {'blk'}, dimensions={0} | all-to-all | bytes 3211264 | tf_op jit(solution)/shard_map/all_to_all | solution.py:66
  171.7 11.7 %fusion.4 = bf16[2048,128]{1,0:T(8,128)(2,1)S(1)} fusion(bf16[8,2048,768]{1,2,0:T(8,128)(2,1)} %fusion, bf16[8,784,128]{2,1,0:T(8,128)(2,1)S(1)} %all_to_all.52, f32[8,128]{1,0:T(8,128)S(1)} %bitcast.59), kind=kOutput, calls=%fused_computation.11 | convolution fusion | flops 3223846912 | bytes 27267072 | tf_op jit(solution)/shard_map/sij,sjc->ic/dot_general | solution.py:119
  183.5 0.2 maximum_maximum_fusion.3
  183.6 21.2 %all_to_all.53 = bf16[16,144,128]{2,1,0:T(8,128)(2,1)S(1)} all-to-all(bf16[16,144,128]{2,1,0:T(8,128)(2,1)S(1)} %maximum_maximum_fusion.3), channel_id=1, replica_groups=mesh['blk'=8,'dom'=16] {'dom'}, dimensions={0} | all-to-all | bytes 1179648 | tf_op jit(solution)/shard_map/all_to_all | solution.py:125
  205.0 0.1 fusion.9
  205.3 15.6 %all_to_all.54 = bf16[16,144,128]{2,1,0:T(8,128)(2,1)S(1)} all-to-all(bf16[16,144,128]{2,1,0:T(8,128)(2,1)S(1)} %broadcast_in_dim.28), channel_id=1, replica_groups=mesh['blk'=8,'dom'=16] {'dom'}, dimensions={0} | all-to-all | bytes 1179648 | tf_op jit(solution)/shard_map/all_to_all | solution.py:66
  221.0 0.1 multiply_convert_fusion.4
  221.1 11.8 %convolution_convert_fusion = bf16[8,768,128]{2,1,0:T(8,128)(2,1)S(1)} fusion(bf16[8,2048,768]{1,2,0:T(8,128)(2,1)} %fusion, bf16[2048,128,1]{1,0,2:T(8,128)(2,1)S(1)} %bitcast.50), kind=kOutput, calls=%fused_computation.12 | convolution fusion | flops 3222011904 | bytes 27262976 | tf_op jit(solution)/shard_map/ic,sij->sjc/dot_general | solution.py:143
  232.9 0.4 maximum_maximum_fusion.1
  233.3 24.2 %all_to_all.55 = bf16[8,784,128]{2,1,0:T(8,128)(2,1)S(1)} all-to-all(bf16[8,784,128]{2,1,0:T(8,128)(2,1)S(1)} %maximum_maximum_fusion.1), channel_id=1, replica_groups=mesh['blk'=8,'dom'=16] {'blk'}, dimensions={0} | all-to-all | bytes 3211264 | tf_op jit(solution)/shard_map/all_to_all | solution.py:150
  257.5 0.2 convert_element_type.227
  257.7 0.2 fusion.1
  257.9 0.9 log_subtract_fusion
  (52 shorter events, 1.2 us)
Async XLA Ops:
  2.9 23.4 %copy-start.1 = (f32[768,128]{1,0:T(8,128)S(1)}, f32[768,128]{1,0:T(8,128)}, u32[]{:S(2)}) copy-start(f32[768,128]{1,0:T(8,128)} %param.9) | copy-start | bytes 1179652
  2.9 18.3 %all-to-all-start.1 = ((bf16[16,128,64]{1,2,0:T(8,128)(2,1)}), bf16[16,128,64]{1,2,0:T(8,128)(2,1)S(1)}, u32[]{:S(2)}, u32[]{:S(2)}) async-start(bf16[16,128,64]{1,2,0:T(8,128)(2,1)} %broadcast_in_dim.21), calls=%async_computation.1 | async-start | bytes 524288 | tf_op jit(solution)/shard_map/all_to_all | solution.py:66
  22.1 17.2 %all-to-all-start = ((bf16[8,768,64]{1,2,0:T(8,128)(2,1)}), bf16[8,768,64]{1,2,0:T(8,128)(2,1)S(1)}, u32[]{:S(2)}, u32[]{:S(2)}) async-start(bf16[8,768,64]{1,2,0:T(8,128)(2,1)} %broadcast_in_dim.20), calls=%async_computation | async-start | bytes 1572864 | tf_op jit(solution)/shard_map/all_to_all | solution.py:66
  40.7 25.4 %all-to-all-start.2 = ((bf16[8,784,128]{2,1,0:T(8,128)(2,1)}), bf16[8,784,128]{2,1,0:T(8,128)(2,1)S(1)}, u32[]{:S(2)}, u32[]{:S(2)}) async-start(bf16[8,784,128]{2,1,0:T(8,128)(2,1)} %broadcast_in_dim.22), calls=%async_computation.2 | async-start | bytes 3211264 | tf_op jit(solution)/shard_map/all_to_all | solution.py:66
  95.0 0.8 copy-start.2
  96.9 15.8 %all-to-all-start.4 = ((bf16[16,144,128]{2,1,0:T(8,128)(2,1)}), bf16[16,144,128]{2,1,0:T(8,128)(2,1)S(1)}, u32[]{:S(2)}, u32[]{:S(2)}) async-start(bf16[16,144,128]{2,1,0:T(8,128)(2,1)} %broadcast_in_dim.24), calls=%async_computation.4 | async-start | bytes 1179648 | tf_op jit(solution)/shard_map/all_to_all | solution.py:66
  148.2 1.0 copy-start
  205.1 27.8 %copy-start.3 = (f32[128,128]{1,0:T(8,128)}, f32[128,128]{1,0:T(8,128)S(1)}, u32[]{:S(2)}) copy-start(f32[128,128]{1,0:T(8,128)S(1)} %get-tuple-element.3) | copy-start | bytes 196612

commit v10 on v9

--- a/solution.py
+++ b/solution.py
@@ -15,51 +15,6 @@
     widened = values.astype(jnp.float32)
     squared = jnp.sum(widened * widened, axis=1, keepdims=True) + 1e-06
     return (widened * lax.rsqrt(squared)).astype(jnp.bfloat16)
-
-
-def kernel_block(row_piece, col_piece):
-    products = jnp.dot(row_piece, col_piece.T, preferred_element_type=jnp.float32)
-    return jnp.exp((products - 1.0) / entropic).astype(jnp.bfloat16)
-
-
-def segment_sums(row_emb, col_segments, weight_segments, factors, row_block):
-    row_count = row_emb.shape[0]
-    row_parts = row_emb.reshape(row_count // row_block, row_block, row_emb.shape[1])
-
-    def one_block(row_piece):
-
-        def add_segment(running, paired):
-            col_piece, weight_piece, factor = paired
-            kernel = kernel_block(row_piece, col_piece)
-            part = jnp.dot(kernel, weight_piece, preferred_element_type=jnp.float32)
-            return (running + factor[None, :] * part, None)
-
-        initial = jnp.zeros((row_piece.shape[0], weight_segments.shape[-1]), jnp.float32)
-        result, unused = lax.scan(add_segment, initial, (col_segments, weight_segments, factors))
-        return result
-
-    return lax.map(one_block, row_parts).reshape(row_count, weight_segments.shape[-1])
-
-
-def plain_sums(row_emb, col_emb, col_weights, row_block, col_block):
-    col_count = col_emb.shape[0]
-    segments = col_count // col_block
-    return segment_sums(
-        row_emb,
-        col_emb.reshape(segments, col_block, col_emb.shape[1]),
-        col_weights.reshape(segments, col_block, col_weights.shape[1]),
-        jnp.ones((segments, col_weights.shape[1]), jnp.float32),
-        row_block,
-    )
-
-
-def permute_gather(value, axis, count):
-    me = lax.axis_index(axis)
-    received = [value]
-    for shift in range(1, count):
-        received.append(lax.ppermute(value, axis, [(i, (i + shift) % count) for i in range(count)]))
-    stacked = jnp.stack(received[::-1], 0)
-    return jnp.roll(stacked, me + 1, axis=0)
 
 
 def copy_gather(value, axis, count):
@@ -80,7 +35,6 @@
     src_rows = source_emb.shape[0]
     tgt_rows = target_emb.shape[0]
     columns = warm_start.shape[1]
-    width = source_emb.shape[1]
     all_sources = src_rows * blk_count * dom_count
     all_targets = tgt_rows * blk_count * dom_count
     block_rows = src_rows * dom_count
@@ -98,9 +52,7 @@
     log_source = jnp.log(source_counts.astype(jnp.float32)) - math.log(all_sources)
 
     tgt_payload_rows = padded_rows(tgt_rows + 1, 16)
-    src_piece_rows = padded_rows(src_rows + 1, 8)
     src_payload_rows = padded_rows(src_rows + 1, 16)
-    tgt_piece_rows = padded_rows(tgt_rows + 1, 8)
 
     target_logs = warm_start
     source_logs = None

time: 260 us -> 260 us (level)
  no operation moved by 1% of the time
where the time goes in v10:
time: 260 us; the launch traced here: 259 us
  blocking collectives  123 us (47%)
  matrix products  59.4 us (23%)
  waiting for transfers between devices  40.5 us (16%)
  starting transfers between devices  21.1 us (8%)
  other arithmetic  8 us (3%)
  local copies, waits for them, and re-layouts  6.23 us (2%)
    all_to_all x2, blocking collectives, body(): lax.all_to_all(pieces.astype(jnp.bfloat16), 'blk', 0, 0, tiled=False)  47 us
    all_to_all x4, waiting for transfers between devices, copy_gather(): lax.all_to_all(jnp.broadcast_to(value[None], (count,) + value.shape), axi...  40.5 us
    all_to_all x2, blocking collectives, body(): lax.all_to_all(pieces.astype(jnp.bfloat16), 'dom', 0, 0, tiled=False)  38.2 us
    all_to_all x2, blocking collectives, copy_gather(): lax.all_to_all(jnp.broadcast_to(value[None], (count,) + value.shape), axi...  37.5 us
    dot_general x2, matrix products, body(): jnp.einsum('ic,sij->sjc', source_weights, kernel, preferred_element_type=...  23.5 us
    dot_general x2, matrix products, body(): jnp.einsum('sij,sjc->ic', kernel, scaled_segments, preferred_element_type...  23.5 us
    all_to_all x4, starting transfers between devices, copy_gather(): lax.all_to_all(jnp.broadcast_to(value[None], (count,) + value.shape), axi...  21.1 us
    dot_general x1, matrix products, body(): jnp.einsum('id,sjd->sij', source_block, target_group.reshape(blk_count, t...  12.4 us
  transfers between devices with their start and end apart: 4, of which 4 were waited for; matrix products, arithmetic and copies ran while one was open for 6% of the time, Pallas kernels for 0%

profile of v10, /device:TPU:1, one launch (start us, length us, event | category | flops | bytes accessed | tf_op | source)
XLA Modules:
  0.0 258.9 jit_solution(8593242403175339282)
XLA Ops:
  0.6 0.7 fusion.14
  1.4 0.7 fusion.15
  2.1 0.8 broadcast_in_dim.21
  2.9 9.6 %all-to-all-start.1 = ((bf16[16,128,64]{1,2,0:T(8,128)(2,1)}), bf16[16,128,64]{1,2,0:T(8,128)(2,1)S(1)}, u32[]{:S(2)}, u32[]{:S(2)}) async-start(bf16[16,128,64]{1,2,0:T(8,128)(2,1)} %broadcast_in_dim.21), calls=%async_computation.1 | async-start | bytes 524288 | tf_op jit(solution)/shard_map/all_to_all | solution.py:21
  12.4 0.9 fusion.11
  13.4 0.9 fusion.12
  14.3 6.8 %all-to-all-done.1 = bf16[16,128,64]{1,2,0:T(8,128)(2,1)S(1)} async-done(((bf16[16,128,64]{1,2,0:T(8,128)(2,1)}), bf16[16,128,64]{1,2,0:T(8,128)(2,1)S(1)}, u32[]{:S(2)}, u32[]{:S(2)}) %all-to-all-start.1) | async-done | bytes 262176 | tf_op jit(solution)/shard_map/all_to_all | solution.py:21
  21.1 0.9 broadcast_in_dim.20
  22.1 4.1 %all-to-all-start = ((bf16[8,768,64]{1,2,0:T(8,128)(2,1)}), bf16[8,768,64]{1,2,0:T(8,128)(2,1)S(1)}, u32[]{:S(2)}, u32[]{:S(2)}) async-start(bf16[8,768,64]{1,2,0:T(8,128)(2,1)} %broadcast_in_dim.20), calls=%async_computation | async-start | bytes 1572864 | tf_op jit(solution)/shard_map/all_to_all | solution.py:21
  26.2 0.1 reduce_max.128
  26.5 0.2 copy.9
  26.7 0.1 reshape.164
  26.8 12.4 %all-to-all-done = bf16[8,768,64]{1,2,0:T(8,128)(2,1)S(1)} async-done(((bf16[8,768,64]{1,2,0:T(8,128)(2,1)}), bf16[8,768,64]{1,2,0:T(8,128)(2,1)S(1)}, u32[]{:S(2)}, u32[]{:S(2)}) %all-to-all-start) | async-done | bytes 786464 | tf_op jit(solution)/shard_map/all_to_all | solution.py:21
  39.3 1.5 broadcast_in_dim.22
  40.7 3.6 %all-to-all-start.2 = ((bf16[8,784,128]{2,1,0:T(8,128)(2,1)}), bf16[8,784,128]{2,1,0:T(8,128)(2,1)S(1)}, u32[]{:S(2)}, u32[]{:S(2)}) async-start(bf16[8,784,128]{2,1,0:T(8,128)(2,1)} %broadcast_in_dim.22), calls=%async_computation.2 | async-start | bytes 3211264 | tf_op jit(solution)/shard_map/all_to_all | solution.py:21
  44.3 12.4 %fusion = bf16[8,2048,768]{1,2,0:T(8,128)(2,1)} fusion(bf16[8,768,64]{1,2,0:T(8,128)(2,1)S(1)} %all-to-all-done, bf16[2048,64,1]{0,1,2:T(8,128)(2,1)S(1)} %reshape.164), kind=kOutput, calls=%fused_computation.1 | convolution fusion | flops 1648361472 | bytes 26214400 | tf_op jit(solution)/shard_map/id,sjd->sij/dot_general | solution.py:47
  56.7 9.4 %all-to-all-done.2 = bf16[8,784,128]{2,1,0:T(8,128)(2,1)S(1)} async-done(((bf16[8,784,128]{2,1,0:T(8,128)(2,1)}), bf16[8,784,128]{2,1,0:T(8,128)(2,1)S(1)}, u32[]{:S(2)}, u32[]{:S(2)}) %all-to-all-start.2) | async-done | bytes 1605664 | tf_op jit(solution)/shard_map/all_to_all | solution.py:21
  66.1 11.7 %fusion.3 = bf16[2048,128]{1,0:T(8,128)(2,1)S(1)} fusion(bf16[8,2048,768]{1,2,0:T(8,128)(2,1)} %fusion, bf16[8,784,128]{2,1,0:T(8,128)(2,1)S(1)} %all-to-all-done.2, f32[8,128]{1,0:T(8,128)S(1)} %bitcast.58), kind=kOutput, calls=%fused_computation.10 | convolution fusion | flops 3223846912 | bytes 27267072 | tf_op jit(solution)/shard_map/sij,sjc->ic/dot_general | solution.py:71
  77.9 0.2 maximum_maximum_fusion.2
  78.1 17.0 %all_to_all.50 = bf16[16,144,128]{2,1,0:T(8,128)(2,1)S(1)} all-to-all(bf16[16,144,128]{2,1,0:T(8,128)(2,1)S(1)} %maximum_maximum_fusion.2), channel_id=1, replica_groups=mesh['blk'=8,'dom'=16] {'dom'}, dimensions={0} | all-to-all | bytes 1179648 | tf_op jit(solution)/shard_map/all_to_all | solution.py:77
  95.2 0.1 fusion.10
  95.3 0.6 copy-done.2
  96.0 0.9 broadcast_in_dim.24
  96.9 3.8 %all-to-all-start.4 = ((bf16[16,144,128]{2,1,0:T(8,128)(2,1)}), bf16[16,144,128]{2,1,0:T(8,128)(2,1)S(1)}, u32[]{:S(2)}, u32[]{:S(2)}) async-start(bf16[16,144,128]{2,1,0:T(8,128)(2,1)} %broadcast_in_dim.24), calls=%async_computation.4 | async-start | bytes 1179648 | tf_op jit(solution)/shard_map/all_to_all | solution.py:21
  100.8 11.9 %all-to-all-done.4 = bf16[16,144,128]{2,1,0:T(8,128)(2,1)S(1)} async-done(((bf16[16,144,128]{2,1,0:T(8,128)(2,1)}), bf16[16,144,128]{2,1,0:T(8,128)(2,1)S(1)}, u32[]{:S(2)}, u32[]{:S(2)}) %all-to-all-start.4) | async-done | bytes 589856 | tf_op jit(solution)/shard_map/all_to_all | solution.py:21
  112.8 0.1 multiply_convert_fusion.5
  112.9 11.8 %convolution_convert_fusion.1 = bf16[8,768,128]{2,1,0:T(8,128)(2,1)S(1)} fusion(bf16[8,2048,768]{1,2,0:T(8,128)(2,1)} %fusion, bf16[2048,128,1]{1,0,2:T(8,128)(2,1)S(1)} %bitcast.51), kind=kOutput, calls=%fused_computation.13 | convolution fusion | flops 3222011904 | bytes 27262976 | tf_op jit(solution)/shard_map/ic,sij->sjc/dot_general | solution.py:95
  124.7 0.4 maximum_maximum_fusion
  125.1 22.9 %all_to_all.51 = bf16[8,784,128]{2,1,0:T(8,128)(2,1)S(1)} all-to-all(bf16[8,784,128]{2,1,0:T(8,128)(2,1)S(1)} %maximum_maximum_fusion), channel_id=1, replica_groups=mesh['blk'=8,'dom'=16] {'blk'}, dimensions={0} | all-to-all | bytes 3211264 | tf_op jit(solution)/shard_map/all_to_all | solution.py:102
  148.0 0.2 convert_element_type.211
  148.2 0.2 fusion.2
  148.4 0.8 copy-done
  149.2 0.2 fusion.13
  149.4 0.2 exponential_convert_fusion.1
  149.6 0.2 broadcast_in_dim.26
  149.8 21.8 %all_to_all.52 = bf16[8,784,128]{2,1,0:T(8,128)(2,1)S(1)} all-to-all(bf16[8,784,128]{2,1,0:T(8,128)(2,1)S(1)} %broadcast_in_dim.26), channel_id=1, replica_groups=mesh['blk'=8,'dom'=16] {'blk'}, dimensions={0} | all-to-all | bytes 3211264 | tf_op jit(solution)/shard_map/all_to_all | solution.py:21
  171.7 11.7 %fusion.4 = bf16[2048,128]{1,0:T(8,128)(2,1)S(1)} fusion(bf16[8,2048,768]{1,2,0:T(8,128)(2,1)} %fusion, bf16[8,784,128]{2,1,0:T(8,128)(2,1)S(1)} %all_to_all.52, f32[8,128]{1,0:T(8,128)S(1)} %bitcast.59), kind=kOutput, calls=%fused_computation.11 | convolution fusion | flops 3223846912 | bytes 27267072 | tf_op jit(solution)/shard_map/sij,sjc->ic/dot_general | solution.py:71
  183.5 0.2 maximum_maximum_fusion.3
  183.6 21.2 %all_to_all.53 = bf16[16,144,128]{2,1,0:T(8,128)(2,1)S(1)} all-to-all(bf16[16,144,128]{2,1,0:T(8,128)(2,1)S(1)} %maximum_maximum_fusion.3), channel_id=1, replica_groups=mesh['blk'=8,'dom'=16] {'dom'}, dimensions={0} | all-to-all | bytes 1179648 | tf_op jit(solution)/shard_map/all_to_all | solution.py:77
  205.0 0.1 fusion.9
  205.3 15.6 %all_to_all.54 = bf16[16,144,128]{2,1,0:T(8,128)(2,1)S(1)} all-to-all(bf16[16,144,128]{2,1,0:T(8,128)(2,1)S(1)} %broadcast_in_dim.28), channel_id=1, replica_groups=mesh['blk'=8,'dom'=16] {'dom'}, dimensions={0} | all-to-all | bytes 1179648 | tf_op jit(solution)/shard_map/all_to_all | solution.py:21
  221.0 0.1 multiply_convert_fusion.4
  221.1 11.8 %convolution_convert_fusion = bf16[8,768,128]{2,1,0:T(8,128)(2,1)S(1)} fusion(bf16[8,2048,768]{1,2,0:T(8,128)(2,1)} %fusion, bf16[2048,128,1]{1,0,2:T(8,128)(2,1)S(1)} %bitcast.50), kind=kOutput, calls=%fused_computation.12 | convolution fusion | flops 3222011904 | bytes 27262976 | tf_op jit(solution)/shard_map/ic,sij->sjc/dot_general | solution.py:95
  232.9 0.4 maximum_maximum_fusion.1
  233.3 24.2 %all_to_all.55 = bf16[8,784,128]{2,1,0:T(8,128)(2,1)S(1)} all-to-all(bf16[8,784,128]{2,1,0:T(8,128)(2,1)S(1)} %maximum_maximum_fusion.1), channel_id=1, replica_groups=mesh['blk'=8,'dom'=16] {'blk'}, dimensions={0} | all-to-all | bytes 3211264 | tf_op jit(solution)/shard_map/all_to_all | solution.py:102
  257.5 0.2 convert_element_type.227
  257.7 0.2 fusion.1
  257.9 0.9 log_subtract_fusion
  (52 shorter events, 1.2 us)
Async XLA Ops:
  2.9 23.4 %copy-start.1 = (f32[768,128]{1,0:T(8,128)S(1)}, f32[768,128]{1,0:T(8,128)}, u32[]{:S(2)}) copy-start(f32[768,128]{1,0:T(8,128)} %param.9) | copy-start | bytes 1179652
  2.9 18.3 %all-to-all-start.1 = ((bf16[16,128,64]{1,2,0:T(8,128)(2,1)}), bf16[16,128,64]{1,2,0:T(8,128)(2,1)S(1)}, u32[]{:S(2)}, u32[]{:S(2)}) async-start(bf16[16,128,64]{1,2,0:T(8,128)(2,1)} %broadcast_in_dim.21), calls=%async_computation.1 | async-start | bytes 524288 | tf_op jit(solution)/shard_map/all_to_all | solution.py:21
  22.1 17.2 %all-to-all-start = ((bf16[8,768,64]{1,2,0:T(8,128)(2,1)}), bf16[8,768,64]{1,2,0:T(8,128)(2,1)S(1)}, u32[]{:S(2)}, u32[]{:S(2)}) async-start(bf16[8,768,64]{1,2,0:T(8,128)(2,1)} %broadcast_in_dim.20), calls=%async_computation | async-start | bytes 1572864 | tf_op jit(solution)/shard_map/all_to_all | solution.py:21
  40.7 25.4 %all-to-all-start.2 = ((bf16[8,784,128]{2,1,0:T(8,128)(2,1)}), bf16[8,784,128]{2,1,0:T(8,128)(2,1)S(1)}, u32[]{:S(2)}, u32[]{:S(2)}) async-start(bf16[8,784,128]{2,1,0:T(8,128)(2,1)} %broadcast_in_dim.22), calls=%async_computation.2 | async-start | bytes 3211264 | tf_op jit(solution)/shard_map/all_to_all | solution.py:21
  95.0 0.8 copy-start.2
  96.9 15.8 %all-to-all-start.4 = ((bf16[16,144,128]{2,1,0:T(8,128)(2,1)}), bf16[16,144,128]{2,1,0:T(8,128)(2,1)S(1)}, u32[]{:S(2)}, u32[]{:S(2)}) async-start(bf16[16,144,128]{2,1,0:T(8,128)(2,1)} %broadcast_in_dim.24), calls=%async_computation.4 | async-start | bytes 1179648 | tf_op jit(solution)/shard_map/all_to_all | solution.py:21
  148.2 1.0 copy-start
  205.1 27.8 %copy-start.3 = (f32[128,128]{1,0:T(8,128)}, f32[128,128]{1,0:T(8,128)S(1)}, u32[]{:S(2)}) copy-start(f32[128,128]{1,0:T(8,128)S(1)} %get-tuple-element.3) | copy-start | bytes 196612

commit v11 on v10

--- a/solution.py
+++ b/solution.py
@@ -4,6 +4,7 @@
 import jax.numpy as jnp
 from jax import lax
 from jax.sharding import PartitionSpec as P
+
 
 ITERS = 2
 
@@ -29,7 +30,7 @@
     return -(-rows // multiple) * multiple
 
 
-def body(source_emb, target_emb, source_counts, target_counts, warm_start):
+def steps(source_emb, target_emb, source_counts, target_counts, warm_start):
     blk_count = lax.axis_size("blk")
     dom_count = lax.axis_size("dom")
     src_rows = source_emb.shape[0]
@@ -42,7 +43,8 @@
 
     source_block = copy_gather(normalized(source_emb), "dom", dom_count).reshape(
         src_rows * dom_count, source_emb.shape[1])
-    target_group = copy_gather(normalized(target_emb), "blk", blk_count).reshape(
+    target_copies = jnp.broadcast_to(normalized(target_emb)[None], (blk_count,) + target_emb.shape)
+    target_group = lax.all_to_all(target_copies, "blk", 0, 0, tiled=False).reshape(
         tgt_rows * blk_count, target_emb.shape[1])
     products = jnp.einsum(
         "id,sjd->sij", source_block, target_group.reshape(blk_count, tgt_rows, source_emb.shape[1]),
@@ -62,7 +64,11 @@
         payload = jnp.concatenate(
             [weights, shift.astype(jnp.bfloat16)[None, :],
              jnp.zeros((tgt_payload_rows - tgt_rows - 1, columns), jnp.bfloat16)], axis=0)
-        gathered = copy_gather(payload, "blk", blk_count)
+        if iteration == 0:
+            copies = jnp.broadcast_to(payload[None], (blk_count,) + payload.shape)
+            gathered = lax.all_to_all(copies, "blk", 0, 0, tiled=False)
+        else:
+            gathered = copy_gather(payload, "blk", blk_count)
         weight_segments = gathered[:, :tgt_rows, :]
         segment_shift = gathered[:, tgt_rows, :].astype(jnp.float32)
         group_shift = jnp.max(segment_shift, axis=0)
@@ -117,4 +123,4 @@
         P(("blk", "dom"), None),
     )
     out_specs = (P(("blk", "dom"), None), P(("blk", "dom"), None))
-    return jax.shard_map(body, mesh=mesh, in_specs=in_specs, out_specs=out_specs, check_vma=False)
+    return jax.shard_map(steps, mesh=mesh, in_specs=in_specs, out_specs=out_specs, check_vma=False)

time: 260 us -> 260 us (level)
    all_to_all x0 -> x2, waiting for transfers between devices: none -> 21.8 us  [the longest x1 12.4 us: steps(): lax.all_to_all(target_copies, 'blk', 0, 0, tiled=False)]
    all_to_all x4 -> x2, waiting for transfers between devices: 40.5 us -> 18.7 us  [copy_gather(): lax.all_to_all(jnp.broadcast_to(value[None], (count,) + value.shape), axi...]
    all_to_all x0 -> x2, starting transfers between devices: none -> 7.72 us  [the longest x1 4.13 us: steps(): lax.all_to_all(target_copies, 'blk', 0, 0, tiled=False)]
    all_to_all x4 -> x2, starting transfers between devices: 21.1 us -> 13.4 us  [copy_gather(): lax.all_to_all(jnp.broadcast_to(value[None], (count,) + value.shape), axi...]
where the time goes in v11:
time: 260 us; the launch traced here: 259 us
  blocking collectives  123 us (47%)
  matrix products  59.4 us (23%)
  waiting for transfers between devices  40.5 us (16%)
  starting transfers between devices  21.1 us (8%)
  other arithmetic  8 us (3%)
  local copies, waits for them, and re-layouts  6.23 us (2%)
    all_to_all x2, blocking collectives, steps(): lax.all_to_all(pieces.astype(jnp.bfloat16), 'blk', 0, 0, tiled=False)  47 us
    all_to_all x2, blocking collectives, steps(): lax.all_to_all(pieces.astype(jnp.bfloat16), 'dom', 0, 0, tiled=False)  38.2 us
    all_to_all x2, blocking collectives, copy_gather(): lax.all_to_all(jnp.broadcast_to(value[None], (count,) + value.shape), axi...  37.5 us
    dot_general x2, matrix products, steps(): jnp.einsum('ic,sij->sjc', source_weights, kernel, preferred_element_type=...  23.5 us
    dot_general x2, matrix products, steps(): jnp.einsum('sij,sjc->ic', kernel, scaled_segments, preferred_element_type...  23.5 us
    all_to_all x2, waiting for transfers between devices, copy_gather(): lax.all_to_all(jnp.broadcast_to(value[None], (count,) + value.shape), axi...  18.7 us
    all_to_all x2, starting transfers between devices, copy_gather(): lax.all_to_all(jnp.broadcast_to(value[None], (count,) + value.shape), axi...  13.4 us
    all_to_all x1, waiting for transfers between devices, steps(): lax.all_to_all(target_copies, 'blk', 0, 0, tiled=False)  12.4 us
  transfers between devices with their start and end apart: 4, of which 4 were waited for; matrix products, arithmetic and copies ran while one was open for 6% of the time, Pallas kernels for 0%

profile of v11, /device:TPU:1, one launch (start us, length us, event | category | flops | bytes accessed | tf_op | source)
XLA Modules:
  0.0 258.9 jit_solution(8593242403175339282)
XLA Ops:
  0.6 0.7 fusion.14
  1.4 0.7 fusion.15
  2.1 0.8 broadcast_in_dim.21
  2.9 9.6 %all-to-all-start.1 = ((bf16[16,128,64]{1,2,0:T(8,128)(2,1)}), bf16[16,128,64]{1,2,0:T(8,128)(2,1)S(1)}, u32[]{:S(2)}, u32[]{:S(2)}) async-start(bf16[16,128,64]{1,2,0:T(8,128)(2,1)} %broadcast_in_dim.21), calls=%async_computation.1 | async-start | bytes 524288 | tf_op jit(solution)/shard_map/all_to_all | solution.py:22
  12.4 0.9 fusion.11
  13.4 0.9 fusion.12
  14.3 6.8 %all-to-all-done.1 = bf16[16,128,64]{1,2,0:T(8,128)(2,1)S(1)} async-done(((bf16[16,128,64]{1,2,0:T(8,128)(2,1)}), bf16[16,128,64]{1,2,0:T(8,128)(2,1)S(1)}, u32[]{:S(2)}, u32[]{:S(2)}) %all-to-all-start.1) | async-done | bytes 262176 | tf_op jit(solution)/shard_map/all_to_all | solution.py:22
  21.1 0.9 broadcast_in_dim.20
  22.1 4.1 %all-to-all-start = ((bf16[8,768,64]{1,2,0:T(8,128)(2,1)}), bf16[8,768,64]{1,2,0:T(8,128)(2,1)S(1)}, u32[]{:S(2)}, u32[]{:S(2)}) async-start(bf16[8,768,64]{1,2,0:T(8,128)(2,1)} %broadcast_in_dim.20), calls=%async_computation | async-start | bytes 1572864 | tf_op jit(solution)/shard_map/all_to_all | solution.py:47
  26.2 0.1 reduce_max.128
  26.5 0.2 copy.9
  26.7 0.1 reshape.164
  26.8 12.4 %all-to-all-done = bf16[8,768,64]{1,2,0:T(8,128)(2,1)S(1)} async-done(((bf16[8,768,64]{1,2,0:T(8,128)(2,1)}), bf16[8,768,64]{1,2,0:T(8,128)(2,1)S(1)}, u32[]{:S(2)}, u32[]{:S(2)}) %all-to-all-start) | async-done | bytes 786464 | tf_op jit(solution)/shard_map/all_to_all | solution.py:47
  39.3 1.5 broadcast_in_dim.22
  40.7 3.6 %all-to-all-start.2 = ((bf16[8,784,128]{2,1,0:T(8,128)(2,1)}), bf16[8,784,128]{2,1,0:T(8,128)(2,1)S(1)}, u32[]{:S(2)}, u32[]{:S(2)}) async-start(bf16[8,784,128]{2,1,0:T(8,128)(2,1)} %broadcast_in_dim.22), calls=%async_computation.2 | async-start | bytes 3211264 | tf_op jit(solution)/shard_map/all_to_all | solution.py:69
  44.3 12.4 %fusion = bf16[8,2048,768]{1,2,0:T(8,128)(2,1)} fusion(bf16[8,768,64]{1,2,0:T(8,128)(2,1)S(1)} %all-to-all-done, bf16[2048,64,1]{0,1,2:T(8,128)(2,1)S(1)} %reshape.164), kind=kOutput, calls=%fused_computation.1 | convolution fusion | flops 1648361472 | bytes 26214400 | tf_op jit(solution)/shard_map/id,sjd->sij/dot_general | solution.py:49
  56.7 9.4 %all-to-all-done.2 = bf16[8,784,128]{2,1,0:T(8,128)(2,1)S(1)} async-done(((bf16[8,784,128]{2,1,0:T(8,128)(2,1)}), bf16[8,784,128]{2,1,0:T(8,128)(2,1)S(1)}, u32[]{:S(2)}, u32[]{:S(2)}) %all-to-all-start.2) | async-done | bytes 1605664 | tf_op jit(solution)/shard_map/all_to_all | solution.py:69
  66.1 11.7 %fusion.3 = bf16[2048,128]{1,0:T(8,128)(2,1)S(1)} fusion(bf16[8,2048,768]{1,2,0:T(8,128)(2,1)} %fusion, bf16[8,784,128]{2,1,0:T(8,128)(2,1)S(1)} %all-to-all-done.2, f32[8,128]{1,0:T(8,128)S(1)} %bitcast.58), kind=kOutput, calls=%fused_computation.10 | convolution fusion | flops 3223846912 | bytes 27267072 | tf_op jit(solution)/shard_map/sij,sjc->ic/dot_general | solution.py:77
  77.9 0.2 maximum_maximum_fusion.2
  78.1 17.0 %all_to_all.50 = bf16[16,144,128]{2,1,0:T(8,128)(2,1)S(1)} all-to-all(bf16[16,144,128]{2,1,0:T(8,128)(2,1)S(1)} %maximum_maximum_fusion.2), channel_id=1, replica_groups=mesh['blk'=8,'dom'=16] {'dom'}, dimensions={0} | all-to-all | bytes 1179648 | tf_op jit(solution)/shard_map/all_to_all | solution.py:83
  95.2 0.1 fusion.10
  95.3 0.6 copy-done.2
  96.0 0.9 broadcast_in_dim.24
  96.9 3.8 %all-to-all-start.4 = ((bf16[16,144,128]{2,1,0:T(8,128)(2,1)}), bf16[16,144,128]{2,1,0:T(8,128)(2,1)S(1)}, u32[]{:S(2)}, u32[]{:S(2)}) async-start(bf16[16,144,128]{2,1,0:T(8,128)(2,1)} %broadcast_in_dim.24), calls=%async_computation.4 | async-start | bytes 1179648 | tf_op jit(solution)/shard_map/all_to_all | solution.py:22
  100.8 11.9 %all-to-all-done.4 = bf16[16,144,128]{2,1,0:T(8,128)(2,1)S(1)} async-done(((bf16[16,144,128]{2,1,0:T(8,128)(2,1)}), bf16[16,144,128]{2,1,0:T(8,128)(2,1)S(1)}, u32[]{:S(2)}, u32[]{:S(2)}) %all-to-all-start.4) | async-done | bytes 589856 | tf_op jit(solution)/shard_map/all_to_all | solution.py:22
  112.8 0.1 multiply_convert_fusion.5
  112.9 11.8 %convolution_convert_fusion.1 = bf16[8,768,128]{2,1,0:T(8,128)(2,1)S(1)} fusion(bf16[8,2048,768]{1,2,0:T(8,128)(2,1)} %fusion, bf16[2048,128,1]{1,0,2:T(8,128)(2,1)S(1)} %bitcast.51), kind=kOutput, calls=%fused_computation.13 | convolution fusion | flops 3222011904 | bytes 27262976 | tf_op jit(solution)/shard_map/ic,sij->sjc/dot_general | solution.py:101
  124.7 0.4 maximum_maximum_fusion
  125.1 22.9 %all_to_all.51 = bf16[8,784,128]{2,1,0:T(8,128)(2,1)S(1)} all-to-all(bf16[8,784,128]{2,1,0:T(8,128)(2,1)S(1)} %maximum_maximum_fusion), channel_id=1, replica_groups=mesh['blk'=8,'dom'=16] {'blk'}, dimensions={0} | all-to-all | bytes 3211264 | tf_op jit(solution)/shard_map/all_to_all | solution.py:108
  148.0 0.2 convert_element_type.211
  148.2 0.2 fusion.2
  148.4 0.8 copy-done
  149.2 0.2 fusion.13
  149.4 0.2 exponential_convert_fusion.1
  149.6 0.2 broadcast_in_dim.26
  149.8 21.8 %all_to_all.52 = bf16[8,784,128]{2,1,0:T(8,128)(2,1)S(1)} all-to-all(bf16[8,784,128]{2,1,0:T(8,128)(2,1)S(1)} %broadcast_in_dim.26), channel_id=1, replica_groups=mesh['blk'=8,'dom'=16] {'blk'}, dimensions={0} | all-to-all | bytes 3211264 | tf_op jit(solution)/shard_map/all_to_all | solution.py:22
  171.7 11.7 %fusion.4 = bf16[2048,128]{1,0:T(8,128)(2,1)S(1)} fusion(bf16[8,2048,768]{1,2,0:T(8,128)(2,1)} %fusion, bf16[8,784,128]{2,1,0:T(8,128)(2,1)S(1)} %all_to_all.52, f32[8,128]{1,0:T(8,128)S(1)} %bitcast.59), kind=kOutput, calls=%fused_computation.11 | convolution fusion | flops 3223846912 | bytes 27267072 | tf_op jit(solution)/shard_map/sij,sjc->ic/dot_general | solution.py:77
  183.5 0.2 maximum_maximum_fusion.3
  183.6 21.2 %all_to_all.53 = bf16[16,144,128]{2,1,0:T(8,128)(2,1)S(1)} all-to-all(bf16[16,144,128]{2,1,0:T(8,128)(2,1)S(1)} %maximum_maximum_fusion.3), channel_id=1, replica_groups=mesh['blk'=8,'dom'=16] {'dom'}, dimensions={0} | all-to-all | bytes 1179648 | tf_op jit(solution)/shard_map/all_to_all | solution.py:83
  205.0 0.1 fusion.9
  205.3 15.6 %all_to_all.54 = bf16[16,144,128]{2,1,0:T(8,128)(2,1)S(1)} all-to-all(bf16[16,144,128]{2,1,0:T(8,128)(2,1)S(1)} %broadcast_in_dim.28), channel_id=1, replica_groups=mesh['blk'=8,'dom'=16] {'dom'}, dimensions={0} | all-to-all | bytes 1179648 | tf_op jit(solution)/shard_map/all_to_all | solution.py:22
  221.0 0.1 multiply_convert_fusion.4
  221.1 11.8 %convolution_convert_fusion = bf16[8,768,128]{2,1,0:T(8,128)(2,1)S(1)} fusion(bf16[8,2048,768]{1,2,0:T(8,128)(2,1)} %fusion, bf16[2048,128,1]{1,0,2:T(8,128)(2,1)S(1)} %bitcast.50), kind=kOutput, calls=%fused_computation.12 | convolution fusion | flops 3222011904 | bytes 27262976 | tf_op jit(solution)/shard_map/ic,sij->sjc/dot_general | solution.py:101
  232.9 0.4 maximum_maximum_fusion.1
  233.3 24.2 %all_to_all.55 = bf16[8,784,128]{2,1,0:T(8,128)(2,1)S(1)} all-to-all(bf16[8,784,128]{2,1,0:T(8,128)(2,1)S(1)} %maximum_maximum_fusion.1), channel_id=1, replica_groups=mesh['blk'=8,'dom'=16] {'blk'}, dimensions={0} | all-to-all | bytes 3211264 | tf_op jit(solution)/shard_map/all_to_all | solution.py:108
  257.5 0.2 convert_element_type.227
  257.7 0.2 fusion.1
  257.9 0.9 log_subtract_fusion
  (52 shorter events, 1.2 us)
Async XLA Ops:
  2.9 23.4 %copy-start.1 = (f32[768,128]{1,0:T(8,128)S(1)}, f32[768,128]{1,0:T(8,128)}, u32[]{:S(2)}) copy-start(f32[768,128]{1,0:T(8,128)} %param.9) | copy-start | bytes 1179652
  2.9 18.3 %all-to-all-start.1 = ((bf16[16,128,64]{1,2,0:T(8,128)(2,1)}), bf16[16,128,64]{1,2,0:T(8,128)(2,1)S(1)}, u32[]{:S(2)}, u32[]{:S(2)}) async-start(bf16[16,128,64]{1,2,0:T(8,128)(2,1)} %broadcast_in_dim.21), calls=%async_computation.1 | async-start | bytes 524288 | tf_op jit(solution)/shard_map/all_to_all | solution.py:22
  22.1 17.2 %all-to-all-start = ((bf16[8,768,64]{1,2,0:T(8,128)(2,1)}), bf16[8,768,64]{1,2,0:T(8,128)(2,1)S(1)}, u32[]{:S(2)}, u32[]{:S(2)}) async-start(bf16[8,768,64]{1,2,0:T(8,128)(2,1)} %broadcast_in_dim.20), calls=%async_computation | async-start | bytes 1572864 | tf_op jit(solution)/shard_map/all_to_all | solution.py:47
  40.7 25.4 %all-to-all-start.2 = ((bf16[8,784,128]{2,1,0:T(8,128)(2,1)}), bf16[8,784,128]{2,1,0:T(8,128)(2,1)S(1)}, u32[]{:S(2)}, u32[]{:S(2)}) async-start(bf16[8,784,128]{2,1,0:T(8,128)(2,1)} %broadcast_in_dim.22), calls=%async_computation.2 | async-start | bytes 3211264 | tf_op jit(solution)/shard_map/all_to_all | solution.py:69
  95.0 0.8 copy-start.2
  96.9 15.8 %all-to-all-start.4 = ((bf16[16,144,128]{2,1,0:T(8,128)(2,1)}), bf16[16,144,128]{2,1,0:T(8,128)(2,1)S(1)}, u32[]{:S(2)}, u32[]{:S(2)}) async-start(bf16[16,144,128]{2,1,0:T(8,128)(2,1)} %broadcast_in_dim.24), calls=%async_computation.4 | async-start | bytes 1179648 | tf_op jit(solution)/shard_map/all_to_all | solution.py:22
  148.2 1.0 copy-start
  205.1 27.8 %copy-start.3 = (f32[128,128]{1,0:T(8,128)}, f32[128,128]{1,0:T(8,128)S(1)}, u32[]{:S(2)}) copy-start(f32[128,128]{1,0:T(8,128)S(1)} %get-tuple-element.3) | copy-start | bytes 196612

commit v12 on v11

--- a/solution.py
+++ b/solution.py
@@ -41,17 +41,18 @@
     block_rows = src_rows * dom_count
     group_rows = tgt_rows * blk_count
 
-    source_block = copy_gather(normalized(source_emb), "dom", dom_count).reshape(
-        src_rows * dom_count, source_emb.shape[1])
+    raw_block = copy_gather(source_emb, "dom", dom_count).reshape(src_rows * dom_count, source_emb.shape[1])
     target_copies = jnp.broadcast_to(normalized(target_emb)[None], (blk_count,) + target_emb.shape)
     target_group = lax.all_to_all(target_copies, "blk", 0, 0, tiled=False).reshape(
         tgt_rows * blk_count, target_emb.shape[1])
+    source_block = normalized(raw_block)
     products = jnp.einsum(
         "id,sjd->sij", source_block, target_group.reshape(blk_count, tgt_rows, source_emb.shape[1]),
         preferred_element_type=jnp.float32)
     kernel = jnp.exp((products - 1.0) / entropic).astype(jnp.bfloat16)
-    log_target = jnp.log(target_counts.astype(jnp.float32)) - math.log(all_targets)
-    log_source = jnp.log(source_counts.astype(jnp.float32)) - math.log(all_sources)
+    log_target, log_source = lax.optimization_barrier((
+        jnp.log(target_counts.astype(jnp.float32)) - math.log(all_targets),
+        jnp.log(source_counts.astype(jnp.float32)) - math.log(all_sources)))
 
     tgt_payload_rows = padded_rows(tgt_rows + 1, 16)
     src_payload_rows = padded_rows(src_rows + 1, 16)

time: 260 us -> 259 us (level)
  blocking collectives: 123 us -> 106 us
  waiting for transfers between devices: 40.5 us -> 51.4 us
  starting transfers between devices: 21.1 us -> 26.2 us
    all_to_all x2 -> x1, blocking collectives: 38.2 us -> 21.4 us  [steps(): lax.all_to_all(pieces.astype(jnp.bfloat16), 'dom', 0, 0, tiled=False)]
    all_to_all x0 -> x1, waiting for transfers between devices: none -> 11.8 us  [steps(): lax.all_to_all(pieces.astype(jnp.bfloat16), 'dom', 0, 0, tiled=False)]
    all_to_all x0 -> x1, starting transfers between devices: none -> 4.44 us  [steps(): lax.all_to_all(pieces.astype(jnp.bfloat16), 'dom', 0, 0, tiled=False)]
  transfers between devices with their start and end apart: 4 -> 5, of which waited for: 4 -> 5; matrix products, arithmetic and copies ran while one was open for 6% -> 6% of each run, Pallas kernels for 0% -> 0%
where the time goes in v12:
time: 259 us; the launch traced here: 258 us
  blocking collectives  106 us (41%)
  matrix products  59.4 us (23%)
  waiting for transfers between devices  51.4 us (20%)
  starting transfers between devices  26.2 us (10%)
  other arithmetic  8.38 us (3%)
  local copies, waits for them, and re-layouts  5.29 us (2%)
    all_to_all x2, blocking collectives, steps(): lax.all_to_all(pieces.astype(jnp.bfloat16), 'blk', 0, 0, tiled=False)  47.5 us
    all_to_all x2, blocking collectives, copy_gather(): lax.all_to_all(jnp.broadcast_to(value[None], (count,) + value.shape), axi...  37.5 us
    dot_general x2, matrix products, steps(): jnp.einsum('ic,sij->sjc', source_weights, kernel, preferred_element_type=...  23.5 us
    dot_general x2, matrix products, steps(): jnp.einsum('sij,sjc->ic', kernel, scaled_segments, preferred_element_type...  23.5 us
    all_to_all x1, blocking collectives, steps(): lax.all_to_all(pieces.astype(jnp.bfloat16), 'dom', 0, 0, tiled=False)  21.4 us
    all_to_all x2, waiting for transfers between devices, copy_gather(): lax.all_to_all(jnp.broadcast_to(value[None], (count,) + value.shape), axi...  17.5 us
    all_to_all x2, starting transfers between devices, copy_gather(): lax.all_to_all(jnp.broadcast_to(value[None], (count,) + value.shape), axi...  14.1 us
    all_to_all x1, waiting for transfers between devices, steps(): lax.all_to_all(target_copies, 'blk', 0, 0, tiled=False)  12.9 us
  transfers between devices with their start and end apart: 5, of which 5 were waited for; matrix products, arithmetic and copies ran while one was open for 6% of the time, Pallas kernels for 0%

profile of v12, /device:TPU:1, one launch (start us, length us, event | category | flops | bytes accessed | tf_op | source)
XLA Modules:
  0.0 258.1 jit_solution(16560071699136971730)
XLA Ops:
  0.6 1.5 broadcast_in_dim.21
  2.1 9.4 %all-to-all-start.1 = ((bf16[16,128,64]{1,2,0:T(8,128)(2,1)}), bf16[16,128,64]{1,2,0:T(8,128)(2,1)S(1)}, u32[]{:S(2)}, u32[]{:S(2)}) async-start(bf16[16,128,64]{1,2,0:T(8,128)(2,1)} %broadcast_in_dim.21), calls=%async_computation.1 | async-start | bytes 524288 | tf_op jit(solution)/shard_map/all_to_all | solution.py:22
  11.6 1.0 fusion.16
  12.5 1.1 reduce_max.128
  13.7 0.1 pad.20.clone
  13.7 0.9 fusion.17
  14.7 5.6 %all-to-all-done.1 = bf16[16,128,64]{1,2,0:T(8,128)(2,1)S(1)} async-done(((bf16[16,128,64]{1,2,0:T(8,128)(2,1)}), bf16[16,128,64]{1,2,0:T(8,128)(2,1)S(1)}, u32[]{:S(2)}, u32[]{:S(2)}) %all-to-all-start.1) | async-done | bytes 262176 | tf_op jit(solution)/shard_map/all_to_all | solution.py:22
  20.2 0.9 broadcast_in_dim.20
  21.2 4.1 %all-to-all-start = ((bf16[8,768,64]{1,2,0:T(8,128)(2,1)}), bf16[8,768,64]{1,2,0:T(8,128)(2,1)S(1)}, u32[]{:S(2)}, u32[]{:S(2)}) async-start(bf16[8,768,64]{1,2,0:T(8,128)(2,1)} %broadcast_in_dim.20), calls=%async_computation | async-start | bytes 1572864 | tf_op jit(solution)/shard_map/all_to_all | solution.py:46
  25.5 12.9 %all-to-all-done = bf16[8,768,64]{1,2,0:T(8,128)(2,1)S(1)} async-done(((bf16[8,768,64]{1,2,0:T(8,128)(2,1)}), bf16[8,768,64]{1,2,0:T(8,128)(2,1)S(1)}, u32[]{:S(2)}, u32[]{:S(2)}) %all-to-all-start) | async-done | bytes 786464 | tf_op jit(solution)/shard_map/all_to_all | solution.py:46
  38.4 1.5 broadcast_in_dim.22
  39.8 3.6 %all-to-all-start.2 = ((bf16[8,784,128]{2,1,0:T(8,128)(2,1)}), bf16[8,784,128]{2,1,0:T(8,128)(2,1)S(1)}, u32[]{:S(2)}, u32[]{:S(2)}) async-start(bf16[8,784,128]{2,1,0:T(8,128)(2,1)} %broadcast_in_dim.22), calls=%async_computation.2 | async-start | bytes 3211264 | tf_op jit(solution)/shard_map/all_to_all | solution.py:70
  43.4 12.4 %fusion = bf16[8,2048,768]{1,2,0:T(8,128)(2,1)} fusion(bf16[8,768,64]{1,2,0:T(8,128)(2,1)S(1)} %all-to-all-done, f32[2048]{0:T(1024)S(1)} %rsqrt_bitcast_fusion, bf16[16,128,64]{1,2,0:T(8,128)(2,1)S(1)} %all-to-all-done.1), kind=kOutput, calls=%fused_computation.1 | convolution fusion | flops 1648754688 | bytes 26222592 | tf_op jit(solution)/shard_map/id,sjd->sij/dot_general | solution.py:49
  55.8 9.4 %all-to-all-done.2 = bf16[8,784,128]{2,1,0:T(8,128)(2,1)S(1)} async-done(((bf16[8,784,128]{2,1,0:T(8,128)(2,1)}), bf16[8,784,128]{2,1,0:T(8,128)(2,1)S(1)}, u32[]{:S(2)}, u32[]{:S(2)}) %all-to-all-start.2) | async-done | bytes 1605664 | tf_op jit(solution)/shard_map/all_to_all | solution.py:70
  65.3 11.7 %fusion.3 = bf16[2048,128]{1,0:T(8,128)(2,1)S(1)} fusion(bf16[8,2048,768]{1,2,0:T(8,128)(2,1)} %fusion, bf16[8,784,128]{2,1,0:T(8,128)(2,1)S(1)} %all-to-all-done.2, f32[8,128]{1,0:T(8,128)S(1)} %bitcast.71), kind=kOutput, calls=%fused_computation.10 | convolution fusion | flops 3223846912 | bytes 27267072 | tf_op jit(solution)/shard_map/sij,sjc->ic/dot_general | solution.py:78
  77.0 1.0 maximum_maximum_fusion.2
  78.1 4.4 %all-to-all-start.3 = ((bf16[16,144,128]{2,1,0:T(8,128)(2,1)}), bf16[16,144,128]{2,1,0:T(8,128)(2,1)S(1)}, u32[]{:S(2)}, u32[]{:S(2)}) async-start(bf16[16,144,128]{2,1,0:T(8,128)(2,1)} %maximum_maximum_fusion.2), calls=%async_computation.3 | async-start | bytes 1179648 | tf_op jit(solution)/shard_map/all_to_all | solution.py:84
  82.6 11.8 %all-to-all-done.3 = bf16[16,144,128]{2,1,0:T(8,128)(2,1)S(1)} async-done(((bf16[16,144,128]{2,1,0:T(8,128)(2,1)}), bf16[16,144,128]{2,1,0:T(8,128)(2,1)S(1)}, u32[]{:S(2)}, u32[]{:S(2)}) %all-to-all-start.3) | async-done | bytes 589856 | tf_op jit(solution)/shard_map/all_to_all | solution.py:84
  94.4 0.1 convert_element_type.211
  94.5 0.1 fusion.10
  94.7 0.9 broadcast_in_dim.24
  95.6 4.6 %all-to-all-start.4 = ((bf16[16,144,128]{2,1,0:T(8,128)(2,1)}), bf16[16,144,128]{2,1,0:T(8,128)(2,1)S(1)}, u32[]{:S(2)}, u32[]{:S(2)}) async-start(bf16[16,144,128]{2,1,0:T(8,128)(2,1)} %broadcast_in_dim.24), calls=%async_computation.4 | async-start | bytes 1179648 | tf_op jit(solution)/shard_map/all_to_all | solution.py:22
  100.3 0.1 pad.14.clone
  100.4 11.9 %all-to-all-done.4 = bf16[16,144,128]{2,1,0:T(8,128)(2,1)S(1)} async-done(((bf16[16,144,128]{2,1,0:T(8,128)(2,1)}), bf16[16,144,128]{2,1,0:T(8,128)(2,1)S(1)}, u32[]{:S(2)}, u32[]{:S(2)}) %all-to-all-start.4) | async-done | bytes 589856 | tf_op jit(solution)/shard_map/all_to_all | solution.py:22
  112.3 0.1 multiply_convert_fusion.5
  112.5 11.8 %convolution_convert_fusion.1 = bf16[8,768,128]{2,1,0:T(8,128)(2,1)S(1)} fusion(bf16[8,2048,768]{1,2,0:T(8,128)(2,1)} %fusion, bf16[2048,128,1]{1,0,2:T(8,128)(2,1)S(1)} %bitcast.64), kind=kOutput, calls=%fused_computation.13 | convolution fusion | flops 3222011904 | bytes 27262976 | tf_op jit(solution)/shard_map/ic,sij->sjc/dot_general | solution.py:102
  124.2 0.4 maximum_maximum_fusion
  124.6 23.3 %all_to_all.50 = bf16[8,784,128]{2,1,0:T(8,128)(2,1)S(1)} all-to-all(bf16[8,784,128]{2,1,0:T(8,128)(2,1)S(1)} %maximum_maximum_fusion), channel_id=1, replica_groups=mesh['blk'=8,'dom'=16] {'blk'}, dimensions={0} | all-to-all | bytes 3211264 | tf_op jit(solution)/shard_map/all_to_all | solution.py:109
  147.9 0.2 convert_element_type.219
  148.2 0.2 fusion.2
  148.4 0.1 fusion.18
  148.6 0.1 exponential_convert_fusion.1
  148.7 0.2 broadcast_in_dim.26
  148.9 21.8 %all_to_all.51 = bf16[8,784,128]{2,1,0:T(8,128)(2,1)S(1)} all-to-all(bf16[8,784,128]{2,1,0:T(8,128)(2,1)S(1)} %broadcast_in_dim.26), channel_id=1, replica_groups=mesh['blk'=8,'dom'=16] {'blk'}, dimensions={0} | all-to-all | bytes 3211264 | tf_op jit(solution)/shard_map/all_to_all | solution.py:22
  170.8 11.7 %fusion.4 = bf16[2048,128]{1,0:T(8,128)(2,1)S(1)} fusion(bf16[8,2048,768]{1,2,0:T(8,128)(2,1)} %fusion, bf16[8,784,128]{2,1,0:T(8,128)(2,1)S(1)} %all_to_all.51, f32[8,128]{1,0:T(8,128)S(1)} %bitcast.72), kind=kOutput, calls=%fused_computation.11 | convolution fusion | flops 3223846912 | bytes 27267072 | tf_op jit(solution)/shard_map/sij,sjc->ic/dot_general | solution.py:78
  182.6 0.2 maximum_maximum_fusion.3
  182.8 21.4 %all_to_all.52 = bf16[16,144,128]{2,1,0:T(8,128)(2,1)S(1)} all-to-all(bf16[16,144,128]{2,1,0:T(8,128)(2,1)S(1)} %maximum_maximum_fusion.3), channel_id=1, replica_groups=mesh['blk'=8,'dom'=16] {'dom'}, dimensions={0} | all-to-all | bytes 1179648 | tf_op jit(solution)/shard_map/all_to_all | solution.py:84
  204.2 0.1 convert_element_type.227
  204.3 0.1 fusion.9
  204.5 0.1 broadcast_in_dim.28
  204.6 15.6 %all_to_all.53 = bf16[16,144,128]{2,1,0:T(8,128)(2,1)S(1)} all-to-all(bf16[16,144,128]{2,1,0:T(8,128)(2,1)S(1)} %broadcast_in_dim.28), channel_id=1, replica_groups=mesh['blk'=8,'dom'=16] {'dom'}, dimensions={0} | all-to-all | bytes 1179648 | tf_op jit(solution)/shard_map/all_to_all | solution.py:22
  220.3 0.1 multiply_convert_fusion.4
  220.5 11.8 %convolution_convert_fusion = bf16[8,768,128]{2,1,0:T(8,128)(2,1)S(1)} fusion(bf16[8,2048,768]{1,2,0:T(8,128)(2,1)} %fusion, bf16[2048,128,1]{1,0,2:T(8,128)(2,1)S(1)} %bitcast.63), kind=kOutput, calls=%fused_computation.12 | convolution fusion | flops 3222011904 | bytes 27262976 | tf_op jit(solution)/shard_map/ic,sij->sjc/dot_general | solution.py:102
  232.3 0.4 maximum_maximum_fusion.1
  232.7 24.2 %all_to_all.54 = bf16[8,784,128]{2,1,0:T(8,128)(2,1)S(1)} all-to-all(bf16[8,784,128]{2,1,0:T(8,128)(2,1)S(1)} %maximum_maximum_fusion.1), channel_id=1, replica_groups=mesh['blk'=8,'dom'=16] {'blk'}, dimensions={0} | all-to-all | bytes 3211264 | tf_op jit(solution)/shard_map/all_to_all | solution.py:109
  256.8 0.2 convert_element_type.235
  257.1 0.2 fusion.1
  257.3 0.8 log_subtract_fusion
  (52 shorter events, 0.9 us)
Async XLA Ops:
  2.1 18.1 %all-to-all-start.1 = ((bf16[16,128,64]{1,2,0:T(8,128)(2,1)}), bf16[16,128,64]{1,2,0:T(8,128)(2,1)S(1)}, u32[]{:S(2)}, u32[]{:S(2)}) async-start(bf16[16,128,64]{1,2,0:T(8,128)(2,1)} %broadcast_in_dim.21), calls=%async_computation.1 | async-start | bytes 524288 | tf_op jit(solution)/shard_map/all_to_all | solution.py:22
  11.5 13.8 %copy-start = (f32[768,128]{1,0:T(8,128)S(1)}, f32[768,128]{1,0:T(8,128)}, u32[]{:S(2)}) copy-start(f32[768,128]{1,0:T(8,128)} %param.9) | copy-start | bytes 1179652
  21.2 17.2 %all-to-all-start = ((bf16[8,768,64]{1,2,0:T(8,128)(2,1)}), bf16[8,768,64]{1,2,0:T(8,128)(2,1)S(1)}, u32[]{:S(2)}, u32[]{:S(2)}) async-start(bf16[8,768,64]{1,2,0:T(8,128)(2,1)} %broadcast_in_dim.20), calls=%async_computation | async-start | bytes 1572864 | tf_op jit(solution)/shard_map/all_to_all | solution.py:46
  39.8 25.4 %all-to-all-start.2 = ((bf16[8,784,128]{2,1,0:T(8,128)(2,1)}), bf16[8,784,128]{2,1,0:T(8,128)(2,1)S(1)}, u32[]{:S(2)}, u32[]{:S(2)}) async-start(bf16[8,784,128]{2,1,0:T(8,128)(2,1)} %broadcast_in_dim.22), calls=%async_computation.2 | async-start | bytes 3211264 | tf_op jit(solution)/shard_map/all_to_all | solution.py:70
  77.0 5.5 %copy-start.3 = (s32[128,128]{1,0:T(8,128)S(1)}, s32[128,128]{1,0:T(8,128)}, u32[]{:S(2)}) copy-start(s32[128,128]{1,0:T(8,128)} %param.7) | copy-start | bytes 196612
  77.0 5.5 %copy-start.1 = (s32[768,128]{1,0:T(8,128)S(1)}, s32[768,128]{1,0:T(8,128)}, u32[]{:S(2)}) copy-start(s32[768,128]{1,0:T(8,128)} %param.8) | copy-start | bytes 1179652
  78.1 16.3 %all-to-all-start.3 = ((bf16[16,144,128]{2,1,0:T(8,128)(2,1)}), bf16[16,144,128]{2,1,0:T(8,128)(2,1)S(1)}, u32[]{:S(2)}, u32[]{:S(2)}) async-start(bf16[16,144,128]{2,1,0:T(8,128)(2,1)} %maximum_maximum_fusion.2), calls=%async_computation.3 | async-start | bytes 1179648 | tf_op jit(solution)/shard_map/all_to_all | solution.py:84
  95.6 16.6 %all-to-all-start.4 = ((bf16[16,144,128]{2,1,0:T(8,128)(2,1)}), bf16[16,144,128]{2,1,0:T(8,128)(2,1)S(1)}, u32[]{:S(2)}, u32[]{:S(2)}) async-start(bf16[16,144,128]{2,1,0:T(8,128)(2,1)} %broadcast_in_dim.24), calls=%async_computation.4 | async-start | bytes 1179648 | tf_op jit(solution)/shard_map/all_to_all | solution.py:22
  204.5 27.8 %copy-start.2 = (f32[128,128]{1,0:T(8,128)}, f32[128,128]{1,0:T(8,128)S(1)}, u32[]{:S(2)}) copy-start(f32[128,128]{1,0:T(8,128)S(1)} %get-tuple-element.7) | copy-start | bytes 196612
